TPU v7x, 512 devices: a whole 4x4x16 slice. The times are simulated.
512 devices in a mesh: gx: 64 (over z, y_lo, core), gz: 8 (over x, y_hi).
Axes of the slice: x: 4, y: 4 (y_hi: 2, y_lo: 2; y = y_hi * 2 + y_lo), z: 16, core: 2. Of those that a mesh axis runs over, the one named last changes fastest.
Arguments:
- adjoint: bfloat16 [3, 512, 256, 256], P(None, 'gx', 'gz'), may hold values from -6 to 6
- strain: bfloat16 [512, 256, 256], P('gx', 'gz'), may hold values from -16 to 16
- correction: float32 [256, 256], P('gz'), may hold values from 0.3 to 3
- metric: float32 [256], replicated, may hold values from 0.5 to 4
- stream_inverse: bfloat16 [512, 512], replicated, may hold values from -0.081 to 1.081
- span_inverse: bfloat16 [256, 256], replicated, may hold values from -0.081 to 1.081
- wall_operator: bfloat16 [256, 256], replicated, may hold values from -0.081 to 1.081
Outputs:
- adjoint_next: bfloat16 [3, 512, 256, 256], P(None, 'gx', 'gz')
- gradient: float32 [256, 256], P('gz', 'gx')
All inputs are finite; a program needn't handle non-finite values.
Results may differ from a plain program's by a relative error of at most 0.013.
Values may be sent and summed in bfloat16 or wider, within the bound.
No kernel may reach another device: no remote copies, remote signals or barrier semaphores. Data moves between devices by JAX's collectives and lax.ppermute only.
A program may use at most 64 MiB of HBM per device.

v0:
```python
import jax
import jax.numpy as jnp
from jax import lax
from jax.sharding import PartitionSpec as P

near_coef = 7.0 / 9.0
far_coef = 1.0 / 36.0
time_step = 0.25


def stencil(source, axis):
    widened = source.astype(jnp.float32)
    near_diff = jnp.roll(widened, -1, axis) - jnp.roll(widened, 1, axis)
    far_diff = jnp.roll(widened, -2, axis) - jnp.roll(widened, 2, axis)
    return (near_coef * near_diff + far_coef * far_diff).astype(jnp.bfloat16)


def stream_derivative(pencil, stream_inverse):
    right_side = stencil(pencil, 1)
    product = jnp.einsum(
        "ij,kjp->kip", stream_inverse, right_side, preferred_element_type=jnp.float32
    )
    return product.astype(jnp.bfloat16)


def span_derivative(pencil, span_inverse):
    right_side = stencil(pencil, 2)
    product = jnp.einsum(
        "ij,kajy->kaiy", span_inverse, right_side, preferred_element_type=jnp.float32
    )
    return product.astype(jnp.bfloat16)


def wall_derivative(source, wall_operator, metric):
    product = jnp.einsum("kxzj,ij->kxzi", source, wall_operator, preferred_element_type=jnp.float32)
    return product * metric


def stream_apply(source, stream_inverse):
    flat_source = source.reshape(source.shape[0], source.shape[1], -1)
    derived = stream_derivative(
        lax.all_to_all(flat_source, "gx", split_axis=2, concat_axis=1, tiled=True), stream_inverse
    )
    result = lax.all_to_all(derived, "gx", split_axis=1, concat_axis=2, tiled=True)
    return result.reshape(source.shape)


def span_apply(source, span_inverse):
    derived = span_derivative(
        lax.all_to_all(source, "gz", split_axis=1, concat_axis=2, tiled=True), span_inverse
    )
    return lax.all_to_all(derived, "gz", split_axis=2, concat_axis=1, tiled=True)


def on_device(adjoint, strain, correction, metric, stream_inverse, span_inverse, wall_operator):
    components, stream_cells, span_cells, wall_cells = adjoint.shape
    strain_wide = strain.astype(jnp.float32)
    viscosity = (correction[None] * strain_wide).astype(jnp.bfloat16)
    viscous = viscosity.astype(jnp.float32)[None]
    stream_grad = stream_apply(adjoint, stream_inverse)
    stream_flux = (viscous * stream_grad.astype(jnp.float32)).astype(jnp.bfloat16)
    stream_diverge = stream_apply(stream_flux, stream_inverse)
    span_grad = span_apply(adjoint, span_inverse)
    span_flux = (viscous * span_grad.astype(jnp.float32)).astype(jnp.bfloat16)
    span_diverge = span_apply(span_flux, span_inverse)
    wall_grad = wall_derivative(adjoint, wall_operator, metric).astype(jnp.bfloat16)
    wall_flux = (viscous * wall_grad.astype(jnp.float32)).astype(jnp.bfloat16)
    wall_diverge = wall_derivative(wall_flux, wall_operator, metric)
    total = stream_diverge.astype(jnp.float32) + wall_diverge + span_diverge.astype(jnp.float32)
    updated = (adjoint.astype(jnp.float32) + time_step * total).astype(jnp.bfloat16)
    squares = stream_grad.astype(jnp.float32) ** 2 + wall_grad.astype(jnp.float32) ** 2
    squares = jnp.sum(squares + span_grad.astype(jnp.float32) ** 2, axis=0)
    partial_sum = jnp.sum(strain_wide * squares, axis=0)
    summed = lax.psum_scatter(partial_sum, "gx", scatter_dimension=1, tiled=True)
    gradient = -summed / (stream_cells * lax.axis_size("gx"))
    return (updated, gradient)


def solution(mesh):
    in_specs = (P(None, "gx", "gz", None), P("gx", "gz", None), P("gz", None), P(), P(), P(), P())
    out_specs = (P(None, "gx", "gz", None), P("gz", "gx"))
    return jax.shard_map(
        on_device, mesh=mesh, in_specs=in_specs, out_specs=out_specs, check_vma=False
    )
```

profile of v0, /device:TPU:1, one launch (start us, length us, event | category | flops | bytes accessed | tf_op | source)
XLA Modules:
  0.0 471.1 jit_solution(11239621789923117145)
XLA Ops:
  0.6 1.9 copy.128
  2.5 7.5 %all-to-all-start.4 = ((bf16[3,8,32,256]{3,2,0,1:T(8,128)(2,1)}), bf16[3,8,32,256]{3,2,0,1:T(8,128)(2,1)S(1)}, u32[]{:S(2)}, u32[]{:S(2)}) async-start(bf16[3,8,32,256]{3,2,0,1:T(8,128)(2,1)} %copy.128), calls=%async_computation.4 | async-start | bytes 786432 | tf_op jit(solution)/shard_map/all_to_all | solution.py:50
  10.0 8.6 %copy.115 = bf16[3,8,32,256]{1,0,3,2:T(4,128)(2,1)} copy(bf16[3,8,32,256]{3,2,1,0:T(8,128)(2,1)} %param.7) | data formatting | bytes 786432 | tf_op args[0]
  18.6 13.6 %reshape.197 = bf16[64,2,1536]{2,1,0:T(2,128)(2,1)} reshape(bf16[8192,3,8]{2,1,0:T(4,128)(2,1)} %bitcast.135) | data formatting | bytes 786432
  32.2 16.7 %all-to-all-start = ((bf16[64,2,1536]{2,1,0:T(2,128)(2,1)}), bf16[64,2,1536]{2,1,0:T(2,128)(2,1)S(1)}, u32[]{:S(2)}, u32[]{:S(2)}) async-start(bf16[64,2,1536]{2,1,0:T(2,128)(2,1)} %reshape.197), calls=%async_computation | async-start | bytes 786432 | tf_op jit(solution)/shard_map/all_to_all | solution.py:42
  50.9 25.8 %all-to-all-done = bf16[64,2,1536]{2,1,0:T(2,128)(2,1)S(1)} async-done(((bf16[64,2,1536]{2,1,0:T(2,128)(2,1)}), bf16[64,2,1536]{2,1,0:T(2,128)(2,1)S(1)}, u32[]{:S(2)}, u32[]{:S(2)}) %all-to-all-start) | async-done | bytes 393248 | tf_op jit(solution)/shard_map/all_to_all | solution.py:42
  76.7 7.5 %all-to-all-start.5 = ((bf16[3,1,256,256]{3,0,1,2:T(4,128)(2,1)}), bf16[3,1,256,256]{3,0,1,2:T(4,128)(2,1)S(1)}, u32[]{:S(2)}, u32[]{:S(2)}) async-start(bf16[3,1,256,256]{3,0,1,2:T(4,128)(2,1)} %copy.131), calls=%async_computation.5 | async-start | bytes 1048576 | tf_op jit(solution)/shard_map/all_to_all | solution.py:52
  84.3 10.7 %reshape.198 = bf16[8192,3,8]{2,1,0:T(4,128)(2,1)} reshape(bf16[64,2,1536]{2,1,0:T(2,128)(2,1)S(1)} %all-to-all-done) | data formatting | bytes 786432
  94.9 9.5 %copy.116 = bf16[3,8,8192]{2,1,0:T(8,128)(2,1)S(1)} copy(bf16[3,8,8192]{1,0,2:T(4,128)(2,1)} %bitcast.132) | data formatting | bytes 786432 | tf_op jit(solution)/shard_map/all_to_all | solution.py:42
  107.0 5.0 %all-to-all-start.1 = ((bf16[3,512,128]{2,0,1:T(4,128)(2,1)}), bf16[3,512,128]{2,0,1:T(4,128)(2,1)S(1)}, u32[]{:S(2)}, u32[]{:S(2)}) async-start(bf16[3,512,128]{2,0,1:T(4,128)(2,1)} %copy.119), calls=%async_computation.1 | async-start | bytes 1048576 | tf_op jit(solution)/shard_map/all_to_all | solution.py:44
  113.1 32.0 %all-to-all-done.1 = bf16[3,512,128]{2,0,1:T(4,128)(2,1)S(1)} async-done(((bf16[3,512,128]{2,0,1:T(4,128)(2,1)}), bf16[3,512,128]{2,0,1:T(4,128)(2,1)S(1)}, u32[]{:S(2)}, u32[]{:S(2)}) %all-to-all-start.1) | async-done | bytes 393248 | tf_op jit(solution)/shard_map/all_to_all | solution.py:44
  145.5 3.1 fusion.16
  149.4 6.9 %all-to-all-start.6 = ((bf16[3,8,32,256]{3,2,0,1:T(8,128)(2,1)}), bf16[3,8,32,256]{3,2,0,1:T(8,128)(2,1)S(1)}, u32[]{:S(2)}, u32[]{:S(2)}) async-start(bf16[3,8,32,256]{3,2,0,1:T(8,128)(2,1)} %copy.133), calls=%async_computation.6 | async-start | bytes 786432 | tf_op jit(solution)/shard_map/all_to_all | solution.py:50
  156.4 8.2 %copy.121 = bf16[3,8,8192]{1,0,2:T(4,128)(2,1)} copy(bf16[3,8,8192]{2,1,0:T(8,128)(2,1)S(1)} %fusion.12) | data formatting | bytes 786432 | tf_op jit(solution)/shard_map/convert_element_type | solution.py:61
  164.6 13.6 %reshape.199 = bf16[64,2,1536]{2,1,0:T(2,128)(2,1)} reshape(bf16[8192,3,8]{2,1,0:T(4,128)(2,1)} %bitcast.133) | data formatting | bytes 786432
  178.1 5.5 %all-to-all-start.2 = ((bf16[64,2,1536]{2,1,0:T(2,128)(2,1)}), bf16[64,2,1536]{2,1,0:T(2,128)(2,1)S(1)}, u32[]{:S(2)}, u32[]{:S(2)}) async-start(bf16[64,2,1536]{2,1,0:T(2,128)(2,1)} %reshape.199), calls=%async_computation.2 | async-start | bytes 786432 | tf_op jit(solution)/shard_map/all_to_all | solution.py:42
  185.7 25.8 %all-to-all-done.2 = bf16[64,2,1536]{2,1,0:T(2,128)(2,1)S(1)} async-done(((bf16[64,2,1536]{2,1,0:T(2,128)(2,1)}), bf16[64,2,1536]{2,1,0:T(2,128)(2,1)S(1)}, u32[]{:S(2)}, u32[]{:S(2)}) %all-to-all-start.2) | async-done | bytes 393248 | tf_op jit(solution)/shard_map/all_to_all | solution.py:42
  211.4 6.9 %all-to-all-start.7 = ((bf16[3,1,256,256]{3,0,1,2:T(4,128)(2,1)}), bf16[3,1,256,256]{3,0,1,2:T(4,128)(2,1)S(1)}, u32[]{:S(2)}, u32[]{:S(2)}) async-start(bf16[3,1,256,256]{3,0,1,2:T(4,128)(2,1)} %copy.136), calls=%async_computation.7 | async-start | bytes 1048576 | tf_op jit(solution)/shard_map/all_to_all | solution.py:52
  218.3 10.7 %reshape.200 = bf16[8192,3,8]{2,1,0:T(4,128)(2,1)} reshape(bf16[64,2,1536]{2,1,0:T(2,128)(2,1)S(1)} %all-to-all-done.2) | data formatting | bytes 786432
  229.0 9.5 %copy.122 = bf16[3,8,8192]{2,1,0:T(8,128)(2,1)S(1)} copy(bf16[3,8,8192]{1,0,2:T(4,128)(2,1)} %bitcast.134) | data formatting | bytes 786432 | tf_op jit(solution)/shard_map/all_to_all | solution.py:42
  241.1 5.2 %all-to-all-start.3 = ((bf16[3,512,128]{2,0,1:T(4,128)(2,1)}), bf16[3,512,128]{2,0,1:T(4,128)(2,1)S(1)}, u32[]{:S(2)}, u32[]{:S(2)}) async-start(bf16[3,512,128]{2,0,1:T(4,128)(2,1)} %copy.125), calls=%async_computation.3 | async-start | bytes 1048576 | tf_op jit(solution)/shard_map/all_to_all | solution.py:44
  246.3 1.3 dynamic-slice
  248.4 218.7 %all-reduce = f32[32,256]{0,1:T(8,128)S(1)} all-reduce(f32[32,256]{0,1:T(8,128)S(1)} %copy.139), channel_id=2, replica_groups=mesh['gx'=64,'gz'=8] {'gx'}, use_global_device_ids=true, to_apply=%region_2.3.clone | all-reduce | flops 8192 | bytes 65536
  468.8 2.2 fusion.6
  (74 shorter events, 13.0 us)
Async XLA Ops:
  0.6 104.8 %copy-start = (bf16[512,512]{1,0:T(8,128)(2,1)S(1)}, bf16[512,512]{1,0:T(8,128)(2,1)}, u32[]{:S(2)}) copy-start(bf16[512,512]{1,0:T(8,128)(2,1)} %param.11) | copy-start | bytes 1572868
  2.5 29.7 %all-to-all-start.4 = ((bf16[3,8,32,256]{3,2,0,1:T(8,128)(2,1)}), bf16[3,8,32,256]{3,2,0,1:T(8,128)(2,1)S(1)}, u32[]{:S(2)}, u32[]{:S(2)}) async-start(bf16[3,8,32,256]{3,2,0,1:T(8,128)(2,1)} %copy.128), calls=%async_computation.4 | async-start | bytes 786432 | tf_op jit(solution)/shard_map/all_to_all | solution.py:50
  18.6 30.7 %copy-start.4 = (bf16[256,256]{1,0:T(8,128)(2,1)S(1)}, bf16[256,256]{1,0:T(8,128)(2,1)}, u32[]{:S(2)}) copy-start(bf16[256,256]{1,0:T(8,128)(2,1)} %param.12) | copy-start | bytes 393220
  32.2 44.6 %all-to-all-start = ((bf16[64,2,1536]{2,1,0:T(2,128)(2,1)}), bf16[64,2,1536]{2,1,0:T(2,128)(2,1)S(1)}, u32[]{:S(2)}, u32[]{:S(2)}) async-start(bf16[64,2,1536]{2,1,0:T(2,128)(2,1)} %reshape.197), calls=%async_computation | async-start | bytes 786432 | tf_op jit(solution)/shard_map/all_to_all | solution.py:42
  76.7 30.3 %all-to-all-start.5 = ((bf16[3,1,256,256]{3,0,1,2:T(4,128)(2,1)}), bf16[3,1,256,256]{3,0,1,2:T(4,128)(2,1)S(1)}, u32[]{:S(2)}, u32[]{:S(2)}) async-start(bf16[3,1,256,256]{3,0,1,2:T(4,128)(2,1)} %copy.131), calls=%async_computation.5 | async-start | bytes 1048576 | tf_op jit(solution)/shard_map/all_to_all | solution.py:52
  104.5 7.5 %copy-start.6 = (bf16[8,32,256]{2,1,0:T(8,128)(2,1)S(1)}, bf16[8,32,256]{2,1,0:T(8,128)(2,1)}, u32[]{:S(2)}) copy-start(bf16[8,32,256]{2,1,0:T(8,128)(2,1)} %param.8) | copy-start | bytes 393220
  104.5 7.5 %copy-start.8 = (f32[32,256]{1,0:T(8,128)S(1)}, f32[32,256]{1,0:T(8,128)}, u32[]{:S(2)}) copy-start(f32[32,256]{1,0:T(8,128)} %param.9) | copy-start | bytes 98308
  105.3 40.2 %copy-start.1 = (bf16[3,8,32,256]{3,2,1,0:T(8,128)(2,1)S(1)}, bf16[3,8,32,256]{3,2,1,0:T(8,128)(2,1)}, u32[]{:S(2)}) copy-start(bf16[3,8,32,256]{3,2,1,0:T(8,128)(2,1)} %param.7) | copy-start | bytes 1179652
  105.3 40.2 %copy-start.9 = (f32[256]{0:T(256)S(1)}, f32[256]{0:T(256)}, u32[]{:S(2)}) copy-start(f32[256]{0:T(256)} %param.10) | copy-start | bytes 3076
  107.0 38.1 %all-to-all-start.1 = ((bf16[3,512,128]{2,0,1:T(4,128)(2,1)}), bf16[3,512,128]{2,0,1:T(4,128)(2,1)S(1)}, u32[]{:S(2)}, u32[]{:S(2)}) async-start(bf16[3,512,128]{2,0,1:T(4,128)(2,1)} %copy.119), calls=%async_computation.1 | async-start | bytes 1048576 | tf_op jit(solution)/shard_map/all_to_all | solution.py:44
  149.4 28.7 %all-to-all-start.6 = ((bf16[3,8,32,256]{3,2,0,1:T(8,128)(2,1)}), bf16[3,8,32,256]{3,2,0,1:T(8,128)(2,1)S(1)}, u32[]{:S(2)}, u32[]{:S(2)}) async-start(bf16[3,8,32,256]{3,2,0,1:T(8,128)(2,1)} %copy.133), calls=%async_computation.6 | async-start | bytes 786432 | tf_op jit(solution)/shard_map/all_to_all | solution.py:50
  164.6 19.5 %copy-start.5 = (bf16[256,256]{1,0:T(8,128)(2,1)S(1)}, bf16[256,256]{1,0:T(8,128)(2,1)}, u32[]{:S(2)}) copy-start(bf16[256,256]{1,0:T(8,128)(2,1)} %param.12) | copy-start | bytes 393220
  178.1 33.3 %all-to-all-start.2 = ((bf16[64,2,1536]{2,1,0:T(2,128)(2,1)}), bf16[64,2,1536]{2,1,0:T(2,128)(2,1)S(1)}, u32[]{:S(2)}, u32[]{:S(2)}) async-start(bf16[64,2,1536]{2,1,0:T(2,128)(2,1)} %reshape.199), calls=%async_computation.2 | async-start | bytes 786432 | tf_op jit(solution)/shard_map/all_to_all | solution.py:42
  211.4 29.7 %all-to-all-start.7 = ((bf16[3,1,256,256]{3,0,1,2:T(4,128)(2,1)}), bf16[3,1,256,256]{3,0,1,2:T(4,128)(2,1)S(1)}, u32[]{:S(2)}, u32[]{:S(2)}) async-start(bf16[3,1,256,256]{3,0,1,2:T(4,128)(2,1)} %copy.136), calls=%async_computation.7 | async-start | bytes 1048576 | tf_op jit(solution)/shard_map/all_to_all | solution.py:52
  238.5 9.7 %copy-start.3 = (f32[8,32,256]{2,1,0:T(8,128)S(1)}, f32[8,32,256]{2,1,0:T(8,128)}, u32[]{:S(2)}) copy-start(f32[8,32,256]{2,1,0:T(8,128)} %get-tuple-element.34) | copy-start | bytes 786436
  238.6 9.7 %copy-start.7 = (bf16[8,32,256]{2,1,0:T(8,128)(2,1)S(1)}, bf16[8,32,256]{2,1,0:T(8,128)(2,1)}, u32[]{:S(2)}) copy-start(bf16[8,32,256]{2,1,0:T(8,128)(2,1)} %param.8) | copy-start | bytes 393220
  239.4 229.5 %copy-start.2 = (f32[3,8,32,256]{3,2,1,0:T(8,128)S(1)}, f32[3,8,32,256]{3,2,1,0:T(8,128)}, u32[]{:S(2)}) copy-start(f32[3,8,32,256]{3,2,1,0:T(8,128)} %get-tuple-element.38) | copy-start | bytes 2359300
  241.1 227.3 %all-to-all-start.3 = ((bf16[3,512,128]{2,0,1:T(4,128)(2,1)}), bf16[3,512,128]{2,0,1:T(4,128)(2,1)S(1)}, u32[]{:S(2)}, u32[]{:S(2)}) async-start(bf16[3,512,128]{2,0,1:T(4,128)(2,1)} %copy.125), calls=%async_computation.3 | async-start | bytes 1048576 | tf_op jit(solution)/shard_map/all_to_all | solution.py:44
where the time goes:
time: 477 us; the launch traced here: 471 us
  blocking collectives  219 us (46%)
  local copies, waits for them, and re-layouts  97.3 us (20%)
  waiting for transfers between devices  83.6 us (18%)
  starting transfers between devices  61.3 us (13%)
  matrix products  7.3 us (2%)
    unnamed x1, blocking collectives  219 us
    unnamed x30, local copies, waits for them, and re-layouts  60.7 us
    all_to_all x2, waiting for transfers between devices, stream_apply(): lax.all_to_all(flat_source, 'gx', split_axis=2, concat_axis=1, tiled=True)  51.6 us
    all_to_all x2, waiting for transfers between devices, stream_apply(): lax.all_to_all(derived, 'gx', split_axis=1, concat_axis=2, tiled=True)  32 us
    all_to_all x2, starting transfers between devices, stream_apply(): lax.all_to_all(flat_source, 'gx', split_axis=2, concat_axis=1, tiled=True)  22.2 us
    all_to_all x2, local copies, waits for them, and re-layouts, stream_apply(): lax.all_to_all(flat_source, 'gx', split_axis=2, concat_axis=1, tiled=True)  19.1 us
    all_to_all x2, starting transfers between devices, span_apply(): lax.all_to_all(derived, 'gz', split_axis=2, concat_axis=1, tiled=True)  14.5 us
    all_to_all x2, starting transfers between devices, span_apply(): lax.all_to_all(source, 'gz', split_axis=1, concat_axis=2, tiled=True)  14.4 us
  transfers between devices with their start and end apart: 8, of which 3 were waited for; matrix products, arithmetic and copies ran while one was open for 21% of the time, Pallas kernels for 0%

commit v1 on v0

--- a/solution.py
+++ b/solution.py
@@ -71,7 +71,10 @@
     squares = stream_grad.astype(jnp.float32) ** 2 + wall_grad.astype(jnp.float32) ** 2
     squares = jnp.sum(squares + span_grad.astype(jnp.float32) ** 2, axis=0)
     partial_sum = jnp.sum(strain_wide * squares, axis=0)
-    summed = lax.psum_scatter(partial_sum, "gx", scatter_dimension=1, tiled=True)
+    groups = lax.axis_size("gx")
+    pieces = partial_sum.reshape(span_cells, groups, wall_cells // groups).transpose(1, 0, 2)
+    pieces = lax.all_to_all(pieces.reshape(groups, -1), "gx", 0, 0, tiled=True)
+    summed = jnp.sum(pieces, axis=0).reshape(span_cells, wall_cells // groups)
     gradient = -summed / (stream_cells * lax.axis_size("gx"))
     return (updated, gradient)
 

time: 477 us -> 309 us (0.65)
  blocking collectives: 219 us -> 0 us
  waiting for transfers between devices: 83.6 us -> 120 us
  starting transfers between devices: 61.3 us -> 75.2 us
    unnamed x1 -> x0, blocking collectives: 219 us -> none
    all_to_all x2, waiting for transfers between devices: 32 us -> 62.2 us  [stream_apply(): lax.all_to_all(derived, 'gx', split_axis=1, concat_axis=2, tiled=True)]
    all_to_all x2, starting transfers between devices: 10.2 us -> 19.3 us  [stream_apply(): lax.all_to_all(derived, 'gx', split_axis=1, concat_axis=2, tiled=True)]
    all_to_all x2, waiting for transfers between devices: 0.01 us -> 6.78 us  [span_apply(): lax.all_to_all(derived, 'gz', split_axis=2, concat_axis=1, tiled=True)]
    all_to_all x0 -> x1, starting transfers between devices: none -> 4.83 us  [on_device(): pieces = lax.all_to_all(pieces.reshape(groups, -1), 'gx', 0, 0, tiled=True)]
    unnamed x30 -> x28, local copies, waits for them, and re-layouts: 60.7 us -> 60.8 us
  transfers between devices with their start and end apart: 8 -> 9, of which waited for: 3 -> 5; matrix products, arithmetic and copies ran while one was open for 21% -> 33% of each run, Pallas kernels for 0% -> 0%
where the time goes in v1:
time: 309 us; the launch traced here: 307 us
  waiting for transfers between devices  120 us (39%)
  local copies, waits for them, and re-layouts  101 us (33%)
  starting transfers between devices  75.2 us (24%)
  matrix products  8.46 us (3%)
    all_to_all x2, waiting for transfers between devices, stream_apply(): lax.all_to_all(derived, 'gx', split_axis=1, concat_axis=2, tiled=True)  62.2 us
    unnamed x28, local copies, waits for them, and re-layouts  60.8 us
    all_to_all x2, waiting for transfers between devices, stream_apply(): lax.all_to_all(flat_source, 'gx', split_axis=2, concat_axis=1, tiled=True)  50.6 us
    all_to_all x2, starting transfers between devices, stream_apply(): lax.all_to_all(flat_source, 'gx', split_axis=2, concat_axis=1, tiled=True)  22.2 us
    all_to_all x2, starting transfers between devices, stream_apply(): lax.all_to_all(derived, 'gx', split_axis=1, concat_axis=2, tiled=True)  19.3 us
    all_to_all x2, local copies, waits for them, and re-layouts, stream_apply(): lax.all_to_all(flat_source, 'gx', split_axis=2, concat_axis=1, tiled=True)  19.1 us
    all_to_all x2, starting transfers between devices, span_apply(): lax.all_to_all(derived, 'gz', split_axis=2, concat_axis=1, tiled=True)  14.5 us
    all_to_all x2, starting transfers between devices, span_apply(): lax.all_to_all(source, 'gz', split_axis=1, concat_axis=2, tiled=True)  14.4 us
  transfers between devices with their start and end apart: 9, of which 5 were waited for; matrix products, arithmetic and copies ran while one was open for 33% of the time, Pallas kernels for 0%

profile of v1, /device:TPU:1, one launch (start us, length us, event | category | flops | bytes accessed | tf_op | source)
XLA Modules:
  0.0 306.7 jit_solution(13346077934333092890)
XLA Ops:
  2.5 7.5 %all-to-all-start.4 = ((bf16[3,8,32,256]{3,2,0,1:T(8,128)(2,1)}), bf16[3,8,32,256]{3,2,0,1:T(8,128)(2,1)S(1)}, u32[]{:S(2)}, u32[]{:S(2)}) async-start(bf16[3,8,32,256]{3,2,0,1:T(8,128)(2,1)} %copy.137), calls=%async_computation.4 | async-start | bytes 786432 | tf_op jit(solution)/shard_map/all_to_all | solution.py:50
  10.0 8.6 %copy.124 = bf16[3,8,32,256]{1,0,3,2:T(4,128)(2,1)} copy(bf16[3,8,32,256]{3,2,1,0:T(8,128)(2,1)} %param.7) | data formatting | bytes 786432 | tf_op args[0]
  18.6 13.6 %reshape.208 = bf16[64,2,1536]{2,1,0:T(2,128)(2,1)} reshape(bf16[8192,3,8]{2,1,0:T(4,128)(2,1)} %bitcast.138) | data formatting | bytes 786432
  32.2 16.7 %all-to-all-start = ((bf16[64,2,1536]{2,1,0:T(2,128)(2,1)}), bf16[64,2,1536]{2,1,0:T(2,128)(2,1)S(1)}, u32[]{:S(2)}, u32[]{:S(2)}) async-start(bf16[64,2,1536]{2,1,0:T(2,128)(2,1)} %reshape.208), calls=%async_computation | async-start | bytes 786432 | tf_op jit(solution)/shard_map/all_to_all | solution.py:42
  50.9 25.8 %all-to-all-done = bf16[64,2,1536]{2,1,0:T(2,128)(2,1)S(1)} async-done(((bf16[64,2,1536]{2,1,0:T(2,128)(2,1)}), bf16[64,2,1536]{2,1,0:T(2,128)(2,1)S(1)}, u32[]{:S(2)}, u32[]{:S(2)}) %all-to-all-start) | async-done | bytes 393248 | tf_op jit(solution)/shard_map/all_to_all | solution.py:42
  76.7 7.5 %all-to-all-start.5 = ((bf16[3,1,256,256]{3,0,1,2:T(4,128)(2,1)}), bf16[3,1,256,256]{3,0,1,2:T(4,128)(2,1)S(1)}, u32[]{:S(2)}, u32[]{:S(2)}) async-start(bf16[3,1,256,256]{3,0,1,2:T(4,128)(2,1)} %copy.140), calls=%async_computation.5 | async-start | bytes 1048576 | tf_op jit(solution)/shard_map/all_to_all | solution.py:52
  84.3 10.7 %reshape.209 = bf16[8192,3,8]{2,1,0:T(4,128)(2,1)} reshape(bf16[64,2,1536]{2,1,0:T(2,128)(2,1)S(1)} %all-to-all-done) | data formatting | bytes 786432
  94.9 9.5 %copy.125 = bf16[3,8,8192]{2,1,0:T(8,128)(2,1)S(1)} copy(bf16[3,8,8192]{1,0,2:T(4,128)(2,1)} %bitcast.135) | data formatting | bytes 786432 | tf_op jit(solution)/shard_map/all_to_all | solution.py:42
  107.1 5.0 %all-to-all-start.1 = ((bf16[3,512,128]{2,0,1:T(4,128)(2,1)}), bf16[3,512,128]{2,0,1:T(4,128)(2,1)S(1)}, u32[]{:S(2)}, u32[]{:S(2)}) async-start(bf16[3,512,128]{2,0,1:T(4,128)(2,1)} %copy.128), calls=%async_computation.1 | async-start | bytes 1048576 | tf_op jit(solution)/shard_map/all_to_all | solution.py:44
  113.8 31.3 %all-to-all-done.1 = bf16[3,512,128]{2,0,1:T(4,128)(2,1)S(1)} async-done(((bf16[3,512,128]{2,0,1:T(4,128)(2,1)}), bf16[3,512,128]{2,0,1:T(4,128)(2,1)S(1)}, u32[]{:S(2)}, u32[]{:S(2)}) %all-to-all-start.1) | async-done | bytes 393248 | tf_op jit(solution)/shard_map/all_to_all | solution.py:44
  145.6 2.4 fusion.16
  148.8 6.9 %all-to-all-start.6 = ((bf16[3,8,32,256]{3,2,0,1:T(8,128)(2,1)}), bf16[3,8,32,256]{3,2,0,1:T(8,128)(2,1)S(1)}, u32[]{:S(2)}, u32[]{:S(2)}) async-start(bf16[3,8,32,256]{3,2,0,1:T(8,128)(2,1)} %copy.142), calls=%async_computation.6 | async-start | bytes 786432 | tf_op jit(solution)/shard_map/all_to_all | solution.py:50
  156.7 8.2 %copy.130 = bf16[3,8,8192]{1,0,2:T(4,128)(2,1)} copy(bf16[3,8,8192]{2,1,0:T(8,128)(2,1)S(1)} %fusion.12) | data formatting | bytes 786432 | tf_op jit(solution)/shard_map/convert_element_type | solution.py:61
  164.9 13.6 %reshape.210 = bf16[64,2,1536]{2,1,0:T(2,128)(2,1)} reshape(bf16[8192,3,8]{2,1,0:T(4,128)(2,1)} %bitcast.136) | data formatting | bytes 786432
  178.5 5.5 %all-to-all-start.2 = ((bf16[64,2,1536]{2,1,0:T(2,128)(2,1)}), bf16[64,2,1536]{2,1,0:T(2,128)(2,1)S(1)}, u32[]{:S(2)}, u32[]{:S(2)}) async-start(bf16[64,2,1536]{2,1,0:T(2,128)(2,1)} %reshape.210), calls=%async_computation.2 | async-start | bytes 786432 | tf_op jit(solution)/shard_map/all_to_all | solution.py:42
  186.9 24.8 %all-to-all-done.2 = bf16[64,2,1536]{2,1,0:T(2,128)(2,1)S(1)} async-done(((bf16[64,2,1536]{2,1,0:T(2,128)(2,1)}), bf16[64,2,1536]{2,1,0:T(2,128)(2,1)S(1)}, u32[]{:S(2)}, u32[]{:S(2)}) %all-to-all-start.2) | async-done | bytes 393248 | tf_op jit(solution)/shard_map/all_to_all | solution.py:42
  211.7 4.8 %all-to-all-start.8 = ((f32[64,1,128]{2,1,0:T(1,128)}), f32[64,1,128]{2,1,0:T(1,128)S(1)}, u32[]{:S(2)}, u32[]{:S(2)}) async-start(f32[64,1,128]{2,1,0:T(1,128)} %copy.150), calls=%async_computation.8 | async-start | bytes 65536 | tf_op jit(solution)/shard_map/all_to_all | solution.py:76
  216.6 10.7 %reshape.211 = bf16[8192,3,8]{2,1,0:T(4,128)(2,1)} reshape(bf16[64,2,1536]{2,1,0:T(2,128)(2,1)S(1)} %all-to-all-done.2) | data formatting | bytes 786432
  227.3 9.5 %copy.131 = bf16[3,8,8192]{2,1,0:T(8,128)(2,1)S(1)} copy(bf16[3,8,8192]{1,0,2:T(4,128)(2,1)} %bitcast.137) | data formatting | bytes 786432 | tf_op jit(solution)/shard_map/all_to_all | solution.py:42
  240.0 6.9 %all-to-all-start.7 = ((bf16[3,1,256,256]{3,0,1,2:T(4,128)(2,1)}), bf16[3,1,256,256]{3,0,1,2:T(4,128)(2,1)S(1)}, u32[]{:S(2)}, u32[]{:S(2)}) async-start(bf16[3,1,256,256]{3,0,1,2:T(4,128)(2,1)} %copy.145), calls=%async_computation.7 | async-start | bytes 1048576 | tf_op jit(solution)/shard_map/all_to_all | solution.py:52
  247.0 2.3 fusion.10
  250.4 6.8 %all-to-all-done.7 = bf16[3,1,256,256]{3,0,1,2:T(4,128)(2,1)S(1)} async-done(((bf16[3,1,256,256]{3,0,1,2:T(4,128)(2,1)}), bf16[3,1,256,256]{3,0,1,2:T(4,128)(2,1)S(1)}, u32[]{:S(2)}, u32[]{:S(2)}) %all-to-all-start.7) | async-done | bytes 393248 | tf_op jit(solution)/shard_map/all_to_all | solution.py:52
  257.2 14.3 %all-to-all-start.3 = ((bf16[3,512,128]{2,0,1:T(4,128)(2,1)}), bf16[3,512,128]{2,0,1:T(4,128)(2,1)S(1)}, u32[]{:S(2)}, u32[]{:S(2)}) async-start(bf16[3,512,128]{2,0,1:T(4,128)(2,1)} %copy.134), calls=%async_computation.3 | async-start | bytes 1048576 | tf_op jit(solution)/shard_map/all_to_all | solution.py:44
  273.2 30.9 %all-to-all-done.3 = bf16[3,512,128]{2,0,1:T(4,128)(2,1)S(1)} async-done(((bf16[3,512,128]{2,0,1:T(4,128)(2,1)}), bf16[3,512,128]{2,0,1:T(4,128)(2,1)S(1)}, u32[]{:S(2)}, u32[]{:S(2)}) %all-to-all-start.3) | async-done | bytes 393248 | tf_op jit(solution)/shard_map/all_to_all | solution.py:44
  (77 shorter events, 21.6 us)
Async XLA Ops:
  0.6 104.9 %copy-start = (bf16[512,512]{1,0:T(8,128)(2,1)S(1)}, bf16[512,512]{1,0:T(8,128)(2,1)}, u32[]{:S(2)}) copy-start(bf16[512,512]{1,0:T(8,128)(2,1)} %param.11) | copy-start | bytes 1572868
  2.5 29.7 %all-to-all-start.4 = ((bf16[3,8,32,256]{3,2,0,1:T(8,128)(2,1)}), bf16[3,8,32,256]{3,2,0,1:T(8,128)(2,1)S(1)}, u32[]{:S(2)}, u32[]{:S(2)}) async-start(bf16[3,8,32,256]{3,2,0,1:T(8,128)(2,1)} %copy.137), calls=%async_computation.4 | async-start | bytes 786432 | tf_op jit(solution)/shard_map/all_to_all | solution.py:50
  18.6 30.7 %copy-start.3 = (bf16[256,256]{1,0:T(8,128)(2,1)S(1)}, bf16[256,256]{1,0:T(8,128)(2,1)}, u32[]{:S(2)}) copy-start(bf16[256,256]{1,0:T(8,128)(2,1)} %param.12) | copy-start | bytes 393220
  32.2 44.6 %all-to-all-start = ((bf16[64,2,1536]{2,1,0:T(2,128)(2,1)}), bf16[64,2,1536]{2,1,0:T(2,128)(2,1)S(1)}, u32[]{:S(2)}, u32[]{:S(2)}) async-start(bf16[64,2,1536]{2,1,0:T(2,128)(2,1)} %reshape.208), calls=%async_computation | async-start | bytes 786432 | tf_op jit(solution)/shard_map/all_to_all | solution.py:42
  76.7 30.3 %all-to-all-start.5 = ((bf16[3,1,256,256]{3,0,1,2:T(4,128)(2,1)}), bf16[3,1,256,256]{3,0,1,2:T(4,128)(2,1)S(1)}, u32[]{:S(2)}, u32[]{:S(2)}) async-start(bf16[3,1,256,256]{3,0,1,2:T(4,128)(2,1)} %copy.140), calls=%async_computation.5 | async-start | bytes 1048576 | tf_op jit(solution)/shard_map/all_to_all | solution.py:52
  104.5 7.6 %copy-start.5 = (bf16[8,32,256]{2,1,0:T(8,128)(2,1)S(1)}, bf16[8,32,256]{2,1,0:T(8,128)(2,1)}, u32[]{:S(2)}) copy-start(bf16[8,32,256]{2,1,0:T(8,128)(2,1)} %param.8) | copy-start | bytes 393220
  104.5 7.6 %copy-start.7 = (f32[32,256]{1,0:T(8,128)S(1)}, f32[32,256]{1,0:T(8,128)}, u32[]{:S(2)}) copy-start(f32[32,256]{1,0:T(8,128)} %param.9) | copy-start | bytes 98308
  105.3 40.2 %copy-start.1 = (bf16[3,8,32,256]{3,2,1,0:T(8,128)(2,1)S(1)}, bf16[3,8,32,256]{3,2,1,0:T(8,128)(2,1)}, u32[]{:S(2)}) copy-start(bf16[3,8,32,256]{3,2,1,0:T(8,128)(2,1)} %param.7) | copy-start | bytes 1179652
  105.3 40.2 %copy-start.8 = (f32[256]{0:T(256)S(1)}, f32[256]{0:T(256)}, u32[]{:S(2)}) copy-start(f32[256]{0:T(256)} %param.10) | copy-start | bytes 3076
  107.1 38.0 %all-to-all-start.1 = ((bf16[3,512,128]{2,0,1:T(4,128)(2,1)}), bf16[3,512,128]{2,0,1:T(4,128)(2,1)S(1)}, u32[]{:S(2)}, u32[]{:S(2)}) async-start(bf16[3,512,128]{2,0,1:T(4,128)(2,1)} %copy.128), calls=%async_computation.1 | async-start | bytes 1048576 | tf_op jit(solution)/shard_map/all_to_all | solution.py:44
  148.8 29.7 %all-to-all-start.6 = ((bf16[3,8,32,256]{3,2,0,1:T(8,128)(2,1)}), bf16[3,8,32,256]{3,2,0,1:T(8,128)(2,1)S(1)}, u32[]{:S(2)}, u32[]{:S(2)}) async-start(bf16[3,8,32,256]{3,2,0,1:T(8,128)(2,1)} %copy.142), calls=%async_computation.6 | async-start | bytes 786432 | tf_op jit(solution)/shard_map/all_to_all | solution.py:50
  156.7 27.3 %copy-start.6 = (bf16[8,32,256]{2,1,0:T(8,128)(2,1)S(1)}, bf16[8,32,256]{2,1,0:T(8,128)(2,1)}, u32[]{:S(2)}) copy-start(bf16[8,32,256]{2,1,0:T(8,128)(2,1)} %param.8) | copy-start | bytes 393220
  164.9 20.5 %copy-start.4 = (bf16[256,256]{1,0:T(8,128)(2,1)S(1)}, bf16[256,256]{1,0:T(8,128)(2,1)}, u32[]{:S(2)}) copy-start(bf16[256,256]{1,0:T(8,128)(2,1)} %param.12) | copy-start | bytes 393220
  178.5 33.3 %all-to-all-start.2 = ((bf16[64,2,1536]{2,1,0:T(2,128)(2,1)}), bf16[64,2,1536]{2,1,0:T(2,128)(2,1)S(1)}, u32[]{:S(2)}, u32[]{:S(2)}) async-start(bf16[64,2,1536]{2,1,0:T(2,128)(2,1)} %reshape.210), calls=%async_computation.2 | async-start | bytes 786432 | tf_op jit(solution)/shard_map/all_to_all | solution.py:42
  211.7 28.3 %all-to-all-start.8 = ((f32[64,1,128]{2,1,0:T(1,128)}), f32[64,1,128]{2,1,0:T(1,128)S(1)}, u32[]{:S(2)}, u32[]{:S(2)}) async-start(f32[64,1,128]{2,1,0:T(1,128)} %copy.150), calls=%async_computation.8 | async-start | bytes 65536 | tf_op jit(solution)/shard_map/all_to_all | solution.py:76
  238.8 65.7 %copy-start.2 = (f32[3,8,32,256]{3,2,1,0:T(8,128)S(1)}, f32[3,8,32,256]{3,2,1,0:T(8,128)}, u32[]{:S(2)}) copy-start(f32[3,8,32,256]{3,2,1,0:T(8,128)} %get-tuple-element.48) | copy-start | bytes 2359300
  240.0 17.1 %all-to-all-start.7 = ((bf16[3,1,256,256]{3,0,1,2:T(4,128)(2,1)}), bf16[3,1,256,256]{3,0,1,2:T(4,128)(2,1)S(1)}, u32[]{:S(2)}, u32[]{:S(2)}) async-start(bf16[3,1,256,256]{3,0,1,2:T(4,128)(2,1)} %copy.145), calls=%async_computation.7 | async-start | bytes 1048576 | tf_op jit(solution)/shard_map/all_to_all | solution.py:52
  257.2 46.9 %all-to-all-start.3 = ((bf16[3,512,128]{2,0,1:T(4,128)(2,1)}), bf16[3,512,128]{2,0,1:T(4,128)(2,1)S(1)}, u32[]{:S(2)}, u32[]{:S(2)}) async-start(bf16[3,512,128]{2,0,1:T(4,128)(2,1)} %copy.134), calls=%async_computation.3 | async-start | bytes 1048576 | tf_op jit(solution)/shard_map/all_to_all | solution.py:44

commit v2 on v0

v2 whole, which is shorter than its diff:
```python
import jax
import jax.numpy as jnp
from jax import lax
from jax.sharding import PartitionSpec as P

near_coef = 7.0 / 9.0
far_coef = 1.0 / 36.0
time_step = 0.25
f32 = jnp.float32
bf16 = jnp.bfloat16


def stencil(source, axis):
    widened = source.astype(f32)
    near_diff = jnp.roll(widened, -1, axis) - jnp.roll(widened, 1, axis)
    far_diff = jnp.roll(widened, -2, axis) - jnp.roll(widened, 2, axis)
    return (near_coef * near_diff + far_coef * far_diff).astype(bf16)


def derivative(pencil, operator):
    right_side = stencil(pencil, 1)
    product = jnp.einsum("ij,cjp->cip", operator, right_side, preferred_element_type=f32)
    return product.astype(bf16)


def wall_derivative(source, wall_operator, metric):
    product = jnp.einsum("kxzj,ij->kxzi", source, wall_operator, preferred_element_type=f32)
    return product * metric


def on_device(adjoint, strain, correction, metric, stream_inverse, span_inverse, wall_operator):
    comps, nxl, nzl, ny = adjoint.shape
    gxn = lax.axis_size("gx")
    lanes = nzl * ny // gxn
    yparts = ny // lanes
    nx = nxl * gxn
    strain_wide = strain.astype(f32)
    viscosity = (correction[None] * strain_wide).astype(bf16)
    viscous = viscosity.astype(f32)

    xs = jnp.concatenate([adjoint, strain[None]], axis=0)
    xs = xs.reshape(comps + 1, nxl, nzl, yparts, lanes).transpose(2, 3, 0, 1, 4)
    xs = xs.reshape(gxn, comps + 1, nxl, lanes)
    xt = lax.all_to_all(xs, "gx", 0, 0, tiled=True)
    xt = xt.transpose(1, 0, 2, 3).reshape(comps + 1, nx, lanes)
    stream_strain = xt[comps].astype(f32)
    me = lax.axis_index("gx")
    z_at, y_at = me // yparts, (me % yparts) * lanes
    corr_row = lax.dynamic_slice(correction, (z_at, y_at), (1, lanes))
    stream_visc = (corr_row * stream_strain).astype(bf16).astype(f32)
    stream_grad = derivative(xt[:comps], stream_inverse)
    stream_flux = (stream_visc[None] * stream_grad.astype(f32)).astype(bf16)
    stream_div = derivative(stream_flux, stream_inverse)
    stream_sq = jnp.sum(stream_strain[None] * stream_grad.astype(f32) ** 2, axis=(0, 1))
    back = stream_div.reshape(comps, gxn, nxl, lanes).transpose(1, 0, 2, 3)
    back = lax.all_to_all(back, "gx", 0, 0, tiled=True)
    back = back.reshape(nzl, yparts, comps, nxl, lanes).transpose(2, 3, 0, 1, 4)
    stream_div = back.reshape(comps, nxl, nzl, ny)
    stream_part = lax.dynamic_update_slice(
        jnp.zeros((nzl, ny), f32), stream_sq[None], (z_at, y_at)
    )

    zs = jnp.concatenate([adjoint, viscosity[None], strain[None]], axis=0)
    zt = lax.all_to_all(zs, "gz", 1, 2, tiled=True)[:, 0]
    span_visc = zt[comps].astype(f32)
    span_strain = zt[comps + 1].astype(f32)
    span_grad = derivative(zt[:comps], span_inverse)
    span_flux = (span_visc[None] * span_grad.astype(f32)).astype(bf16)
    span_div = derivative(span_flux, span_inverse)
    span_sq = jnp.sum(span_strain[None] * span_grad.astype(f32) ** 2, axis=0)
    span_div = lax.all_to_all(span_div[:, None], "gz", 2, 1, tiled=True)
    span_part = jnp.sum(lax.all_to_all(span_sq[None], "gz", 1, 0, tiled=True), axis=0)

    wall_grad = wall_derivative(adjoint, wall_operator, metric).astype(bf16)
    wall_flux = (viscous[None] * wall_grad.astype(f32)).astype(bf16)
    wall_div = wall_derivative(wall_flux, wall_operator, metric)
    wall_part = jnp.sum(strain_wide[None] * wall_grad.astype(f32) ** 2, axis=(0, 1))

    total = stream_div.astype(f32) + wall_div
    total = total + span_div.astype(f32)
    updated = (adjoint.astype(f32) + time_step * total).astype(bf16)

    partial_sum = stream_part + span_part + wall_part
    pieces = partial_sum.reshape(nzl, gxn, ny // gxn).transpose(1, 0, 2)
    pieces = lax.all_to_all(pieces.reshape(gxn, -1), "gx", 0, 0, tiled=True)
    summed = jnp.sum(pieces, axis=0).reshape(nzl, ny // gxn)
    gradient = -summed / nx
    return (updated, gradient)


def solution(mesh):
    in_specs = (P(None, "gx", "gz", None), P("gx", "gz", None), P("gz", None), P(), P(), P(), P())
    out_specs = (P(None, "gx", "gz", None), P("gz", "gx"))
    return jax.shard_map(
        on_device, mesh=mesh, in_specs=in_specs, out_specs=out_specs, check_vma=False
    )
```

time: 477 us -> 177 us (0.37); the launches traced: 471 us -> 176 us
  blocking collectives: 219 us -> 17.9 us
  local copies, waits for them, and re-layouts: 97.3 us -> 33.3 us
  starting transfers between devices: 61.3 us -> 38 us
  waiting for transfers between devices: 83.6 us -> 67.3 us
  other arithmetic: 1.12 us -> 8.31 us
    unnamed x1 -> x0, blocking collectives: 219 us -> none
    unnamed x30, local copies, waits for them, and re-layouts: 60.7 us -> 10.6 us
    all_to_all x8 -> x5, starting transfers between devices: 61.3 us -> 38 us  [the longest x1 20.1 us: on_device(): xt = lax.all_to_all(xs, 'gx', 0, 0, tiled=True)]
    all_to_all x0 -> x1, blocking collectives: none -> 17.9 us  [on_device(): zt = lax.all_to_all(zs, 'gz', 1, 2, tiled=True)[:, 0]]
    all_to_all x6 -> x3, local copies, waits for them, and re-layouts: 20.7 us -> 3.48 us  [the longest x1 1.86 us: on_device(): span_div = lax.all_to_all(span_div[:, None], 'gz', 2, 1, tiled=True)]
    all_to_all x8 -> x5, waiting for transfers between devices: 83.6 us -> 67.3 us  [the longest x1 26.9 us: on_device(): xt = lax.all_to_all(xs, 'gx', 0, 0, tiled=True)]
    convert_element_type x10 -> x6, local copies, waits for them, and re-layouts: 14.5 us -> 4.93 us  [the longest x1 1.79 us: on_device(): stream_visc = (corr_row * stream_strain).astype(bf16).astype(f32)]
  transfers between devices with their start and end apart: 8 -> 5, of which waited for: 3 -> 4; matrix products, arithmetic and copies ran while one was open for 21% -> 25% of each run, Pallas kernels for 0% -> 0%
where the time goes in v2:
time: 177 us; the launch traced here: 176 us
  waiting for transfers between devices  67.3 us (38%)
  starting transfers between devices  38 us (21%)
  local copies, waits for them, and re-layouts  33.3 us (19%)
  blocking collectives  17.9 us (10%)
  matrix products  10.2 us (6%)
  other arithmetic  8.31 us (5%)
    all_to_all x1, waiting for transfers between devices, on_device(): xt = lax.all_to_all(xs, 'gx', 0, 0, tiled=True)  26.9 us
    all_to_all x1, waiting for transfers between devices, on_device(): back = lax.all_to_all(back, 'gx', 0, 0, tiled=True)  25 us
    all_to_all x1, starting transfers between devices, on_device(): xt = lax.all_to_all(xs, 'gx', 0, 0, tiled=True)  20.1 us
    all_to_all x1, blocking collectives, on_device(): zt = lax.all_to_all(zs, 'gz', 1, 2, tiled=True)[:, 0]  17.9 us
    unnamed x30, local copies, waits for them, and re-layouts  10.6 us
    all_to_all x1, waiting for transfers between devices, on_device(): pieces = lax.all_to_all(pieces.reshape(gxn, -1), 'gx', 0, 0, tiled=True)  9.85 us
    dot_general x4, matrix products, derivative(): jnp.einsum('ij,cjp->cip', operator, right_side, preferred_element_type=f32)  6.14 us
    all_to_all x1, starting transfers between devices, on_device(): pieces = lax.all_to_all(pieces.reshape(gxn, -1), 'gx', 0, 0, tiled=True)  5.59 us
  transfers between devices with their start and end apart: 5, of which 4 were waited for; matrix products, arithmetic and copies ran while one was open for 25% of the time, Pallas kernels for 0%

profile of v2, /device:TPU:1, one launch (start us, length us, event | category | flops | bytes accessed | tf_op | source)
XLA Modules:
  0.0 175.9 jit_solution(9287657349913188172)
XLA Ops:
  2.7 17.9 %all_to_all.49 = bf16[5,8,32,256]{3,2,0,1:T(8,128)(2,1)S(1)} all-to-all(bf16[5,8,32,256]{3,2,0,1:T(8,128)(2,1)S(1)} %pad_maximum_fusion), channel_id=1, replica_groups=mesh['gx'=64,'gz'=8] {'gz'}, dimensions={1} | all-to-all | bytes 1310720 | tf_op jit(solution)/shard_map/all_to_all | solution.py:64
  23.3 3.4 %all-to-all-start.4 = ((f32[1,256,256]{2,0,1:T(1,128)}), f32[1,256,256]{2,0,1:T(1,128)S(1)}, u32[]{:S(2)}, u32[]{:S(2)}) async-start(f32[1,256,256]{2,0,1:T(1,128)} %broadcast_in_dim.13), calls=%async_computation.4 | async-start | bytes 524288 | tf_op jit(solution)/shard_map/all_to_all | solution.py:72
  28.4 5.6 %all-to-all-done.4 = f32[1,256,256]{2,0,1:T(1,128)S(1)} async-done(((f32[1,256,256]{2,0,1:T(1,128)}), f32[1,256,256]{2,0,1:T(1,128)S(1)}, u32[]{:S(2)}, u32[]{:S(2)}) %all-to-all-start.4) | async-done | bytes 262176 | tf_op jit(solution)/shard_map/all_to_all | solution.py:72
  34.0 20.1 %all-to-all-start = ((bf16[64,4,8,128]{3,2,1,0:T(8,128)(2,1)}), bf16[64,4,8,128]{3,2,1,0:T(8,128)(2,1)S(1)}, u32[]{:S(2)}, u32[]{:S(2)}) async-start(bf16[64,4,8,128]{3,2,1,0:T(8,128)(2,1)} %bitcast.2), calls=%async_computation | async-start | bytes 1048576 | tf_op jit(solution)/shard_map/all_to_all | solution.py:44
  55.4 1.8 %multiply_reduce_fusion = (f32[32,256]{1,0:T(8,128)}, f32[3,8,32,256]{3,2,1,0:T(8,128)}) fusion(f32[8,32,256]{2,1,0:T(8,128)S(1)} %convert_element_type.180, f32[256]{0:T(256)S(1)} %copy-done.8, bf16[3,8,32,256]{3,2,1,0:T(8,128)(2,1)S(1)} %copy-done.1, bf16[256,256]{1,0:T(8,128)(2,1)S(1)} %copy-done.7), kind=kOutput, calls=%fused_computation.44 | convolution fusion | flops 101834752 | bytes 1606656 | tf_op jit(solution)/shard_map/kxzj,ij->kxzi/dot_general | solution.py:27
  59.7 26.9 %all-to-all-done = bf16[64,4,8,128]{3,2,1,0:T(8,128)(2,1)S(1)} async-done(((bf16[64,4,8,128]{3,2,1,0:T(8,128)(2,1)}), bf16[64,4,8,128]{3,2,1,0:T(8,128)(2,1)S(1)}, u32[]{:S(2)}, u32[]{:S(2)}) %all-to-all-start) | async-done | bytes 524320 | tf_op jit(solution)/shard_map/all_to_all | solution.py:44
  86.6 4.1 %all-to-all-start.3 = ((bf16[3,1,256,256]{3,0,1,2:T(4,128)(2,1)}), bf16[3,1,256,256]{3,0,1,2:T(4,128)(2,1)}, u32[]{:S(2)}, u32[]{:S(2)}) async-start(bf16[3,1,256,256]{3,0,1,2:T(4,128)(2,1)} %copy.76), calls=%async_computation.3 | async-start | bytes 1048576 | tf_op jit(solution)/shard_map/all_to_all | solution.py:71
  92.8 1.8 %copy.78 = f32[512,128]{0,1:T(8,128)} copy(f32[512,128]{1,0:T(8,128)} %fusion.42) | data formatting | bytes 524288 | tf_op jit(solution)/shard_map/convert_element_type | solution.py:46
  94.6 1.6 fusion.41
  96.3 1.8 %copy.61 = f32[512,128]{0,1:T(8,128)} copy(f32[512,128]{1,0:T(8,128)} %fusion.41) | data formatting | bytes 524288 | tf_op jit(solution)/shard_map/convert_element_type | solution.py:50
  98.9 2.3 %copy.86 = f32[3,511,128]{1,2,0:T(8,128)} copy(f32[3,511,128]{2,1,0:T(8,128)} %get-tuple-element.45) | data formatting | bytes 1569792
  106.5 2.8 %multiply_reduce_fusion.1 = (f32[128]{0:T(128)S(1)}, f32[3,512,128]{1,2,0:T(8,128)S(1)}) fusion(f32[512,128]{0,1:T(8,128)} %copy.78, f32[512,128]{0,1:T(8,128)} %copy.61, bf16[512,512]{1,0:T(8,128)(2,1)S(1)} %copy-done, f32[3,1,128]{1,2,0:T(8,128)} %copy.87, f32[3,511,128]{1,2,0:T(8,128)S(1)} %copy-done.3, f32[3,511,128]{1,2,0:T(8,128)} %copy.89, ...), kind=kOutput, calls=%fused_computation.45 | convolution fusion | flops 204865408 | bytes 4981248 | tf_op jit(solution)/shard_map/ij,cjp->cip/dot_general | solution.py:22
  113.3 1.4 add.52
  114.6 1.5 copy.79
  116.2 1.6 copy.80
  117.8 1.5 copy.81
  119.3 1.5 fusion.70
  120.7 5.6 %all-to-all-start.5 = ((f32[64,1,128]{2,1,0:T(1,128)}), f32[64,1,128]{2,1,0:T(1,128)S(1)}, u32[]{:S(2)}, u32[]{:S(2)}) async-start(f32[64,1,128]{2,1,0:T(1,128)} %copy.81), calls=%async_computation.5 | async-start | bytes 65536 | tf_op jit(solution)/shard_map/all_to_all | solution.py:85
  126.3 2.4 %fusion.12 = bf16[3,512,128]{1,2,0:T(8,128)(2,1)S(1)} fusion(bf16[512,512]{1,0:T(8,128)(2,1)S(1)} %copy-done, f32[3,1,128]{1,2,0:T(8,128)} %get-tuple-element.35, f32[3,511,128]{1,2,0:T(8,128)S(1)} %get-tuple-element.37, f32[3,511,128]{1,2,0:T(8,128)S(1)} %get-tuple-element.36, f32[3,1,128]{1,2,0:T(8,128)} %get-tuple-element.34, ...), kind=kOutput, calls=%fused_computation.18 | convolution fusion | flops 203489280 | bytes 4063232 | tf_op jit(solution)/shard_map/ij,cjp->cip/dot_general | solution.py:22
  129.8 9.9 %all-to-all-done.5 = f32[64,1,128]{2,1,0:T(1,128)S(1)} async-done(((f32[64,1,128]{2,1,0:T(1,128)}), f32[64,1,128]{2,1,0:T(1,128)S(1)}, u32[]{:S(2)}, u32[]{:S(2)}) %all-to-all-start.5) | async-done | bytes 32800 | tf_op jit(solution)/shard_map/all_to_all | solution.py:85
  139.7 4.7 %all-to-all-start.1 = ((bf16[64,3,8,128]{3,2,1,0:T(8,128)(2,1)}), bf16[64,3,8,128]{3,2,1,0:T(8,128)(2,1)S(1)}, u32[]{:S(2)}, u32[]{:S(2)}) async-start(bf16[64,3,8,128]{3,2,1,0:T(8,128)(2,1)} %copy.71), calls=%async_computation.1 | async-start | bytes 786432 | tf_op jit(solution)/shard_map/all_to_all | solution.py:56
  144.4 1.9 %copy.77 = bf16[3,1,256,256]{3,2,1,0:T(8,128)(2,1)} copy(bf16[3,1,256,256]{3,0,1,2:T(4,128)(2,1)} %all-to-all-done.3) | data formatting | bytes 786432 | tf_op jit(solution)/shard_map/all_to_all | solution.py:71
  147.1 25.0 %all-to-all-done.1 = bf16[64,3,8,128]{3,2,1,0:T(8,128)(2,1)S(1)} async-done(((bf16[64,3,8,128]{3,2,1,0:T(8,128)(2,1)}), bf16[64,3,8,128]{3,2,1,0:T(8,128)(2,1)S(1)}, u32[]{:S(2)}, u32[]{:S(2)}) %all-to-all-start.1) | async-done | bytes 393248 | tf_op jit(solution)/shard_map/all_to_all | solution.py:56
  173.7 2.2 %fusion.6 = bf16[3,8,32,256]{3,2,1,0:T(8,128)(2,1)} fusion(f32[3,8,32,256]{3,2,1,0:T(8,128)S(1)} %reshape.110, bf16[3,8,32,256]{3,2,1,0:T(8,128)(2,1)} %bitcast.94, bf16[3,8,32,256]{3,2,1,0:T(8,128)(2,1)S(1)} %copy-done.1, f32[3,8,32,256]{3,2,1,0:T(8,128)S(1)} %copy-done.2, f32[256]{0:T(256)S(1)} %copy-done.9, f32[8,32,256]{2,1,0:T(8,128)S(1)} %get-tuple-element.48, ...), kind=kOutput, calls=%fused_computation.8 | convolution fusion | flops 102629376 | bytes 3146752 | tf_op jit(solution)/shard_map/kxzj,ij->kxzi/dot_general | solution.py:27
  (75 shorter events, 25.8 us)
Async XLA Ops:
  0.6 105.9 %copy-start = (bf16[512,512]{1,0:T(8,128)(2,1)S(1)}, bf16[512,512]{1,0:T(8,128)(2,1)}, u32[]{:S(2)}) copy-start(bf16[512,512]{1,0:T(8,128)(2,1)} %param.11) | copy-start | bytes 1572868
  0.6 1.1 copy-start.1
  21.0 0.9 copy-start.6
  22.4 4.3 %copy-start.5 = (bf16[8,32,256]{2,1,0:T(8,128)(2,1)S(1)}, bf16[8,32,256]{2,1,0:T(8,128)(2,1)}, u32[]{:S(2)}) copy-start(bf16[8,32,256]{2,1,0:T(8,128)(2,1)} %param.8) | copy-start | bytes 393220
  23.3 10.6 %all-to-all-start.4 = ((f32[1,256,256]{2,0,1:T(1,128)}), f32[1,256,256]{2,0,1:T(1,128)S(1)}, u32[]{:S(2)}, u32[]{:S(2)}) async-start(f32[1,256,256]{2,0,1:T(1,128)} %broadcast_in_dim.13), calls=%async_computation.4 | async-start | bytes 524288 | tf_op jit(solution)/shard_map/all_to_all | solution.py:72
  28.4 27.0 %copy-start.7 = (bf16[256,256]{1,0:T(8,128)(2,1)S(1)}, bf16[256,256]{1,0:T(8,128)(2,1)}, u32[]{:S(2)}) copy-start(bf16[256,256]{1,0:T(8,128)(2,1)} %param.13) | copy-start | bytes 393220
  28.4 27.0 %copy-start.8 = (f32[256]{0:T(256)S(1)}, f32[256]{0:T(256)}, u32[]{:S(2)}) copy-start(f32[256]{0:T(256)} %param.10) | copy-start | bytes 3076
  34.0 52.6 %all-to-all-start = ((bf16[64,4,8,128]{3,2,1,0:T(8,128)(2,1)}), bf16[64,4,8,128]{3,2,1,0:T(8,128)(2,1)S(1)}, u32[]{:S(2)}, u32[]{:S(2)}) async-start(bf16[64,4,8,128]{3,2,1,0:T(8,128)(2,1)} %bitcast.2), calls=%async_computation | async-start | bytes 1048576 | tf_op jit(solution)/shard_map/all_to_all | solution.py:44
  86.6 34.2 %all-to-all-start.3 = ((bf16[3,1,256,256]{3,0,1,2:T(4,128)(2,1)}), bf16[3,1,256,256]{3,0,1,2:T(4,128)(2,1)}, u32[]{:S(2)}, u32[]{:S(2)}) async-start(bf16[3,1,256,256]{3,0,1,2:T(4,128)(2,1)} %copy.76), calls=%async_computation.3 | async-start | bytes 1048576 | tf_op jit(solution)/shard_map/all_to_all | solution.py:71
  90.8 0.9 copy-start.4
  105.2 1.3 copy-start.3
  120.7 18.9 %all-to-all-start.5 = ((f32[64,1,128]{2,1,0:T(1,128)}), f32[64,1,128]{2,1,0:T(1,128)S(1)}, u32[]{:S(2)}, u32[]{:S(2)}) async-start(f32[64,1,128]{2,1,0:T(1,128)} %copy.81), calls=%async_computation.5 | async-start | bytes 65536 | tf_op jit(solution)/shard_map/all_to_all | solution.py:85
  139.7 32.5 %all-to-all-start.1 = ((bf16[64,3,8,128]{3,2,1,0:T(8,128)(2,1)}), bf16[64,3,8,128]{3,2,1,0:T(8,128)(2,1)S(1)}, u32[]{:S(2)}, u32[]{:S(2)}) async-start(bf16[64,3,8,128]{3,2,1,0:T(8,128)(2,1)} %copy.71), calls=%async_computation.1 | async-start | bytes 786432 | tf_op jit(solution)/shard_map/all_to_all | solution.py:56
  172.6 1.1 copy-start.2
  172.6 1.1 copy-start.9

commit v3 on v2

--- a/solution.py
+++ b/solution.py
@@ -23,6 +23,11 @@
     return product.astype(bf16)
 
 
+def row_derivative(pencil, operator):
+    right_side = stencil(pencil, 0)
+    return jnp.dot(operator, right_side, preferred_element_type=f32).astype(bf16)
+
+
 def wall_derivative(source, wall_operator, metric):
     product = jnp.einsum("kxzj,ij->kxzi", source, wall_operator, preferred_element_type=f32)
     return product * metric
@@ -39,26 +44,27 @@
     viscous = viscosity.astype(f32)
 
     xs = jnp.concatenate([adjoint, strain[None]], axis=0)
-    xs = xs.reshape(comps + 1, nxl, nzl, yparts, lanes).transpose(2, 3, 0, 1, 4)
-    xs = xs.reshape(gxn, comps + 1, nxl, lanes)
-    xt = lax.all_to_all(xs, "gx", 0, 0, tiled=True)
-    xt = xt.transpose(1, 0, 2, 3).reshape(comps + 1, nx, lanes)
-    stream_strain = xt[comps].astype(f32)
+    xs = xs.reshape(comps + 1, nxl, nzl, yparts, lanes).transpose(2, 3, 1, 0, 4)
+    xs = xs.reshape(gxn, nxl, (comps + 1) * lanes)
+    xt = lax.all_to_all(xs, "gx", 0, 0, tiled=True).reshape(nx, (comps + 1) * lanes)
+    stream_strain = xt[:, comps * lanes:].astype(f32)
     me = lax.axis_index("gx")
-    z_at, y_at = me // yparts, (me % yparts) * lanes
-    corr_row = lax.dynamic_slice(correction, (z_at, y_at), (1, lanes))
+    z_at, y_at = me // yparts, me % yparts
+    corr_row = lax.dynamic_slice(correction, (z_at, y_at * lanes), (1, lanes))
     stream_visc = (corr_row * stream_strain).astype(bf16).astype(f32)
-    stream_grad = derivative(xt[:comps], stream_inverse)
-    stream_flux = (stream_visc[None] * stream_grad.astype(f32)).astype(bf16)
-    stream_div = derivative(stream_flux, stream_inverse)
-    stream_sq = jnp.sum(stream_strain[None] * stream_grad.astype(f32) ** 2, axis=(0, 1))
-    back = stream_div.reshape(comps, gxn, nxl, lanes).transpose(1, 0, 2, 3)
-    back = lax.all_to_all(back, "gx", 0, 0, tiled=True)
-    back = back.reshape(nzl, yparts, comps, nxl, lanes).transpose(2, 3, 0, 1, 4)
+    stream_visc = jnp.tile(stream_visc, (1, comps))
+    stream_grad = row_derivative(xt[:, : comps * lanes], stream_inverse)
+    stream_flux = (stream_visc * stream_grad.astype(f32)).astype(bf16)
+    stream_div = row_derivative(stream_flux, stream_inverse)
+    stream_sq = (stream_grad.astype(f32) ** 2).reshape(nx, comps, lanes).sum(axis=1)
+    stream_sq = jnp.sum(stream_strain * stream_sq, axis=0)
+    back = lax.all_to_all(stream_div.reshape(gxn, nxl, comps * lanes), "gx", 0, 0, tiled=True)
+    back = back.reshape(nzl, yparts, nxl, comps, lanes).transpose(3, 2, 0, 1, 4)
     stream_div = back.reshape(comps, nxl, nzl, ny)
-    stream_part = lax.dynamic_update_slice(
-        jnp.zeros((nzl, ny), f32), stream_sq[None], (z_at, y_at)
-    )
+    z_ids = lax.broadcasted_iota(jnp.int32, (nzl, yparts, lanes), 0)
+    y_ids = lax.broadcasted_iota(jnp.int32, (nzl, yparts, lanes), 1)
+    owned = (z_ids == z_at) & (y_ids == y_at)
+    stream_part = jnp.where(owned, stream_sq[None, None], 0.0).reshape(nzl, ny)
 
     zs = jnp.concatenate([adjoint, viscosity[None], strain[None]], axis=0)
     zt = lax.all_to_all(zs, "gz", 1, 2, tiled=True)[:, 0]
@@ -81,9 +87,9 @@
     updated = (adjoint.astype(f32) + time_step * total).astype(bf16)
 
     partial_sum = stream_part + span_part + wall_part
-    pieces = partial_sum.reshape(nzl, gxn, ny // gxn).transpose(1, 0, 2)
-    pieces = lax.all_to_all(pieces.reshape(gxn, -1), "gx", 0, 0, tiled=True)
-    summed = jnp.sum(pieces, axis=0).reshape(nzl, ny // gxn)
+    pieces = partial_sum.T.reshape(gxn, -1)
+    pieces = lax.all_to_all(pieces, "gx", 0, 0, tiled=True)
+    summed = jnp.sum(pieces, axis=0).reshape(ny // gxn, nzl).T
     gradient = -summed / nx
     return (updated, gradient)
 

time: 177 us -> 162 us (0.915)
  local copies, waits for them, and re-layouts: 33.3 us -> 17.9 us
  waiting for transfers between devices: 67.3 us -> 69.3 us
    unnamed x30 -> x21, local copies, waits for them, and re-layouts: 10.6 us -> 1.66 us
    dot_general x0 -> x2, matrix products: none -> 5.68 us  [row_derivative(): jnp.dot(operator, right_side, preferred_element_type=f32).astype(bf16)]
    dot_general x4 -> x2, matrix products: 6.14 us -> 0.98 us  [derivative(): jnp.einsum('ij,cjp->cip', operator, right_side, preferred_element_type=f32)]
    reduce_sum x1 -> x3, other arithmetic: 0.08 us -> 3.06 us  [the longest x1 1.92 us: on_device(): (stream_grad.astype(f32) ** 2).reshape(nx, comps, lanes).sum(axis=1)]
    convert_element_type x3 -> x1, local copies, waits for them, and re-layouts: 3.82 us -> 0.94 us  [row_derivative(): jnp.dot(operator, right_side, preferred_element_type=f32).astype(bf16)]
    add x2 -> x1, local copies, waits for them, and re-layouts: 2.8 us -> 0.1 us  [on_device(): partial_sum = stream_part + span_part + wall_part]
    transpose x2 -> x0, local copies, waits for them, and re-layouts: 2.43 us -> none  [the longest x1 1.61 us: on_device(): pieces = partial_sum.reshape(nzl, gxn, ny // gxn).transpose(1, 0, 2)]
    slice x8, local copies, waits for them, and re-layouts: 2.39 us -> 4.64 us  [stencil(): near_diff = jnp.roll(widened, -1, axis) - jnp.roll(widened, 1, axis)]
  transfers between devices with their start and end apart: 5 -> 5, of which waited for: 4 -> 4; matrix products, arithmetic and copies ran while one was open for 25% -> 16% of each run, Pallas kernels for 0% -> 0%
where the time goes in v3:
time: 162 us; the launch traced here: 161 us
  waiting for transfers between devices  69.3 us (43%)
  starting transfers between devices  38.1 us (24%)
  local copies, waits for them, and re-layouts  17.9 us (11%)
  blocking collectives  17.9 us (11%)
  matrix products  10.1 us (6%)
  other arithmetic  6.95 us (4%)
    all_to_all x1, waiting for transfers between devices, on_device(): lax.all_to_all(xs, 'gx', 0, 0, tiled=True).reshape(nx, (comps + 1) * lanes)  28.5 us
    all_to_all x1, waiting for transfers between devices, on_device(): lax.all_to_all(stream_div.reshape(gxn, nxl, comps * lanes), 'gx', 0, 0, t...  25.1 us
    all_to_all x1, starting transfers between devices, on_device(): lax.all_to_all(xs, 'gx', 0, 0, tiled=True).reshape(nx, (comps + 1) * lanes)  20.1 us
    all_to_all x1, blocking collectives, on_device(): zt = lax.all_to_all(zs, 'gz', 1, 2, tiled=True)[:, 0]  17.9 us
    all_to_all x1, waiting for transfers between devices, on_device(): pieces = lax.all_to_all(pieces, 'gx', 0, 0, tiled=True)  10.1 us
    dot_general x2, matrix products, row_derivative(): jnp.dot(operator, right_side, preferred_element_type=f32).astype(bf16)  5.68 us
    all_to_all x1, starting transfers between devices, on_device(): pieces = lax.all_to_all(pieces, 'gx', 0, 0, tiled=True)  5.58 us
    all_to_all x1, waiting for transfers between devices, on_device(): lax.all_to_all(span_sq[None], 'gz', 1, 0, tiled=True)  5.57 us
  transfers between devices with their start and end apart: 5, of which 4 were waited for; matrix products, arithmetic and copies ran while one was open for 16% of the time, Pallas kernels for 0%

profile of v3, /device:TPU:1, one launch (start us, length us, event | category | flops | bytes accessed | tf_op | source)
XLA Modules:
  0.0 161.1 jit_solution(12862687627070958672)
XLA Ops:
  0.7 1.7 %fusion.47 = (f32[8,32,256]{2,1,0:T(8,128)}, bf16[1,8,32,256]{3,2,0,1:T(8,128)(2,1)S(1)}) fusion(bf16[8,32,256]{2,1,0:T(8,128)(2,1)} %param.8, f32[32,256]{1,0:T(8,128)} %param.9), kind=kLoop, calls=%fused_computation.71 | loop fusion | flops 262144 | bytes 557056 | tf_op jit(solution)/shard_map/convert_element_type | solution.py:44
  2.4 0.9 pad_maximum_fusion
  3.3 17.9 %all_to_all.49 = bf16[5,8,32,256]{3,2,0,1:T(8,128)(2,1)S(1)} all-to-all(bf16[5,8,32,256]{3,2,0,1:T(8,128)(2,1)S(1)} %pad_maximum_fusion), channel_id=1, replica_groups=mesh['gx'=64,'gz'=8] {'gz'}, dimensions={1} | all-to-all | bytes 1310720 | tf_op jit(solution)/shard_map/all_to_all | solution.py:70
  23.9 3.5 %all-to-all-start.4 = ((f32[1,256,256]{2,0,1:T(1,128)}), f32[1,256,256]{2,0,1:T(1,128)S(1)}, u32[]{:S(2)}, u32[]{:S(2)}) async-start(f32[1,256,256]{2,0,1:T(1,128)} %broadcast_in_dim.44), calls=%async_computation.4 | async-start | bytes 524288 | tf_op jit(solution)/shard_map/all_to_all | solution.py:78
  29.1 5.6 %all-to-all-done.4 = f32[1,256,256]{2,0,1:T(1,128)S(1)} async-done(((f32[1,256,256]{2,0,1:T(1,128)}), f32[1,256,256]{2,0,1:T(1,128)S(1)}, u32[]{:S(2)}, u32[]{:S(2)}) %all-to-all-start.4) | async-done | bytes 262176 | tf_op jit(solution)/shard_map/all_to_all | solution.py:78
  34.7 20.1 %all-to-all-start = ((bf16[64,8,512]{2,1,0:T(8,128)(2,1)}), bf16[64,8,512]{2,1,0:T(8,128)(2,1)S(1)}, u32[]{:S(2)}, u32[]{:S(2)}) async-start(bf16[64,8,512]{2,1,0:T(8,128)(2,1)} %bitcast.2), calls=%async_computation | async-start | bytes 1048576 | tf_op jit(solution)/shard_map/all_to_all | solution.py:49
  55.7 1.2 multiply_reduce_fusion
  57.7 1.1 copy.43
  58.8 28.5 %all-to-all-done = bf16[64,8,512]{2,1,0:T(8,128)(2,1)S(1)} async-done(((bf16[64,8,512]{2,1,0:T(8,128)(2,1)}), bf16[64,8,512]{2,1,0:T(8,128)(2,1)S(1)}, u32[]{:S(2)}, u32[]{:S(2)}) %all-to-all-start) | async-done | bytes 524320 | tf_op jit(solution)/shard_map/all_to_all | solution.py:49
  87.3 4.1 %all-to-all-start.3 = ((bf16[3,1,256,256]{3,0,1,2:T(4,128)(2,1)}), bf16[3,1,256,256]{3,0,1,2:T(4,128)(2,1)}, u32[]{:S(2)}, u32[]{:S(2)}) async-start(bf16[3,1,256,256]{3,0,1,2:T(4,128)(2,1)} %copy.43), calls=%async_computation.3 | async-start | bytes 1048576 | tf_op jit(solution)/shard_map/all_to_all | solution.py:77
  91.7 1.1 fusion.74
  92.8 1.3 fusion.76
  95.2 3.4 %fusion.31 = (f32[512,384]{0,1:T(8,128)S(1)}, f32[512,384]{0,1:T(8,128)}) fusion(f32[512,128]{0,1:T(8,128)S(1)} %fusion.41, bf16[512,512]{1,0:T(8,128)(2,1)S(1)} %copy-done, f32[1,384]{0,1:T(8,128)} %get-tuple-element.37, f32[511,384]{0,1:T(8,128)} %get-tuple-element.39, f32[511,384]{0,1:T(8,128)} %get-tuple-element.38, f32[1,384]{0,1:T(8,128)} %get-tuple-element.36, ...), kind=kOutput, calls=%fused_computation.53 | convolution fusion | flops 204472320 | bytes 5505024 | tf_op jit(solution)/shard_map/dot_general | solution.py:28
  100.6 1.9 %reduce_sum.58 = f32[512,128]{0,1:T(8,128)} reduce(f32[512,3,128]{0,2,1:T(8,128)} %bitcast.79, f32[]{:T(128)} %constant.48.clone.1), dimensions={1}, to_apply=%region_0.1 | reduce | flops 131072 | bytes 1048580 | tf_op jit(solution)/shard_map/reduce_sum | solution.py:59
  102.5 1.1 fusion.40
  104.4 1.5 fusion.71
  105.9 5.6 %all-to-all-start.5 = ((f32[64,1,128]{2,1,0:T(1,128)}), f32[64,1,128]{2,1,0:T(1,128)S(1)}, u32[]{:S(2)}, u32[]{:S(2)}) async-start(f32[64,1,128]{2,1,0:T(1,128)} %bitcast.27), calls=%async_computation.5 | async-start | bytes 65536 | tf_op jit(solution)/shard_map/all_to_all | solution.py:91
  111.5 2.3 %fusion.12 = bf16[512,384]{0,1:T(8,128)(2,1)S(1)} fusion(bf16[512,512]{1,0:T(8,128)(2,1)S(1)} %copy-done, f32[1,384]{0,1:T(8,128)} %get-tuple-element.27, f32[511,384]{0,1:T(8,128)} %get-tuple-element.29, f32[511,384]{0,1:T(8,128)} %get-tuple-element.28, f32[1,384]{0,1:T(8,128)} %get-tuple-element.26, f32[2,384]{0,1:T(8,128)} %get-tuple-element.23, ...), kind=kOutput, calls=%fused_computation.18 | convolution fusion | flops 203489280 | bytes 4063232 | tf_op jit(solution)/shard_map/dot_general | solution.py:28
  113.8 0.9 copy.38
  114.7 10.1 %all-to-all-done.5 = f32[64,1,128]{2,1,0:T(1,128)S(1)} async-done(((f32[64,1,128]{2,1,0:T(1,128)}), f32[64,1,128]{2,1,0:T(1,128)S(1)}, u32[]{:S(2)}, u32[]{:S(2)}) %all-to-all-start.5) | async-done | bytes 32800 | tf_op jit(solution)/shard_map/all_to_all | solution.py:91
  124.8 4.7 %all-to-all-start.1 = ((bf16[64,8,384]{2,1,0:T(8,128)(2,1)}), bf16[64,8,384]{2,1,0:T(8,128)(2,1)S(1)}, u32[]{:S(2)}, u32[]{:S(2)}) async-start(bf16[64,8,384]{2,1,0:T(8,128)(2,1)} %bitcast.7), calls=%async_computation.1 | async-start | bytes 786432 | tf_op jit(solution)/shard_map/all_to_all | solution.py:61
  129.5 1.9 %copy.44 = bf16[3,1,256,256]{3,2,1,0:T(8,128)(2,1)} copy(bf16[3,1,256,256]{3,0,1,2:T(4,128)(2,1)} %all-to-all-done.3) | data formatting | bytes 786432 | tf_op jit(solution)/shard_map/all_to_all | solution.py:77
  132.1 25.1 %all-to-all-done.1 = bf16[64,8,384]{2,1,0:T(8,128)(2,1)S(1)} async-done(((bf16[64,8,384]{2,1,0:T(8,128)(2,1)}), bf16[64,8,384]{2,1,0:T(8,128)(2,1)S(1)}, u32[]{:S(2)}, u32[]{:S(2)}) %all-to-all-start.1) | async-done | bytes 393248 | tf_op jit(solution)/shard_map/all_to_all | solution.py:61
  158.9 2.2 %fusion.6 = bf16[3,8,32,256]{3,2,1,0:T(8,128)(2,1)} fusion(f32[3,8,32,256]{3,2,1,0:T(8,128)S(1)} %reshape.85, bf16[3,8,32,256]{3,2,1,0:T(8,128)(2,1)} %bitcast.85, bf16[3,8,32,256]{3,2,1,0:T(8,128)(2,1)S(1)} %copy-done.1, f32[3,8,32,256]{3,2,1,0:T(8,128)S(1)} %copy-done.2, f32[256]{0:T(256)S(1)} %copy-done.8, f32[8,32,256]{2,1,0:T(8,128)S(1)} %copy-done.4, ...), kind=kOutput, calls=%fused_computation.8 | convolution fusion | flops 102629376 | bytes 3146752 | tf_op jit(solution)/shard_map/kxzj,ij->kxzi/dot_general | solution.py:32
  (65 shorter events, 12.4 us)
Async XLA Ops:
  0.6 94.6 %copy-start = (bf16[512,512]{1,0:T(8,128)(2,1)S(1)}, bf16[512,512]{1,0:T(8,128)(2,1)}, u32[]{:S(2)}) copy-start(bf16[512,512]{1,0:T(8,128)(2,1)} %param.11) | copy-start | bytes 1572868
  0.6 1.7 %copy-start.1 = (bf16[3,8,32,256]{3,2,1,0:T(8,128)(2,1)S(1)}, bf16[3,8,32,256]{3,2,1,0:T(8,128)(2,1)}, u32[]{:S(2)}) copy-start(bf16[3,8,32,256]{3,2,1,0:T(8,128)(2,1)} %param.7) | copy-start | bytes 1179652
  21.6 0.9 copy-start.6
  23.9 3.7 %copy-start.3 = (bf16[8,32,256]{2,1,0:T(8,128)(2,1)S(1)}, bf16[8,32,256]{2,1,0:T(8,128)(2,1)}, u32[]{:S(2)}) copy-start(bf16[8,32,256]{2,1,0:T(8,128)(2,1)} %param.8) | copy-start | bytes 393220
  23.9 10.8 %all-to-all-start.4 = ((f32[1,256,256]{2,0,1:T(1,128)}), f32[1,256,256]{2,0,1:T(1,128)S(1)}, u32[]{:S(2)}, u32[]{:S(2)}) async-start(f32[1,256,256]{2,0,1:T(1,128)} %broadcast_in_dim.44), calls=%async_computation.4 | async-start | bytes 524288 | tf_op jit(solution)/shard_map/all_to_all | solution.py:78
  29.1 26.6 %copy-start.7 = (bf16[256,256]{1,0:T(8,128)(2,1)S(1)}, bf16[256,256]{1,0:T(8,128)(2,1)}, u32[]{:S(2)}) copy-start(bf16[256,256]{1,0:T(8,128)(2,1)} %param.13) | copy-start | bytes 393220
  29.1 26.6 %copy-start.8 = (f32[256]{0:T(256)S(1)}, f32[256]{0:T(256)}, u32[]{:S(2)}) copy-start(f32[256]{0:T(256)} %param.10) | copy-start | bytes 3076
  34.7 52.6 %all-to-all-start = ((bf16[64,8,512]{2,1,0:T(8,128)(2,1)}), bf16[64,8,512]{2,1,0:T(8,128)(2,1)S(1)}, u32[]{:S(2)}, u32[]{:S(2)}) async-start(bf16[64,8,512]{2,1,0:T(8,128)(2,1)} %bitcast.2), calls=%async_computation | async-start | bytes 1048576 | tf_op jit(solution)/shard_map/all_to_all | solution.py:49
  87.3 18.6 %all-to-all-start.3 = ((bf16[3,1,256,256]{3,0,1,2:T(4,128)(2,1)}), bf16[3,1,256,256]{3,0,1,2:T(4,128)(2,1)}, u32[]{:S(2)}, u32[]{:S(2)}) async-start(bf16[3,1,256,256]{3,0,1,2:T(4,128)(2,1)} %copy.43), calls=%async_computation.3 | async-start | bytes 1048576 | tf_op jit(solution)/shard_map/all_to_all | solution.py:77
  104.4 7.1 %copy-start.5 = (f32[2,384]{0,1:T(8,128)S(1)}, f32[2,384]{0,1:T(8,128)}, u32[]{:S(2)}) copy-start(f32[2,384]{0,1:T(8,128)} %get-tuple-element.22) | copy-start | bytes 9220
  105.9 18.9 %all-to-all-start.5 = ((f32[64,1,128]{2,1,0:T(1,128)}), f32[64,1,128]{2,1,0:T(1,128)S(1)}, u32[]{:S(2)}, u32[]{:S(2)}) async-start(f32[64,1,128]{2,1,0:T(1,128)} %bitcast.27), calls=%async_computation.5 | async-start | bytes 65536 | tf_op jit(solution)/shard_map/all_to_all | solution.py:91
  124.8 32.5 %all-to-all-start.1 = ((bf16[64,8,384]{2,1,0:T(8,128)(2,1)}), bf16[64,8,384]{2,1,0:T(8,128)(2,1)S(1)}, u32[]{:S(2)}, u32[]{:S(2)}) async-start(bf16[64,8,384]{2,1,0:T(8,128)(2,1)} %bitcast.7), calls=%async_computation.1 | async-start | bytes 786432 | tf_op jit(solution)/shard_map/all_to_all | solution.py:61
  157.7 1.1 copy-start.2
  157.7 1.2 copy-start.4

commit v4 on v3

--- a/solution.py
+++ b/solution.py
@@ -21,6 +21,15 @@
     right_side = stencil(pencil, 1)
     product = jnp.einsum("ij,cjp->cip", operator, right_side, preferred_element_type=f32)
     return product.astype(bf16)
+
+
+def split_wide(value):
+    high = lax.reduce_precision(value, exponent_bits=8, mantissa_bits=7)
+    return jnp.stack([high.astype(bf16), (value - high).astype(bf16)])
+
+
+def join_wide(parts):
+    return parts[0].astype(f32) + parts[1].astype(f32)
 
 
 def row_derivative(pencil, operator):
@@ -58,9 +67,6 @@
     stream_div = row_derivative(stream_flux, stream_inverse)
     stream_sq = (stream_grad.astype(f32) ** 2).reshape(nx, comps, lanes).sum(axis=1)
     stream_sq = jnp.sum(stream_strain * stream_sq, axis=0)
-    back = lax.all_to_all(stream_div.reshape(gxn, nxl, comps * lanes), "gx", 0, 0, tiled=True)
-    back = back.reshape(nzl, yparts, nxl, comps, lanes).transpose(3, 2, 0, 1, 4)
-    stream_div = back.reshape(comps, nxl, nzl, ny)
     z_ids = lax.broadcasted_iota(jnp.int32, (nzl, yparts, lanes), 0)
     y_ids = lax.broadcasted_iota(jnp.int32, (nzl, yparts, lanes), 1)
     owned = (z_ids == z_at) & (y_ids == y_at)
@@ -74,22 +80,31 @@
     span_flux = (span_visc[None] * span_grad.astype(f32)).astype(bf16)
     span_div = derivative(span_flux, span_inverse)
     span_sq = jnp.sum(span_strain[None] * span_grad.astype(f32) ** 2, axis=0)
-    span_div = lax.all_to_all(span_div[:, None], "gz", 2, 1, tiled=True)
-    span_part = jnp.sum(lax.all_to_all(span_sq[None], "gz", 1, 0, tiled=True), axis=0)
+    span_back = jnp.concatenate([span_div, split_wide(span_sq)], axis=0)
+    span_back = lax.all_to_all(span_back[:, None], "gz", 2, 1, tiled=True)
+    span_div = span_back[:comps]
+    span_part = jnp.sum(join_wide(span_back[comps:]), axis=0)
 
     wall_grad = wall_derivative(adjoint, wall_operator, metric).astype(bf16)
     wall_flux = (viscous[None] * wall_grad.astype(f32)).astype(bf16)
     wall_div = wall_derivative(wall_flux, wall_operator, metric)
     wall_part = jnp.sum(strain_wide[None] * wall_grad.astype(f32) ** 2, axis=(0, 1))
 
+    partial_sum = stream_part + span_part + wall_part
+    pieces = split_wide(partial_sum.T.reshape(gxn, -1))
+    extra = jnp.zeros((gxn, nxl - 2, lanes), bf16)
+    extra = jnp.concatenate([pieces[0][:, None], pieces[1][:, None], extra], axis=1)
+    back = jnp.concatenate([stream_div.reshape(gxn, nxl, comps * lanes), extra], axis=2)
+    back = lax.all_to_all(back, "gx", 0, 0, tiled=True)
+    summed = jnp.sum(join_wide(back[:, :2, comps * lanes:].transpose(1, 0, 2)), axis=0)
+    summed = summed.reshape(ny // gxn, nzl).T
+    back = back[:, :, : comps * lanes].reshape(nzl, yparts, nxl, comps, lanes)
+    stream_div = back.transpose(3, 2, 0, 1, 4).reshape(comps, nxl, nzl, ny)
+
     total = stream_div.astype(f32) + wall_div
     total = total + span_div.astype(f32)
     updated = (adjoint.astype(f32) + time_step * total).astype(bf16)
 
-    partial_sum = stream_part + span_part + wall_part
-    pieces = partial_sum.T.reshape(gxn, -1)
-    pieces = lax.all_to_all(pieces, "gx", 0, 0, tiled=True)
-    summed = jnp.sum(pieces, axis=0).reshape(ny // gxn, nzl).T
     gradient = -summed / nx
     return (updated, gradient)
 

time: 162 us -> 159 us (0.981)
  starting transfers between devices: 38.1 us -> 29.9 us
  local copies, waits for them, and re-layouts: 17.9 us -> 20.4 us
  waiting for transfers between devices: 69.3 us -> 71.2 us
    all_to_all x4 -> x2, starting transfers between devices: 18 us -> 9.37 us  [the longest x1 5.68 us: on_device(): back = lax.all_to_all(back, 'gx', 0, 0, tiled=True)]
    unnamed x21 -> x35, local copies, waits for them, and re-layouts: 1.66 us -> 4.63 us
    all_to_all x4 -> x2, waiting for transfers between devices: 40.8 us -> 43.7 us  [the longest x1 32.1 us: on_device(): back = lax.all_to_all(back, 'gx', 0, 0, tiled=True)]
    all_to_all x2 -> x0, local copies, waits for them, and re-layouts: 2.57 us -> none  [the longest x1 1.87 us: on_device(): span_div = lax.all_to_all(span_div[:, None], 'gz', 2, 1, tiled=True)]
    dot_general x2, matrix products: 5.68 us -> 3.31 us  [row_derivative(): jnp.dot(operator, right_side, preferred_element_type=f32).astype(bf16)]
    reduce_sum x1, other arithmetic: 1.92 us -> 0.06 us  [on_device(): (stream_grad.astype(f32) ** 2).reshape(nx, comps, lanes).sum(axis=1)]
    dot_general x2, matrix products: 0.98 us -> 2.81 us  [derivative(): jnp.einsum('ij,cjp->cip', operator, right_side, preferred_element_type=f32)]
  transfers between devices with their start and end apart: 5 -> 3, of which waited for: 4 -> 3; matrix products, arithmetic and copies ran while one was open for 16% -> 5% of each run, Pallas kernels for 0% -> 0%
where the time goes in v4:
time: 159 us; the launch traced here: 158 us
  waiting for transfers between devices  71.2 us (45%)
  starting transfers between devices  29.9 us (19%)
  local copies, waits for them, and re-layouts  20.4 us (13%)
  blocking collectives  17.9 us (11%)
  matrix products  10.2 us (6%)
  other arithmetic  7.42 us (5%)
    all_to_all x1, waiting for transfers between devices, on_device(): back = lax.all_to_all(back, 'gx', 0, 0, tiled=True)  32.1 us
    all_to_all x1, waiting for transfers between devices, on_device(): lax.all_to_all(xs, 'gx', 0, 0, tiled=True).reshape(nx, (comps + 1) * lanes)  27.5 us
    all_to_all x1, starting transfers between devices, on_device(): lax.all_to_all(xs, 'gx', 0, 0, tiled=True).reshape(nx, (comps + 1) * lanes)  20.5 us
    all_to_all x1, blocking collectives, on_device(): zt = lax.all_to_all(zs, 'gz', 1, 2, tiled=True)[:, 0]  17.9 us
    all_to_all x1, waiting for transfers between devices, on_device(): span_back = lax.all_to_all(span_back[:, None], 'gz', 2, 1, tiled=True)  11.7 us
    all_to_all x1, starting transfers between devices, on_device(): back = lax.all_to_all(back, 'gx', 0, 0, tiled=True)  5.68 us
    unnamed x35, local copies, waits for them, and re-layouts  4.63 us
    slice x8, local copies, waits for them, and re-layouts, stencil(): near_diff = jnp.roll(widened, -1, axis) - jnp.roll(widened, 1, axis)  4.59 us
  transfers between devices with their start and end apart: 3, of which 3 were waited for; matrix products, arithmetic and copies ran while one was open for 5% of the time, Pallas kernels for 0%

profile of v4, /device:TPU:1, one launch (start us, length us, event | category | flops | bytes accessed | tf_op | source)
XLA Modules:
  0.0 158.0 jit_solution(5447469259278901918)
XLA Ops:
  0.6 1.7 %fusion.47 = (f32[8,32,256]{2,1,0:T(8,128)}, bf16[1,8,32,256]{3,2,0,1:T(8,128)(2,1)S(1)}) fusion(bf16[8,32,256]{2,1,0:T(8,128)(2,1)} %param.8, f32[32,256]{1,0:T(8,128)} %param.9), kind=kLoop, calls=%fused_computation.76 | loop fusion | flops 262144 | bytes 557056 | tf_op jit(solution)/shard_map/convert_element_type | solution.py:53
  2.3 1.1 pad_maximum_fusion
  3.5 17.9 %all_to_all.28 = bf16[5,8,32,256]{3,2,0,1:T(8,128)(2,1)S(1)} all-to-all(bf16[5,8,32,256]{3,2,0,1:T(8,128)(2,1)S(1)} %pad_maximum_fusion), channel_id=1, replica_groups=mesh['gx'=64,'gz'=8] {'gz'}, dimensions={1} | all-to-all | bytes 1310720 | tf_op jit(solution)/shard_map/all_to_all | solution.py:76
  22.6 1.2 fusion.30
  24.0 1.3 fusion.72
  26.2 0.9 copy-done.3
  27.0 1.6 %fusion.11 = bf16[3,256,256]{1,2,0:T(8,128)(2,1)S(1)} fusion(f32[3,1,256]{2,1,0:T(1,128)} %get-tuple-element.19, f32[3,255,256]{2,1,0:T(8,128)} %get-tuple-element.21, f32[3,255,256]{2,1,0:T(8,128)S(1)} %copy-done.3, f32[3,1,256]{2,1,0:T(1,128)} %get-tuple-element.18, f32[3,2,256]{2,1,0:T(2,128)S(1)} %get-tuple-element.15, ...), kind=kOutput, calls=%fused_computation.17 | convolution fusion | flops 102825984 | bytes 3670016 | tf_op jit(solution)/shard_map/ij,cjp->cip/dot_general | solution.py:22
  28.7 1.7 %copy.50 = bf16[5,1,256,256]{3,0,1,2:T(8,128)(2,1)} copy(bf16[5,1,256,256]{2,3,0,1:T(8,128)(2,1)S(1)} %maximum_bitcast_fusion) | data formatting | bytes 1310720 | tf_op jit(solution)/shard_map/broadcast_in_dim | solution.py:84
  30.5 3.7 %all-to-all-start.2 = ((bf16[5,1,256,256]{3,0,1,2:T(8,128)(2,1)}), bf16[5,1,256,256]{3,0,1,2:T(8,128)(2,1)S(1)}, u32[]{:S(2)}, u32[]{:S(2)}) async-start(bf16[5,1,256,256]{3,0,1,2:T(8,128)(2,1)} %copy.50), calls=%async_computation.2 | async-start | bytes 2097152 | tf_op jit(solution)/shard_map/all_to_all | solution.py:84
  35.0 0.9 pad_maximum_fusion.1
  35.9 11.7 %all-to-all-done.2 = bf16[5,1,256,256]{3,0,1,2:T(8,128)(2,1)S(1)} async-done(((bf16[5,1,256,256]{3,0,1,2:T(8,128)(2,1)}), bf16[5,1,256,256]{3,0,1,2:T(8,128)(2,1)S(1)}, u32[]{:S(2)}, u32[]{:S(2)}) %all-to-all-start.2) | async-done | bytes 655392 | tf_op jit(solution)/shard_map/all_to_all | solution.py:84
  47.5 20.5 %all-to-all-start = ((bf16[64,8,512]{2,1,0:T(8,128)(2,1)}), bf16[64,8,512]{2,1,0:T(8,128)(2,1)S(1)}, u32[]{:S(2)}, u32[]{:S(2)}) async-start(bf16[64,8,512]{2,1,0:T(8,128)(2,1)} %bitcast.2), calls=%async_computation | async-start | bytes 1048576 | tf_op jit(solution)/shard_map/all_to_all | solution.py:58
  70.1 1.8 %multiply_reduce_fusion = (f32[32,256]{1,0:T(8,128)}, f32[3,8,32,256]{3,2,1,0:T(8,128)}) fusion(f32[8,32,256]{2,1,0:T(8,128)S(1)} %convert_element_type.215, f32[256]{0:T(256)S(1)} %copy-done.14, bf16[3,8,32,256]{3,2,1,0:T(8,128)(2,1)S(1)} %copy-done.1, bf16[256,256]{1,0:T(8,128)(2,1)S(1)} %copy-done.13), kind=kOutput, calls=%fused_computation.47 | convolution fusion | flops 101834752 | bytes 1606656 | tf_op jit(solution)/shard_map/kxzj,ij->kxzi/dot_general | solution.py:41
  73.0 27.5 %all-to-all-done = bf16[64,8,512]{2,1,0:T(8,128)(2,1)S(1)} async-done(((bf16[64,8,512]{2,1,0:T(8,128)(2,1)}), bf16[64,8,512]{2,1,0:T(8,128)(2,1)S(1)}, u32[]{:S(2)}, u32[]{:S(2)}) %all-to-all-start) | async-done | bytes 524320 | tf_op jit(solution)/shard_map/all_to_all | solution.py:58
  101.4 1.1 fusion.79
  102.6 1.4 fusion.81
  106.3 2.6 %fusion.31 = (f32[512,384]{0,1:T(8,128)S(1)}, f32[512,384]{0,1:T(8,128)S(1)}) fusion(f32[512,128]{0,1:T(8,128)S(1)} %fusion.42, bf16[512,512]{1,0:T(8,128)(2,1)S(1)} %copy-done, f32[1,384]{0,1:T(8,128)} %get-tuple-element.39, f32[511,384]{0,1:T(8,128)} %get-tuple-element.41, f32[511,384]{0,1:T(8,128)} %get-tuple-element.40, ...), kind=kOutput, calls=%fused_computation.55 | convolution fusion | flops 204472320 | bytes 5505024 | tf_op jit(solution)/shard_map/dot_general | solution.py:37
  110.7 0.8 copy-done.7
  111.7 0.9 bitcast_add_fusion
  112.8 1.0 maximum_maximum_fusion
  113.9 5.7 %all-to-all-start.3 = ((bf16[64,8,512]{2,1,0:T(8,128)(2,1)}), bf16[64,8,512]{2,1,0:T(8,128)(2,1)S(1)}, u32[]{:S(2)}, u32[]{:S(2)}) async-start(bf16[64,8,512]{2,1,0:T(8,128)(2,1)} %maximum_maximum_fusion), calls=%async_computation.3 | async-start | bytes 1048576 | tf_op jit(solution)/shard_map/all_to_all | solution.py:98
  120.5 32.1 %all-to-all-done.3 = bf16[64,8,512]{2,1,0:T(8,128)(2,1)S(1)} async-done(((bf16[64,8,512]{2,1,0:T(8,128)(2,1)}), bf16[64,8,512]{2,1,0:T(8,128)(2,1)S(1)}, u32[]{:S(2)}, u32[]{:S(2)}) %all-to-all-start.3) | async-done | bytes 524320 | tf_op jit(solution)/shard_map/all_to_all | solution.py:98
  154.1 0.9 slice_bitcast_fusion
  155.8 2.2 %fusion.6 = bf16[3,8,32,256]{3,2,1,0:T(8,128)(2,1)} fusion(f32[3,8,32,256]{3,2,1,0:T(8,128)S(1)} %reshape.150, bf16[3,8,32,256]{3,2,1,0:T(8,128)(2,1)} %bitcast.90, bf16[3,8,32,256]{3,2,1,0:T(8,128)(2,1)S(1)} %copy-done.1, f32[3,8,32,256]{3,2,1,0:T(8,128)S(1)} %copy-done.2, f32[8,32,256]{2,1,0:T(8,128)S(1)} %copy-done.8, f32[256]{0:T(256)S(1)} %copy-done.14, ...), kind=kOutput, calls=%fused_computation.8 | convolution fusion | flops 102629376 | bytes 3146752 | tf_op jit(solution)/shard_map/kxzj,ij->kxzi/dot_general | solution.py:41
  (87 shorter events, 14.8 us)
Async XLA Ops:
  0.6 105.6 %copy-start = (bf16[512,512]{1,0:T(8,128)(2,1)S(1)}, bf16[512,512]{1,0:T(8,128)(2,1)}, u32[]{:S(2)}) copy-start(bf16[512,512]{1,0:T(8,128)(2,1)} %param.11) | copy-start | bytes 1572868
  21.7 0.9 copy-start.10
  23.9 1.9 %copy-start.9 = (f32[256,256]{1,0:T(8,128)S(1)}, f32[256,256]{1,0:T(8,128)}, u32[]{:S(2)}) copy-start(f32[256,256]{1,0:T(8,128)} %get-tuple-element.23) | copy-start | bytes 786436
  25.3 0.9 copy-start.11
  25.9 1.1 copy-start.3
  30.5 3.7 %copy-start.1 = (bf16[3,8,32,256]{3,2,1,0:T(8,128)(2,1)S(1)}, bf16[3,8,32,256]{3,2,1,0:T(8,128)(2,1)}, u32[]{:S(2)}) copy-start(bf16[3,8,32,256]{3,2,1,0:T(8,128)(2,1)} %param.7) | copy-start | bytes 1179652
  30.5 3.8 %copy-start.4 = (bf16[8,32,256]{2,1,0:T(8,128)(2,1)S(1)}, bf16[8,32,256]{2,1,0:T(8,128)(2,1)}, u32[]{:S(2)}) copy-start(bf16[8,32,256]{2,1,0:T(8,128)(2,1)} %param.8) | copy-start | bytes 393220
  30.5 17.0 %all-to-all-start.2 = ((bf16[5,1,256,256]{3,0,1,2:T(8,128)(2,1)}), bf16[5,1,256,256]{3,0,1,2:T(8,128)(2,1)S(1)}, u32[]{:S(2)}, u32[]{:S(2)}) async-start(bf16[5,1,256,256]{3,0,1,2:T(8,128)(2,1)} %copy.50), calls=%async_computation.2 | async-start | bytes 2097152 | tf_op jit(solution)/shard_map/all_to_all | solution.py:84
  35.0 35.1 %copy-start.13 = (bf16[256,256]{1,0:T(8,128)(2,1)S(1)}, bf16[256,256]{1,0:T(8,128)(2,1)}, u32[]{:S(2)}) copy-start(bf16[256,256]{1,0:T(8,128)(2,1)} %param.13) | copy-start | bytes 393220
  35.0 35.1 %copy-start.14 = (f32[256]{0:T(256)S(1)}, f32[256]{0:T(256)}, u32[]{:S(2)}) copy-start(f32[256]{0:T(256)} %param.10) | copy-start | bytes 3076
  47.5 53.0 %all-to-all-start = ((bf16[64,8,512]{2,1,0:T(8,128)(2,1)}), bf16[64,8,512]{2,1,0:T(8,128)(2,1)S(1)}, u32[]{:S(2)}, u32[]{:S(2)}) async-start(bf16[64,8,512]{2,1,0:T(8,128)(2,1)} %bitcast.2), calls=%async_computation | async-start | bytes 1048576 | tf_op jit(solution)/shard_map/all_to_all | solution.py:58
  103.9 1.6 copy-start.12
  105.6 0.6 copy-start.6
  110.4 1.3 copy-start.15
  110.7 0.9 copy-start.7
  113.9 38.7 %all-to-all-start.3 = ((bf16[64,8,512]{2,1,0:T(8,128)(2,1)}), bf16[64,8,512]{2,1,0:T(8,128)(2,1)S(1)}, u32[]{:S(2)}, u32[]{:S(2)}) async-start(bf16[64,8,512]{2,1,0:T(8,128)(2,1)} %maximum_maximum_fusion), calls=%async_computation.3 | async-start | bytes 1048576 | tf_op jit(solution)/shard_map/all_to_all | solution.py:98
  152.6 0.8 copy-start.5
  153.4 2.3 %copy-start.2 = (f32[3,8,32,256]{3,2,1,0:T(8,128)S(1)}, f32[3,8,32,256]{3,2,1,0:T(8,128)}, u32[]{:S(2)}) copy-start(f32[3,8,32,256]{3,2,1,0:T(8,128)} %get-tuple-element.49) | copy-start | bytes 2359300
  153.4 2.3 %copy-start.8 = (f32[8,32,256]{2,1,0:T(8,128)S(1)}, f32[8,32,256]{2,1,0:T(8,128)}, u32[]{:S(2)}) copy-start(f32[8,32,256]{2,1,0:T(8,128)} %get-tuple-element.44) | copy-start | bytes 786436

commit v5 on v4

--- a/solution.py
+++ b/solution.py
@@ -21,6 +21,20 @@
     right_side = stencil(pencil, 1)
     product = jnp.einsum("ij,cjp->cip", operator, right_side, preferred_element_type=f32)
     return product.astype(bf16)
+
+
+def exchange(block_for, size, mine):
+    received = [block_for(mine)]
+    for shift in range(1, size):
+        pairs = [(src, (src + shift) % size) for src in range(size)]
+        received.append(lax.ppermute(block_for((mine + shift) % size), "gz", pairs))
+    return jnp.stack(received)
+
+
+def in_order(received, size, mine):
+    flipped = jnp.concatenate([received[:1], received[1:][::-1]], axis=0)
+    doubled = jnp.concatenate([flipped, flipped], axis=0)
+    return lax.dynamic_slice_in_dim(doubled, size - mine, size, 0)
 
 
 def split_wide(value):
@@ -72,8 +86,12 @@
     owned = (z_ids == z_at) & (y_ids == y_at)
     stream_part = jnp.where(owned, stream_sq[None, None], 0.0).reshape(nzl, ny)
 
+    gzn = lax.axis_size("gz")
+    mine = lax.axis_index("gz")
     zs = jnp.concatenate([adjoint, viscosity[None], strain[None]], axis=0)
-    zt = lax.all_to_all(zs, "gz", 1, 2, tiled=True)[:, 0]
+    span_in = exchange(lambda dst: lax.dynamic_index_in_dim(zs, dst, 1, False), gzn, mine)
+    zt = in_order(span_in, gzn, mine)
+    zt = zt.transpose(1, 0, 2, 3).reshape(zs.shape[0], gzn * nzl, ny)
     span_visc = zt[comps].astype(f32)
     span_strain = zt[comps + 1].astype(f32)
     span_grad = derivative(zt[:comps], span_inverse)
@@ -81,9 +99,11 @@
     span_div = derivative(span_flux, span_inverse)
     span_sq = jnp.sum(span_strain[None] * span_grad.astype(f32) ** 2, axis=0)
     span_back = jnp.concatenate([span_div, split_wide(span_sq)], axis=0)
-    span_back = lax.all_to_all(span_back[:, None], "gz", 2, 1, tiled=True)
-    span_div = span_back[:comps]
-    span_part = jnp.sum(join_wide(span_back[comps:]), axis=0)
+    span_out = exchange(
+        lambda dst: lax.dynamic_slice_in_dim(span_back, dst * nzl, nzl, 1), gzn, mine
+    )
+    span_part = jnp.sum(join_wide(span_out[:, comps:].transpose(1, 0, 2, 3)), axis=0)
+    span_div = in_order(span_out[:, :comps], gzn, mine).transpose(1, 0, 2, 3)
 
     wall_grad = wall_derivative(adjoint, wall_operator, metric).astype(bf16)
     wall_flux = (viscous[None] * wall_grad.astype(f32)).astype(bf16)

time: 159 us -> 158 us (level)
  starting transfers between devices: 29.9 us -> 87.3 us
  waiting for transfers between devices: 71.2 us -> 39.7 us
  blocking collectives: 17.9 us -> 0 us
  local copies, waits for them, and re-layouts: 20.4 us -> 16.8 us
  matrix products: 10.2 us -> 6.98 us
  other arithmetic: 7.42 us -> 4.33 us
    ppermute x0 -> x14, starting transfers between devices: none -> 50 us  [exchange(): received.append(lax.ppermute(block_for((mine + shift) % size), 'gz', pairs))]
    all_to_all x1, waiting for transfers between devices: 27.5 us -> 0.01 us  [on_device(): lax.all_to_all(xs, 'gx', 0, 0, tiled=True).reshape(nx, (comps + 1) * lanes)]
    all_to_all x1 -> x0, blocking collectives: 17.9 us -> none  [on_device(): zt = lax.all_to_all(zs, 'gz', 1, 2, tiled=True)[:, 0]]
    all_to_all x1, starting transfers between devices: 5.68 us -> 19 us  [on_device(): back = lax.all_to_all(back, 'gx', 0, 0, tiled=True)]
    all_to_all x1 -> x0, waiting for transfers between devices: 11.7 us -> none  [on_device(): span_back = lax.all_to_all(span_back[:, None], 'gz', 2, 1, tiled=True)]
    ppermute x0 -> x14, waiting for transfers between devices: none -> 7.32 us  [exchange(): received.append(lax.ppermute(block_for((mine + shift) % size), 'gz', pairs))]
    all_to_all x1 -> x0, starting transfers between devices: 3.69 us -> none  [on_device(): span_back = lax.all_to_all(span_back[:, None], 'gz', 2, 1, tiled=True)]
    all_to_all x1, starting transfers between devices: 20.5 us -> 18.3 us  [on_device(): lax.all_to_all(xs, 'gx', 0, 0, tiled=True).reshape(nx, (comps + 1) * lanes)]
  transfers between devices with their start and end apart: 3 -> 16, of which waited for: 3 -> 4; matrix products, arithmetic and copies ran while one was open for 5% -> 6% of each run, Pallas kernels for 0% -> 0%
where the time goes in v5:
time: 158 us; the launch traced here: 157 us
  starting transfers between devices  87.3 us (55%)
  waiting for transfers between devices  39.7 us (25%)
  local copies, waits for them, and re-layouts  16.8 us (11%)
  matrix products  6.98 us (4%)
  other arithmetic  4.33 us (3%)
  between operations  1.61 us (1%)
    ppermute x14, starting transfers between devices, exchange(): received.append(lax.ppermute(block_for((mine + shift) % size), 'gz', pairs))  50 us
    all_to_all x1, waiting for transfers between devices, on_device(): back = lax.all_to_all(back, 'gx', 0, 0, tiled=True)  32.4 us
    all_to_all x1, starting transfers between devices, on_device(): back = lax.all_to_all(back, 'gx', 0, 0, tiled=True)  19 us
    all_to_all x1, starting transfers between devices, on_device(): lax.all_to_all(xs, 'gx', 0, 0, tiled=True).reshape(nx, (comps + 1) * lanes)  18.3 us
    ppermute x14, waiting for transfers between devices, exchange(): received.append(lax.ppermute(block_for((mine + shift) % size), 'gz', pairs))  7.32 us
    unnamed x48, local copies, waits for them, and re-layouts  5.99 us
  transfers between devices with their start and end apart: 16, of which 4 were waited for; matrix products, arithmetic and copies ran while one was open for 6% of the time, Pallas kernels for 0%

profile of v5, /device:TPU:1, one launch (start us, length us, event | category | flops | bytes accessed | tf_op | source)
XLA Modules:
  0.0 156.7 jit_solution(5918000454658001324)
XLA Ops:
  0.7 1.2 concatenate.87
  3.4 18.3 %all-to-all-start = ((bf16[64,8,512]{2,1,0:T(8,128)(2,1)}), bf16[64,8,512]{2,1,0:T(8,128)(2,1)S(1)}, u32[]{:S(2)}, u32[]{:S(2)}) async-start(bf16[64,8,512]{2,1,0:T(8,128)(2,1)} %bitcast.2), calls=%async_computation | async-start | bytes 1048576 | tf_op jit(solution)/shard_map/all_to_all | solution.py:72
  22.7 4.5 %collective-permute-start = (bf16[5,32,256]{2,1,0:T(8,128)(2,1)S(1)}, bf16[5,32,256]{2,1,0:T(8,128)(2,1)S(1)}, u32[]{:S(2)}, u32[]{:S(2)}) collective-permute-start(bf16[5,32,256]{2,1,0:T(8,128)(2,1)S(1)} %get-tuple-element.55), channel_id=1, source_target_pairs={{0,1},{1,2},{2,3},{3,4},{4,5},{5,6},{6,7},{7,0},{8,9},{9,10},{10,1... | collective-permute-start | bytes 245768 | tf_op jit(solution)/shard_map/ppermute | solution.py:30
  27.2 3.1 %collective-permute-start.1 = (bf16[5,32,256]{2,1,0:T(8,128)(2,1)S(1)}, bf16[5,32,256]{2,1,0:T(8,128)(2,1)}, u32[]{:S(2)}, u32[]{:S(2)}) collective-permute-start(bf16[5,32,256]{2,1,0:T(8,128)(2,1)S(1)} %get-tuple-element.54), channel_id=1, source_target_pairs={{0,2},{1,3},{2,4},{3,5},{4,6},{5,7},{6,0},{7,1},{8,10},{9,11},{10,... | collective-permute-start | bytes 245768 | tf_op jit(solution)/shard_map/ppermute | solution.py:30
  30.4 3.8 %collective-permute-start.2 = (bf16[5,32,256]{2,1,0:T(8,128)(2,1)S(1)}, bf16[5,32,256]{2,1,0:T(8,128)(2,1)S(1)}, u32[]{:S(2)}, u32[]{:S(2)}) collective-permute-start(bf16[5,32,256]{2,1,0:T(8,128)(2,1)S(1)} %get-tuple-element.53), channel_id=1, source_target_pairs={{0,3},{1,4},{2,5},{3,6},{4,7},{5,0},{6,1},{7,2},{8,11},{9,12},{10,... | collective-permute-start | bytes 245768 | tf_op jit(solution)/shard_map/ppermute | solution.py:30
  34.2 3.6 %collective-permute-start.3 = (bf16[5,32,256]{2,1,0:T(8,128)(2,1)S(1)}, bf16[5,32,256]{2,1,0:T(8,128)(2,1)S(1)}, u32[]{:S(2)}, u32[]{:S(2)}) collective-permute-start(bf16[5,32,256]{2,1,0:T(8,128)(2,1)S(1)} %get-tuple-element.52), channel_id=1, source_target_pairs={{0,4},{1,5},{2,6},{3,7},{4,0},{5,1},{6,2},{7,3},{8,12},{9,13},{10,... | collective-permute-start | bytes 245768 | tf_op jit(solution)/shard_map/ppermute | solution.py:30
  37.8 6.1 %collective-permute-start.4 = (bf16[5,32,256]{2,1,0:T(8,128)(2,1)S(1)}, bf16[5,32,256]{2,1,0:T(8,128)(2,1)S(1)}, u32[]{:S(2)}, u32[]{:S(2)}) collective-permute-start(bf16[5,32,256]{2,1,0:T(8,128)(2,1)S(1)} %get-tuple-element.51), channel_id=1, source_target_pairs={{0,5},{1,6},{2,7},{3,0},{4,1},{5,2},{6,3},{7,4},{8,13},{9,14},{10,... | collective-permute-start | bytes 245768 | tf_op jit(solution)/shard_map/ppermute | solution.py:30
  45.8 1.2 multiply_reduce_fusion
  48.3 3.0 %collective-permute-start.5 = (bf16[5,32,256]{2,1,0:T(8,128)(2,1)S(1)}, bf16[5,32,256]{2,1,0:T(8,128)(2,1)S(1)}, u32[]{:S(2)}, u32[]{:S(2)}) collective-permute-start(bf16[5,32,256]{2,1,0:T(8,128)(2,1)S(1)} %get-tuple-element.50), channel_id=1, source_target_pairs={{0,6},{1,7},{2,0},{3,1},{4,2},{5,3},{6,4},{7,5},{8,14},{9,15},{10,... | collective-permute-start | bytes 245768 | tf_op jit(solution)/shard_map/ppermute | solution.py:30
  52.2 1.9 %collective-permute-start.6 = (bf16[5,32,256]{2,1,0:T(8,128)(2,1)S(1)}, bf16[5,32,256]{2,1,0:T(8,128)(2,1)S(1)}, u32[]{:S(2)}, u32[]{:S(2)}) collective-permute-start(bf16[5,32,256]{2,1,0:T(8,128)(2,1)S(1)} %get-tuple-element.49), channel_id=1, source_target_pairs={{0,7},{1,0},{2,1},{3,2},{4,3},{5,4},{6,5},{7,6},{8,15},{9,8},{10,9... | collective-permute-start | bytes 245768 | tf_op jit(solution)/shard_map/ppermute | solution.py:30
  55.1 3.8 %collective-permute-done.6 = bf16[5,32,256]{2,1,0:T(8,128)(2,1)S(1)} collective-permute-done((bf16[5,32,256]{2,1,0:T(8,128)(2,1)S(1)}, bf16[5,32,256]{2,1,0:T(8,128)(2,1)S(1)}, u32[]{:S(2)}, u32[]{:S(2)}) %collective-permute-start.6) | collective-permute-done | bytes 81952 | tf_op jit(solution)/shard_map/ppermute | solution.py:30
  62.1 2.3 %collective-permute-start.7 = (bf16[5,32,256]{2,1,0:T(8,128)(2,1)S(1)}, bf16[5,32,256]{2,1,0:T(8,128)(2,1)S(1)}, u32[]{:S(2)}, u32[]{:S(2)}) collective-permute-start(bf16[5,32,256]{2,1,0:T(8,128)(2,1)S(1)} %get-tuple-element.46), channel_id=1, source_target_pairs={{0,1},{1,2},{2,3},{3,4},{4,5},{5,6},{6,7},{7,0},{8,9},{9,10},{10,1... | collective-permute-start | bytes 245768 | tf_op jit(solution)/shard_map/ppermute | solution.py:30
  64.4 2.1 %collective-permute-start.8 = (bf16[5,32,256]{2,1,0:T(8,128)(2,1)S(1)}, bf16[5,32,256]{2,1,0:T(8,128)(2,1)S(1)}, u32[]{:S(2)}, u32[]{:S(2)}) collective-permute-start(bf16[5,32,256]{2,1,0:T(8,128)(2,1)S(1)} %get-tuple-element.45), channel_id=1, source_target_pairs={{0,2},{1,3},{2,4},{3,5},{4,6},{5,7},{6,0},{7,1},{8,10},{9,11},{10,... | collective-permute-start | bytes 245768 | tf_op jit(solution)/shard_map/ppermute | solution.py:30
  66.5 4.6 %collective-permute-start.9 = (bf16[5,32,256]{2,1,0:T(8,128)(2,1)S(1)}, bf16[5,32,256]{2,1,0:T(8,128)(2,1)S(1)}, u32[]{:S(2)}, u32[]{:S(2)}) collective-permute-start(bf16[5,32,256]{2,1,0:T(8,128)(2,1)S(1)} %get-tuple-element.44), channel_id=1, source_target_pairs={{0,3},{1,4},{2,5},{3,6},{4,7},{5,0},{6,1},{7,2},{8,11},{9,12},{10,... | collective-permute-start | bytes 245768 | tf_op jit(solution)/shard_map/ppermute | solution.py:30
  71.1 5.2 %collective-permute-start.10 = (bf16[5,32,256]{2,1,0:T(8,128)(2,1)S(1)}, bf16[5,32,256]{2,1,0:T(8,128)(2,1)S(1)}, u32[]{:S(2)}, u32[]{:S(2)}) collective-permute-start(bf16[5,32,256]{2,1,0:T(8,128)(2,1)S(1)} %get-tuple-element.43), channel_id=1, source_target_pairs={{0,4},{1,5},{2,6},{3,7},{4,0},{5,1},{6,2},{7,3},{8,12},{9,13},{10,... | collective-permute-start | bytes 245768 | tf_op jit(solution)/shard_map/ppermute | solution.py:30
  76.4 4.7 %collective-permute-start.11 = (bf16[5,32,256]{2,1,0:T(8,128)(2,1)S(1)}, bf16[5,32,256]{2,1,0:T(8,128)(2,1)S(1)}, u32[]{:S(2)}, u32[]{:S(2)}) collective-permute-start(bf16[5,32,256]{2,1,0:T(8,128)(2,1)S(1)} %get-tuple-element.42), channel_id=1, source_target_pairs={{0,5},{1,6},{2,7},{3,0},{4,1},{5,2},{6,3},{7,4},{8,13},{9,14},{10,... | collective-permute-start | bytes 245768 | tf_op jit(solution)/shard_map/ppermute | solution.py:30
  81.1 1.9 %collective-permute-start.12 = (bf16[5,32,256]{2,1,0:T(8,128)(2,1)S(1)}, bf16[5,32,256]{2,1,0:T(8,128)(2,1)S(1)}, u32[]{:S(2)}, u32[]{:S(2)}) collective-permute-start(bf16[5,32,256]{2,1,0:T(8,128)(2,1)S(1)} %get-tuple-element.41), channel_id=1, source_target_pairs={{0,6},{1,7},{2,0},{3,1},{4,2},{5,3},{6,4},{7,5},{8,14},{9,15},{10,... | collective-permute-start | bytes 245768 | tf_op jit(solution)/shard_map/ppermute | solution.py:30
  83.0 3.0 %collective-permute-start.13 = (bf16[5,32,256]{2,1,0:T(8,128)(2,1)S(1)}, bf16[5,32,256]{2,1,0:T(8,128)(2,1)S(1)}, u32[]{:S(2)}, u32[]{:S(2)}) collective-permute-start(bf16[5,32,256]{2,1,0:T(8,128)(2,1)S(1)} %get-tuple-element.40), channel_id=1, source_target_pairs={{0,7},{1,0},{2,1},{3,2},{4,3},{5,4},{6,5},{7,6},{8,15},{9,8},{10,9... | collective-permute-start | bytes 245768 | tf_op jit(solution)/shard_map/ppermute | solution.py:30
  86.6 3.1 %collective-permute-done.13 = bf16[5,32,256]{2,1,0:T(8,128)(2,1)S(1)} collective-permute-done((bf16[5,32,256]{2,1,0:T(8,128)(2,1)S(1)}, bf16[5,32,256]{2,1,0:T(8,128)(2,1)S(1)}, u32[]{:S(2)}, u32[]{:S(2)}) %collective-permute-start.13) | collective-permute-done | bytes 81952 | tf_op jit(solution)/shard_map/ppermute | solution.py:30
  91.1 1.4 fusion.88
  94.3 2.3 %fusion.35 = (f32[512,384]{0,1:T(8,128)S(1)}, f32[512,384]{0,1:T(8,128)S(1)}) fusion(f32[512,128]{0,1:T(8,128)S(1)} %fusion.50, bf16[512,512]{1,0:T(8,128)(2,1)S(1)} %copy-done, f32[1,384]{0,1:T(8,128)} %get-tuple-element.62, f32[511,384]{0,1:T(8,128)} %get-tuple-element.64, f32[511,384]{0,1:T(8,128)} %get-tuple-element.63, ...), kind=kOutput, calls=%fused_computation.67 | convolution fusion | flops 204472320 | bytes 5505024 | tf_op jit(solution)/shard_map/dot_general | solution.py:51
  100.6 19.0 %all-to-all-start.1 = ((bf16[64,8,512]{2,1,0:T(8,128)(2,1)}), bf16[64,8,512]{2,1,0:T(8,128)(2,1)S(1)}, u32[]{:S(2)}, u32[]{:S(2)}) async-start(bf16[64,8,512]{2,1,0:T(8,128)(2,1)} %maximum_maximum_fusion), calls=%async_computation.1 | async-start | bytes 1048576 | tf_op jit(solution)/shard_map/all_to_all | solution.py:118
  119.6 32.4 %all-to-all-done.1 = bf16[64,8,512]{2,1,0:T(8,128)(2,1)S(1)} async-done(((bf16[64,8,512]{2,1,0:T(8,128)(2,1)}), bf16[64,8,512]{2,1,0:T(8,128)(2,1)S(1)}, u32[]{:S(2)}, u32[]{:S(2)}) %all-to-all-start.1) | async-done | bytes 524320 | tf_op jit(solution)/shard_map/all_to_all | solution.py:118
  153.5 1.7 %fusion.6 = bf16[3,8,32,256]{3,2,0,1:T(8,128)(2,1)S(1)} fusion(f32[3,8,32,256]{3,2,0,1:T(8,128)S(1)} %reshape.131, f32[3,8,32,256]{3,2,0,1:T(8,128)} %get-tuple-element.86, s32[]{:T(128)S(6)} %select_n.138, bf16[1,3,32,256]{3,2,1,0:T(8,128)(2,1)S(1)} %slice.249, bf16[7,3,32,256]{3,2,1,0:T(8,128)(2,1)S(1)} %rev.7, f32[8,32,256]{2,1,0:T(8,128)} %get-tuple-element.67, ...), kind=kOutput, calls=%fused_computation.12 | convolution fusion | flops 103219200 | bytes 3146756 | tf_op jit(solution)/shard_map/kxzj,ij->kxzi/dot_general | solution.py:55
  (130 shorter events, 20.8 us)
Async XLA Ops:
  0.6 93.7 %copy-start = (bf16[512,512]{1,0:T(8,128)(2,1)S(1)}, bf16[512,512]{1,0:T(8,128)(2,1)}, u32[]{:S(2)}) copy-start(bf16[512,512]{1,0:T(8,128)(2,1)} %param.11) | copy-start | bytes 1572868
  0.6 1.7 %copy-start.2 = (bf16[8,32,256]{2,1,0:T(8,128)(2,1)S(1)}, bf16[8,32,256]{2,1,0:T(8,128)(2,1)}, u32[]{:S(2)}) copy-start(bf16[8,32,256]{2,1,0:T(8,128)(2,1)} %param.8) | copy-start | bytes 393220
  3.4 18.4 %copy-start.9 = (f32[32,256]{1,0:T(8,128)S(1)}, f32[32,256]{1,0:T(8,128)}, u32[]{:S(2)}) copy-start(f32[32,256]{1,0:T(8,128)} %param.9) | copy-start | bytes 98308
  3.4 19.1 %copy-start.1 = (bf16[3,8,32,256]{3,2,1,0:T(8,128)(2,1)S(1)}, bf16[3,8,32,256]{3,2,1,0:T(8,128)(2,1)}, u32[]{:S(2)}) copy-start(bf16[3,8,32,256]{3,2,1,0:T(8,128)(2,1)} %param.7) | copy-start | bytes 1179652
  3.4 87.2 %all-to-all-start = ((bf16[64,8,512]{2,1,0:T(8,128)(2,1)}), bf16[64,8,512]{2,1,0:T(8,128)(2,1)S(1)}, u32[]{:S(2)}, u32[]{:S(2)}) async-start(bf16[64,8,512]{2,1,0:T(8,128)(2,1)} %bitcast.2), calls=%async_computation | async-start | bytes 1048576 | tf_op jit(solution)/shard_map/all_to_all | solution.py:72
  22.6 23.2 %copy-start.6 = (bf16[256,256]{1,0:T(8,128)(2,1)S(1)}, bf16[256,256]{1,0:T(8,128)(2,1)}, u32[]{:S(2)}) copy-start(bf16[256,256]{1,0:T(8,128)(2,1)} %param.13) | copy-start | bytes 393220
  22.6 23.2 %copy-start.12 = (f32[256]{0:T(256)S(1)}, f32[256]{0:T(256)}, u32[]{:S(2)}) copy-start(f32[256]{0:T(256)} %param.10) | copy-start | bytes 3076
  22.7 24.9 %collective-permute-start = (bf16[5,32,256]{2,1,0:T(8,128)(2,1)S(1)}, bf16[5,32,256]{2,1,0:T(8,128)(2,1)S(1)}, u32[]{:S(2)}, u32[]{:S(2)}) collective-permute-start(bf16[5,32,256]{2,1,0:T(8,128)(2,1)S(1)} %get-tuple-element.55), channel_id=1, source_target_pairs={{0,1},{1,2},{2,3},{3,4},{4,5},{5,6},{6,7},{7,0},{8,9},{9,10},{10,1... | collective-permute-start | bytes 245768 | tf_op jit(solution)/shard_map/ppermute | solution.py:30
  27.2 25.0 %collective-permute-start.1 = (bf16[5,32,256]{2,1,0:T(8,128)(2,1)S(1)}, bf16[5,32,256]{2,1,0:T(8,128)(2,1)}, u32[]{:S(2)}, u32[]{:S(2)}) collective-permute-start(bf16[5,32,256]{2,1,0:T(8,128)(2,1)S(1)} %get-tuple-element.54), channel_id=1, source_target_pairs={{0,2},{1,3},{2,4},{3,5},{4,6},{5,7},{6,0},{7,1},{8,10},{9,11},{10,... | collective-permute-start | bytes 245768 | tf_op jit(solution)/shard_map/ppermute | solution.py:30
  30.4 24.7 %collective-permute-start.2 = (bf16[5,32,256]{2,1,0:T(8,128)(2,1)S(1)}, bf16[5,32,256]{2,1,0:T(8,128)(2,1)S(1)}, u32[]{:S(2)}, u32[]{:S(2)}) collective-permute-start(bf16[5,32,256]{2,1,0:T(8,128)(2,1)S(1)} %get-tuple-element.53), channel_id=1, source_target_pairs={{0,3},{1,4},{2,5},{3,6},{4,7},{5,0},{6,1},{7,2},{8,11},{9,12},{10,... | collective-permute-start | bytes 245768 | tf_op jit(solution)/shard_map/ppermute | solution.py:30
  34.2 20.9 %collective-permute-start.3 = (bf16[5,32,256]{2,1,0:T(8,128)(2,1)S(1)}, bf16[5,32,256]{2,1,0:T(8,128)(2,1)S(1)}, u32[]{:S(2)}, u32[]{:S(2)}) collective-permute-start(bf16[5,32,256]{2,1,0:T(8,128)(2,1)S(1)} %get-tuple-element.52), channel_id=1, source_target_pairs={{0,4},{1,5},{2,6},{3,7},{4,0},{5,1},{6,2},{7,3},{8,12},{9,13},{10,... | collective-permute-start | bytes 245768 | tf_op jit(solution)/shard_map/ppermute | solution.py:30
  37.8 17.3 %collective-permute-start.4 = (bf16[5,32,256]{2,1,0:T(8,128)(2,1)S(1)}, bf16[5,32,256]{2,1,0:T(8,128)(2,1)S(1)}, u32[]{:S(2)}, u32[]{:S(2)}) collective-permute-start(bf16[5,32,256]{2,1,0:T(8,128)(2,1)S(1)} %get-tuple-element.51), channel_id=1, source_target_pairs={{0,5},{1,6},{2,7},{3,0},{4,1},{5,2},{6,3},{7,4},{8,13},{9,14},{10,... | collective-permute-start | bytes 245768 | tf_op jit(solution)/shard_map/ppermute | solution.py:30
  48.3 6.9 %collective-permute-start.5 = (bf16[5,32,256]{2,1,0:T(8,128)(2,1)S(1)}, bf16[5,32,256]{2,1,0:T(8,128)(2,1)S(1)}, u32[]{:S(2)}, u32[]{:S(2)}) collective-permute-start(bf16[5,32,256]{2,1,0:T(8,128)(2,1)S(1)} %get-tuple-element.50), channel_id=1, source_target_pairs={{0,6},{1,7},{2,0},{3,1},{4,2},{5,3},{6,4},{7,5},{8,14},{9,15},{10,... | collective-permute-start | bytes 245768 | tf_op jit(solution)/shard_map/ppermute | solution.py:30
  52.2 6.7 %collective-permute-start.6 = (bf16[5,32,256]{2,1,0:T(8,128)(2,1)S(1)}, bf16[5,32,256]{2,1,0:T(8,128)(2,1)S(1)}, u32[]{:S(2)}, u32[]{:S(2)}) collective-permute-start(bf16[5,32,256]{2,1,0:T(8,128)(2,1)S(1)} %get-tuple-element.49), channel_id=1, source_target_pairs={{0,7},{1,0},{2,1},{3,2},{4,3},{5,4},{6,5},{7,6},{8,15},{9,8},{10,9... | collective-permute-start | bytes 245768 | tf_op jit(solution)/shard_map/ppermute | solution.py:30
  62.1 18.9 %collective-permute-start.7 = (bf16[5,32,256]{2,1,0:T(8,128)(2,1)S(1)}, bf16[5,32,256]{2,1,0:T(8,128)(2,1)S(1)}, u32[]{:S(2)}, u32[]{:S(2)}) collective-permute-start(bf16[5,32,256]{2,1,0:T(8,128)(2,1)S(1)} %get-tuple-element.46), channel_id=1, source_target_pairs={{0,1},{1,2},{2,3},{3,4},{4,5},{5,6},{6,7},{7,0},{8,9},{9,10},{10,1... | collective-permute-start | bytes 245768 | tf_op jit(solution)/shard_map/ppermute | solution.py:30
  64.4 18.6 %collective-permute-start.8 = (bf16[5,32,256]{2,1,0:T(8,128)(2,1)S(1)}, bf16[5,32,256]{2,1,0:T(8,128)(2,1)S(1)}, u32[]{:S(2)}, u32[]{:S(2)}) collective-permute-start(bf16[5,32,256]{2,1,0:T(8,128)(2,1)S(1)} %get-tuple-element.45), channel_id=1, source_target_pairs={{0,2},{1,3},{2,4},{3,5},{4,6},{5,7},{6,0},{7,1},{8,10},{9,11},{10,... | collective-permute-start | bytes 245768 | tf_op jit(solution)/shard_map/ppermute | solution.py:30
  66.5 19.6 %collective-permute-start.9 = (bf16[5,32,256]{2,1,0:T(8,128)(2,1)S(1)}, bf16[5,32,256]{2,1,0:T(8,128)(2,1)S(1)}, u32[]{:S(2)}, u32[]{:S(2)}) collective-permute-start(bf16[5,32,256]{2,1,0:T(8,128)(2,1)S(1)} %get-tuple-element.44), channel_id=1, source_target_pairs={{0,3},{1,4},{2,5},{3,6},{4,7},{5,0},{6,1},{7,2},{8,11},{9,12},{10,... | collective-permute-start | bytes 245768 | tf_op jit(solution)/shard_map/ppermute | solution.py:30
  71.1 15.0 %collective-permute-start.10 = (bf16[5,32,256]{2,1,0:T(8,128)(2,1)S(1)}, bf16[5,32,256]{2,1,0:T(8,128)(2,1)S(1)}, u32[]{:S(2)}, u32[]{:S(2)}) collective-permute-start(bf16[5,32,256]{2,1,0:T(8,128)(2,1)S(1)} %get-tuple-element.43), channel_id=1, source_target_pairs={{0,4},{1,5},{2,6},{3,7},{4,0},{5,1},{6,2},{7,3},{8,12},{9,13},{10,... | collective-permute-start | bytes 245768 | tf_op jit(solution)/shard_map/ppermute | solution.py:30
  76.4 9.8 %collective-permute-start.11 = (bf16[5,32,256]{2,1,0:T(8,128)(2,1)S(1)}, bf16[5,32,256]{2,1,0:T(8,128)(2,1)S(1)}, u32[]{:S(2)}, u32[]{:S(2)}) collective-permute-start(bf16[5,32,256]{2,1,0:T(8,128)(2,1)S(1)} %get-tuple-element.42), channel_id=1, source_target_pairs={{0,5},{1,6},{2,7},{3,0},{4,1},{5,2},{6,3},{7,4},{8,13},{9,14},{10,... | collective-permute-start | bytes 245768 | tf_op jit(solution)/shard_map/ppermute | solution.py:30
  81.1 5.5 %collective-permute-start.12 = (bf16[5,32,256]{2,1,0:T(8,128)(2,1)S(1)}, bf16[5,32,256]{2,1,0:T(8,128)(2,1)S(1)}, u32[]{:S(2)}, u32[]{:S(2)}) collective-permute-start(bf16[5,32,256]{2,1,0:T(8,128)(2,1)S(1)} %get-tuple-element.41), channel_id=1, source_target_pairs={{0,6},{1,7},{2,0},{3,1},{4,2},{5,3},{6,4},{7,5},{8,14},{9,15},{10,... | collective-permute-start | bytes 245768 | tf_op jit(solution)/shard_map/ppermute | solution.py:30
  83.0 6.7 %collective-permute-start.13 = (bf16[5,32,256]{2,1,0:T(8,128)(2,1)S(1)}, bf16[5,32,256]{2,1,0:T(8,128)(2,1)S(1)}, u32[]{:S(2)}, u32[]{:S(2)}) collective-permute-start(bf16[5,32,256]{2,1,0:T(8,128)(2,1)S(1)} %get-tuple-element.40), channel_id=1, source_target_pairs={{0,7},{1,0},{2,1},{3,2},{4,3},{5,4},{6,5},{7,6},{8,15},{9,8},{10,9... | collective-permute-start | bytes 245768 | tf_op jit(solution)/shard_map/ppermute | solution.py:30
  92.5 1.7 %copy-start.11 = (f32[128]{0:T(128)S(1)}, f32[128]{0:T(128)}, u32[]{:S(2)}) copy-start(f32[128]{0:T(128)} %dynamic-slice_bitcast_fusion.9) | copy-start | bytes 1540
  100.6 19.0 %copy-start.5 = (bf16[7,5,32,256]{3,2,1,0:T(8,128)(2,1)S(1)}, bf16[7,5,32,256]{3,2,1,0:T(8,128)(2,1)}, u32[]{:S(2)}) copy-start(bf16[7,5,32,256]{3,2,1,0:T(8,128)(2,1)} %copy-done.4) | copy-start | bytes 1720324
  100.6 51.5 %all-to-all-start.1 = ((bf16[64,8,512]{2,1,0:T(8,128)(2,1)}), bf16[64,8,512]{2,1,0:T(8,128)(2,1)S(1)}, u32[]{:S(2)}, u32[]{:S(2)}) async-start(bf16[64,8,512]{2,1,0:T(8,128)(2,1)} %maximum_maximum_fusion), calls=%async_computation.1 | async-start | bytes 1048576 | tf_op jit(solution)/shard_map/all_to_all | solution.py:118
  (8 other events, 6.5 us)

commit v6 on v4

--- a/solution.py
+++ b/solution.py
@@ -21,6 +21,29 @@
     right_side = stencil(pencil, 1)
     product = jnp.einsum("ij,cjp->cip", operator, right_side, preferred_element_type=f32)
     return product.astype(bf16)
+
+
+def xor_order(blocks, mine):
+    size = blocks.shape[0]
+    bit = 1
+    while bit < size:
+        swapped = blocks.reshape(size // (2 * bit), 2, bit, *blocks.shape[1:])[:, ::-1]
+        blocks = jnp.where((mine // bit) % 2 == 1, swapped.reshape(blocks.shape), blocks)
+        bit *= 2
+    return blocks
+
+
+def butterfly(blocks, mine):
+    size = blocks.shape[0]
+    blocks = xor_order(blocks, mine)
+    bit = 1
+    while bit < size:
+        split = blocks.reshape(size // (2 * bit), 2, bit, *blocks.shape[1:])
+        pairs = [(src, src ^ bit) for src in range(size)]
+        moved = lax.ppermute(split[:, 1], "gz", pairs)
+        blocks = jnp.stack([split[:, 0], moved], axis=1).reshape(blocks.shape)
+        bit *= 2
+    return xor_order(blocks, mine)
 
 
 def split_wide(value):
@@ -72,8 +95,11 @@
     owned = (z_ids == z_at) & (y_ids == y_at)
     stream_part = jnp.where(owned, stream_sq[None, None], 0.0).reshape(nzl, ny)
 
+    gzn = lax.axis_size("gz")
+    mine = lax.axis_index("gz")
     zs = jnp.concatenate([adjoint, viscosity[None], strain[None]], axis=0)
-    zt = lax.all_to_all(zs, "gz", 1, 2, tiled=True)[:, 0]
+    zt = butterfly(zs.transpose(1, 0, 2, 3), mine)
+    zt = zt.transpose(1, 0, 2, 3).reshape(zs.shape[0], gzn * nzl, ny)
     span_visc = zt[comps].astype(f32)
     span_strain = zt[comps + 1].astype(f32)
     span_grad = derivative(zt[:comps], span_inverse)
@@ -81,9 +107,10 @@
     span_div = derivative(span_flux, span_inverse)
     span_sq = jnp.sum(span_strain[None] * span_grad.astype(f32) ** 2, axis=0)
     span_back = jnp.concatenate([span_div, split_wide(span_sq)], axis=0)
-    span_back = lax.all_to_all(span_back[:, None], "gz", 2, 1, tiled=True)
-    span_div = span_back[:comps]
-    span_part = jnp.sum(join_wide(span_back[comps:]), axis=0)
+    span_back = span_back.reshape(span_back.shape[0], gzn, nzl, ny).transpose(1, 0, 2, 3)
+    span_out = butterfly(span_back, mine)
+    span_part = jnp.sum(join_wide(span_out[:, comps:].transpose(1, 0, 2, 3)), axis=0)
+    span_div = span_out[:, :comps].transpose(1, 0, 2, 3)
 
     wall_grad = wall_derivative(adjoint, wall_operator, metric).astype(bf16)
     wall_flux = (viscous[None] * wall_grad.astype(f32)).astype(bf16)

time: 159 us -> 171 us (1.075)
  waiting for transfers between devices: 71.2 us -> 26.8 us
  blocking collectives: 17.9 us -> 45.6 us
  starting transfers between devices: 29.9 us -> 52.3 us
  local copies, waits for them, and re-layouts: 20.4 us -> 23.8 us
  other arithmetic: 7.42 us -> 10.6 us
  matrix products: 10.2 us -> 7.89 us
    all_to_all x2 -> x0, waiting for transfers between devices: 43.7 us -> none  [the longest x1 32.1 us: on_device(): back = lax.all_to_all(back, 'gx', 0, 0, tiled=True)]
    ppermute x0 -> x6, starting transfers between devices: none -> 32.6 us  [butterfly(): moved = lax.ppermute(split[:, 1], 'gz', pairs)]
    all_to_all x1, blocking collectives: 17.9 us -> 45.6 us  [on_device(): back = lax.all_to_all(back, 'gx', 0, 0, tiled=True)]
    all_to_all x1, waiting for transfers between devices: 27.5 us -> 1.85 us  [on_device(): lax.all_to_all(xs, 'gx', 0, 0, tiled=True).reshape(nx, (comps + 1) * lanes)]
    ppermute x0 -> x6, waiting for transfers between devices: none -> 25 us  [butterfly(): moved = lax.ppermute(split[:, 1], 'gz', pairs)]
    all_to_all x2 -> x0, starting transfers between devices: 9.37 us -> none  [the longest x1 5.68 us: on_device(): back = lax.all_to_all(back, 'gx', 0, 0, tiled=True)]
    rev x0 -> x12, local copies, waits for them, and re-layouts: none -> 6.58 us  [xor_order(): blocks.reshape(size // (2 * bit), 2, bit, *blocks.shape[1:])[:, ::-1]]
    select_n x0 -> x11, other arithmetic: none -> 5.37 us  [xor_order(): jnp.where(mine // bit % 2 == 1, swapped.reshape(blocks.shape), blocks)]
  transfers between devices with their start and end apart: 3 -> 7, of which waited for: 3 -> 6; matrix products, arithmetic and copies ran while one was open for 5% -> 6% of each run, Pallas kernels for 0% -> 0%
where the time goes in v6:
time: 171 us; the launch traced here: 168 us
  starting transfers between devices  52.3 us (31%)
  blocking collectives  45.6 us (27%)
  waiting for transfers between devices  26.8 us (16%)
  local copies, waits for them, and re-layouts  23.8 us (14%)
  other arithmetic  10.6 us (6%)
  matrix products  7.89 us (5%)
    all_to_all x1, blocking collectives, on_device(): back = lax.all_to_all(back, 'gx', 0, 0, tiled=True)  45.6 us
    ppermute x6, starting transfers between devices, butterfly(): moved = lax.ppermute(split[:, 1], 'gz', pairs)  32.6 us
    ppermute x6, waiting for transfers between devices, butterfly(): moved = lax.ppermute(split[:, 1], 'gz', pairs)  25 us
    all_to_all x1, starting transfers between devices, on_device(): lax.all_to_all(xs, 'gx', 0, 0, tiled=True).reshape(nx, (comps + 1) * lanes)  19.7 us
    rev x12, local copies, waits for them, and re-layouts, xor_order(): blocks.reshape(size // (2 * bit), 2, bit, *blocks.shape[1:])[:, ::-1]  6.58 us
    unnamed x44, local copies, waits for them, and re-layouts  5.79 us
    select_n x11, other arithmetic, xor_order(): jnp.where(mine // bit % 2 == 1, swapped.reshape(blocks.shape), blocks)  5.37 us
    dot_general x2, matrix products, wall_derivative(): jnp.einsum('kxzj,ij->kxzi', source, wall_operator, preferred_element_type...  3.97 us
  transfers between devices with their start and end apart: 7, of which 6 were waited for; matrix products, arithmetic and copies ran while one was open for 6% of the time, Pallas kernels for 0%

profile of v6, /device:TPU:1, one launch (start us, length us, event | category | flops | bytes accessed | tf_op | source)
XLA Modules:
  0.0 168.5 jit_solution(957778309546886761)
XLA Ops:
  1.5 1.7 %fusion.48 = (f32[8,32,256]{2,1,0:T(8,128)}, bf16[1,8,32,256]{3,2,1,0:T(8,128)(2,1)S(1)}) fusion(bf16[8,32,256]{2,1,0:T(8,128)(2,1)} %param.8, f32[32,256]{1,0:T(8,128)S(1)} %copy-done.15), kind=kLoop, calls=%fused_computation.108 | loop fusion | flops 262144 | bytes 557056 | tf_op jit(solution)/shard_map/convert_element_type | solution.py:76
  3.8 5.6 %collective-permute-start = (bf16[4,1,5,32,256]{4,3,0,2,1:T(8,128)(2,1)S(1)}, bf16[4,1,5,32,256]{4,3,0,2,1:T(8,128)(2,1)S(1)}, u32[]{:S(2)}, u32[]{:S(2)}) collective-permute-start(bf16[4,1,5,32,256]{4,3,0,2,1:T(8,128)(2,1)S(1)} %get-tuple-element.45), channel_id=1, source_target_pairs={{0,1},{1,0},{2,3},{3,2},{4,5},{5,4},{6,7},{7,6},{8,9},{9,8},{10,11... | collective-permute-start | bytes 983048 | tf_op jit(solution)/shard_map/ppermute | solution.py:43
  9.4 4.4 %collective-permute-done = bf16[4,1,5,32,256]{4,3,0,2,1:T(8,128)(2,1)S(1)} collective-permute-done((bf16[4,1,5,32,256]{4,3,0,2,1:T(8,128)(2,1)S(1)}, bf16[4,1,5,32,256]{4,3,0,2,1:T(8,128)(2,1)S(1)}, u32[]{:S(2)}, u32[]{:S(2)}) %collective-permute-start) | collective-permute-done | bytes 327712 | tf_op jit(solution)/shard_map/ppermute | solution.py:43
  13.9 5.8 %collective-permute-start.1 = (bf16[2,2,5,32,256]{4,3,1,2,0:T(8,128)(2,1)S(1)}, bf16[2,2,5,32,256]{4,3,1,2,0:T(8,128)(2,1)S(1)}, u32[]{:S(2)}, u32[]{:S(2)}) collective-permute-start(bf16[2,2,5,32,256]{4,3,1,2,0:T(8,128)(2,1)S(1)} %bitcast.221), channel_id=1, source_target_pairs={{0,2},{1,3},{2,0},{3,1},{4,6},{5,7},{6,4},{7,5},{8,10},{9,11},{10,... | collective-permute-start | bytes 983048 | tf_op jit(solution)/shard_map/ppermute | solution.py:43
  19.8 4.4 %collective-permute-done.1 = bf16[2,2,5,32,256]{4,3,1,2,0:T(8,128)(2,1)S(1)} collective-permute-done((bf16[2,2,5,32,256]{4,3,1,2,0:T(8,128)(2,1)S(1)}, bf16[2,2,5,32,256]{4,3,1,2,0:T(8,128)(2,1)S(1)}, u32[]{:S(2)}, u32[]{:S(2)}) %collective-permute-start.1) | collective-permute-done | bytes 327712 | tf_op jit(solution)/shard_map/ppermute | solution.py:43
  24.4 6.7 %collective-permute-start.2 = (bf16[1,4,5,32,256]{4,3,1,2,0:T(8,128)(2,1)S(1)}, bf16[1,4,5,32,256]{4,3,1,2,0:T(8,128)(2,1)S(1)}, u32[]{:S(2)}, u32[]{:S(2)}) collective-permute-start(bf16[1,4,5,32,256]{4,3,1,2,0:T(8,128)(2,1)S(1)} %get-tuple-element.41), channel_id=1, source_target_pairs={{0,4},{1,5},{2,6},{3,7},{4,0},{5,1},{6,2},{7,3},{8,12},{9,13},{10,... | collective-permute-start | bytes 983048 | tf_op jit(solution)/shard_map/ppermute | solution.py:43
  31.1 4.7 %collective-permute-done.2 = bf16[1,4,5,32,256]{4,3,1,2,0:T(8,128)(2,1)S(1)} collective-permute-done((bf16[1,4,5,32,256]{4,3,1,2,0:T(8,128)(2,1)S(1)}, bf16[1,4,5,32,256]{4,3,1,2,0:T(8,128)(2,1)S(1)}, u32[]{:S(2)}, u32[]{:S(2)}) %collective-permute-start.2) | collective-permute-done | bytes 327712 | tf_op jit(solution)/shard_map/ppermute | solution.py:43
  37.5 1.1 rev.40
  38.6 1.9 %select_select_fusion.2 = bf16[1,2,4,5,32,256]{5,4,2,1,3,0:T(8,128)(2,1)} fusion(bf16[1,2,4,5,32,256]{5,4,2,1,3,0:T(8,128)(2,1)S(1)} %bitcast.176, bf16[1,2,4,5,32,256]{5,4,2,1,3,0:T(8,128)(2,1)S(1)} %bitcast.167, pred[]{:T(512)S(6)} %eq.52, pred[]{:T(512)S(6)} %eq.51, bf16[1,1,4,5,32,256]{5,4,2,1,3,0:T(8,128)(2,1)} %bitcast.192, ...), kind=kLoop, calls=%fused_computation.66 | loop fusion | flops 983040 | bytes 2621442 | tf_op jit(solution)/shard_map/jit(_where)/select_n | solution.py:31
  40.5 2.0 %rev.41 = bf16[1,2,4,5,32,256]{5,4,2,1,3,0:T(8,128)(2,1)} reverse(bf16[1,2,4,5,32,256]{5,4,2,1,3,0:T(8,128)(2,1)} %select_select_fusion.2), dimensions={1} | reverse | bytes 1310720 | tf_op jit(solution)/shard_map/rev | solution.py:30
  45.9 5.6 %collective-permute-start.3 = (bf16[4,1,5,32,256]{4,3,0,2,1:T(8,128)(2,1)S(1)}, bf16[4,1,5,32,256]{4,3,0,2,1:T(8,128)(2,1)S(1)}, u32[]{:S(2)}, u32[]{:S(2)}) collective-permute-start(bf16[4,1,5,32,256]{4,3,0,2,1:T(8,128)(2,1)S(1)} %get-tuple-element.36), channel_id=1, source_target_pairs={{0,1},{1,0},{2,3},{3,2},{4,5},{5,4},{6,7},{7,6},{8,9},{9,8},{10,11... | collective-permute-start | bytes 983048 | tf_op jit(solution)/shard_map/ppermute | solution.py:43
  53.1 19.7 %all-to-all-start = ((bf16[64,8,512]{2,1,0:T(8,128)(2,1)}), bf16[64,8,512]{2,1,0:T(8,128)(2,1)}, u32[]{:S(2)}, u32[]{:S(2)}) async-start(bf16[64,8,512]{2,1,0:T(8,128)(2,1)} %bitcast.2), calls=%async_computation | async-start | bytes 1048576 | tf_op jit(solution)/shard_map/all_to_all | solution.py:81
  73.0 3.1 %collective-permute-start.4 = (bf16[2,2,5,32,256]{4,3,1,2,0:T(8,128)(2,1)S(1)}, bf16[2,2,5,32,256]{4,3,1,2,0:T(8,128)(2,1)S(1)}, u32[]{:S(2)}, u32[]{:S(2)}) collective-permute-start(bf16[2,2,5,32,256]{4,3,1,2,0:T(8,128)(2,1)S(1)} %bitcast.220), channel_id=1, source_target_pairs={{0,2},{1,3},{2,0},{3,1},{4,6},{5,7},{6,4},{7,5},{8,10},{9,11},{10,... | collective-permute-start | bytes 983048 | tf_op jit(solution)/shard_map/ppermute | solution.py:43
  77.3 6.5 %collective-permute-done.4 = bf16[2,2,5,32,256]{4,3,1,2,0:T(8,128)(2,1)S(1)} collective-permute-done((bf16[2,2,5,32,256]{4,3,1,2,0:T(8,128)(2,1)S(1)}, bf16[2,2,5,32,256]{4,3,1,2,0:T(8,128)(2,1)S(1)}, u32[]{:S(2)}, u32[]{:S(2)}) %collective-permute-start.4) | collective-permute-done | bytes 327712 | tf_op jit(solution)/shard_map/ppermute | solution.py:43
  84.0 5.7 %collective-permute-start.5 = (bf16[1,4,5,32,256]{4,3,1,2,0:T(8,128)(2,1)S(1)}, bf16[1,4,5,32,256]{4,3,1,2,0:T(8,128)(2,1)S(1)}, u32[]{:S(2)}, u32[]{:S(2)}) collective-permute-start(bf16[1,4,5,32,256]{4,3,1,2,0:T(8,128)(2,1)S(1)} %get-tuple-element.32), channel_id=1, source_target_pairs={{0,4},{1,5},{2,6},{3,7},{4,0},{5,1},{6,2},{7,3},{8,12},{9,13},{10,... | collective-permute-start | bytes 983048 | tf_op jit(solution)/shard_map/ppermute | solution.py:43
  89.8 1.8 %multiply_reduce_fusion = (f32[32,256]{1,0:T(8,128)}, f32[3,8,32,256]{3,2,1,0:T(8,128)}) fusion(f32[8,32,256]{2,1,0:T(8,128)S(1)} %convert_element_type.211, f32[256]{0:T(256)S(1)} %copy-done.16, bf16[3,8,32,256]{3,2,1,0:T(8,128)(2,1)S(1)} %copy-done.1, bf16[256,256]{1,0:T(8,128)(2,1)S(1)} %copy-done.11), kind=kOutput, calls=%fused_computation.46 | convolution fusion | flops 101834752 | bytes 1606656 | tf_op jit(solution)/shard_map/kxzj,ij->kxzi/dot_general | solution.py:64
  91.6 5.0 %collective-permute-done.5 = bf16[1,4,5,32,256]{4,3,1,2,0:T(8,128)(2,1)S(1)} collective-permute-done((bf16[1,4,5,32,256]{4,3,1,2,0:T(8,128)(2,1)S(1)}, bf16[1,4,5,32,256]{4,3,1,2,0:T(8,128)(2,1)S(1)}, u32[]{:S(2)}, u32[]{:S(2)}) %collective-permute-start.5) | collective-permute-done | bytes 327712 | tf_op jit(solution)/shard_map/ppermute | solution.py:43
  97.7 1.1 rev.46
  99.7 2.0 %rev.47 = bf16[1,2,4,5,32,256]{5,4,2,1,3,0:T(8,128)(2,1)} reverse(bf16[1,2,4,5,32,256]{5,4,2,1,3,0:T(8,128)(2,1)} %select_select_fusion.1), dimensions={1} | reverse | bytes 1310720 | tf_op jit(solution)/shard_map/rev | solution.py:30
  103.4 1.8 %all-to-all-done = bf16[64,8,512]{2,1,0:T(8,128)(2,1)} async-done(((bf16[64,8,512]{2,1,0:T(8,128)(2,1)}), bf16[64,8,512]{2,1,0:T(8,128)(2,1)}, u32[]{:S(2)}, u32[]{:S(2)}) %all-to-all-start) | async-done | bytes 524320 | tf_op jit(solution)/shard_map/all_to_all | solution.py:81
  107.6 1.3 fusion.85
  111.6 2.2 %fusion.30 = (f32[512,384]{0,1:T(8,128)S(1)}, f32[512,384]{0,1:T(8,128)S(1)}) fusion(f32[512,128]{0,1:T(8,128)S(1)} %fusion.43, bf16[512,512]{1,0:T(8,128)(2,1)S(1)} %copy-done, f32[1,384]{0,1:T(8,128)} %get-tuple-element.51, f32[511,384]{0,1:T(8,128)} %get-tuple-element.53, f32[511,384]{0,1:T(8,128)} %get-tuple-element.52, ...), kind=kOutput, calls=%fused_computation.74 | convolution fusion | flops 204472320 | bytes 5505024 | tf_op jit(solution)/shard_map/dot_general | solution.py:60
  117.2 45.6 %all_to_all.10 = bf16[64,8,512]{2,1,0:T(8,128)(2,1)S(1)} all-to-all(bf16[64,8,512]{2,1,0:T(8,128)(2,1)S(1)} %maximum_maximum_fusion), channel_id=1, replica_groups=mesh['gx'=64,'gz'=8] {'gx'}, dimensions={0} | all-to-all | bytes 1048576 | tf_op jit(solution)/shard_map/all_to_all | solution.py:125
  166.4 2.1 %fusion.6 = bf16[3,8,32,256]{3,2,1,0:T(8,128)(2,1)} fusion(f32[3,8,32,256]{3,2,1,0:T(8,128)S(1)} %reshape.353, bf16[3,8,32,256]{3,2,1,0:T(8,128)(2,1)S(1)} %copy-done.1, f32[3,8,32,256]{3,2,1,0:T(8,128)S(1)} %copy-done.3, bf16[8,5,32,256]{3,2,0,1:T(8,128)(2,1)} %copy-done.5, f32[8,32,256]{2,1,0:T(8,128)S(1)} %copy-done.7, f32[256]{0:T(256)S(1)} %copy-done.16, ...), kind=kOutput, calls=%fused_computation.8 | convolution fusion | flops 102629376 | bytes 3146752 | tf_op jit(solution)/shard_map/kxzj,ij->kxzi/dot_general | solution.py:64
  (134 shorter events, 24.9 us)
Async XLA Ops:
  0.6 110.1 %copy-start = (bf16[512,512]{1,0:T(8,128)(2,1)S(1)}, bf16[512,512]{1,0:T(8,128)(2,1)}, u32[]{:S(2)}) copy-start(bf16[512,512]{1,0:T(8,128)(2,1)} %param.11) | copy-start | bytes 1572868
  0.6 0.8 copy-start.15
  0.7 2.5 %copy-start.1 = (bf16[3,8,32,256]{3,2,1,0:T(8,128)(2,1)S(1)}, bf16[3,8,32,256]{3,2,1,0:T(8,128)(2,1)}, u32[]{:S(2)}) copy-start(bf16[3,8,32,256]{3,2,1,0:T(8,128)(2,1)} %param.7) | copy-start | bytes 1179652
  1.5 1.7 %copy-start.2 = (bf16[8,32,256]{2,1,0:T(8,128)(2,1)S(1)}, bf16[8,32,256]{2,1,0:T(8,128)(2,1)}, u32[]{:S(2)}) copy-start(bf16[8,32,256]{2,1,0:T(8,128)(2,1)} %param.8) | copy-start | bytes 393220
  3.8 10.1 %collective-permute-start = (bf16[4,1,5,32,256]{4,3,0,2,1:T(8,128)(2,1)S(1)}, bf16[4,1,5,32,256]{4,3,0,2,1:T(8,128)(2,1)S(1)}, u32[]{:S(2)}, u32[]{:S(2)}) collective-permute-start(bf16[4,1,5,32,256]{4,3,0,2,1:T(8,128)(2,1)S(1)} %get-tuple-element.45), channel_id=1, source_target_pairs={{0,1},{1,0},{2,3},{3,2},{4,5},{5,4},{6,7},{7,6},{8,9},{9,8},{10,11... | collective-permute-start | bytes 983048 | tf_op jit(solution)/shard_map/ppermute | solution.py:43
  13.9 10.3 %collective-permute-start.1 = (bf16[2,2,5,32,256]{4,3,1,2,0:T(8,128)(2,1)S(1)}, bf16[2,2,5,32,256]{4,3,1,2,0:T(8,128)(2,1)S(1)}, u32[]{:S(2)}, u32[]{:S(2)}) collective-permute-start(bf16[2,2,5,32,256]{4,3,1,2,0:T(8,128)(2,1)S(1)} %bitcast.221), channel_id=1, source_target_pairs={{0,2},{1,3},{2,0},{3,1},{4,6},{5,7},{6,4},{7,5},{8,10},{9,11},{10,... | collective-permute-start | bytes 983048 | tf_op jit(solution)/shard_map/ppermute | solution.py:43
  24.4 11.4 %collective-permute-start.2 = (bf16[1,4,5,32,256]{4,3,1,2,0:T(8,128)(2,1)S(1)}, bf16[1,4,5,32,256]{4,3,1,2,0:T(8,128)(2,1)S(1)}, u32[]{:S(2)}, u32[]{:S(2)}) collective-permute-start(bf16[1,4,5,32,256]{4,3,1,2,0:T(8,128)(2,1)S(1)} %get-tuple-element.41), channel_id=1, source_target_pairs={{0,4},{1,5},{2,6},{3,7},{4,0},{5,1},{6,2},{7,3},{8,12},{9,13},{10,... | collective-permute-start | bytes 983048 | tf_op jit(solution)/shard_map/ppermute | solution.py:43
  35.8 0.7 copy-start.4
  43.1 0.9 copy-start.10
  45.9 27.0 %collective-permute-start.3 = (bf16[4,1,5,32,256]{4,3,0,2,1:T(8,128)(2,1)S(1)}, bf16[4,1,5,32,256]{4,3,0,2,1:T(8,128)(2,1)S(1)}, u32[]{:S(2)}, u32[]{:S(2)}) collective-permute-start(bf16[4,1,5,32,256]{4,3,0,2,1:T(8,128)(2,1)S(1)} %get-tuple-element.36), channel_id=1, source_target_pairs={{0,1},{1,0},{2,3},{3,2},{4,5},{5,4},{6,7},{7,6},{8,9},{9,8},{10,11... | collective-permute-start | bytes 983048 | tf_op jit(solution)/shard_map/ppermute | solution.py:43
  53.1 52.1 %all-to-all-start = ((bf16[64,8,512]{2,1,0:T(8,128)(2,1)}), bf16[64,8,512]{2,1,0:T(8,128)(2,1)}, u32[]{:S(2)}, u32[]{:S(2)}) async-start(bf16[64,8,512]{2,1,0:T(8,128)(2,1)} %bitcast.2), calls=%async_computation | async-start | bytes 1048576 | tf_op jit(solution)/shard_map/all_to_all | solution.py:81
  73.0 10.7 %collective-permute-start.4 = (bf16[2,2,5,32,256]{4,3,1,2,0:T(8,128)(2,1)S(1)}, bf16[2,2,5,32,256]{4,3,1,2,0:T(8,128)(2,1)S(1)}, u32[]{:S(2)}, u32[]{:S(2)}) collective-permute-start(bf16[2,2,5,32,256]{4,3,1,2,0:T(8,128)(2,1)S(1)} %bitcast.220), channel_id=1, source_target_pairs={{0,2},{1,3},{2,0},{3,1},{4,6},{5,7},{6,4},{7,5},{8,10},{9,11},{10,... | collective-permute-start | bytes 983048 | tf_op jit(solution)/shard_map/ppermute | solution.py:43
  83.8 6.0 %copy-start.11 = (bf16[256,256]{1,0:T(8,128)(2,1)S(1)}, bf16[256,256]{1,0:T(8,128)(2,1)}, u32[]{:S(2)}) copy-start(bf16[256,256]{1,0:T(8,128)(2,1)} %param.13) | copy-start | bytes 393220
  83.9 5.8 %copy-start.16 = (f32[256]{0:T(256)S(1)}, f32[256]{0:T(256)}, u32[]{:S(2)}) copy-start(f32[256]{0:T(256)} %param.10) | copy-start | bytes 3076
  84.0 12.6 %collective-permute-start.5 = (bf16[1,4,5,32,256]{4,3,1,2,0:T(8,128)(2,1)S(1)}, bf16[1,4,5,32,256]{4,3,1,2,0:T(8,128)(2,1)S(1)}, u32[]{:S(2)}, u32[]{:S(2)}) collective-permute-start(bf16[1,4,5,32,256]{4,3,1,2,0:T(8,128)(2,1)S(1)} %get-tuple-element.32), channel_id=1, source_target_pairs={{0,4},{1,5},{2,6},{3,7},{4,0},{5,1},{6,2},{7,3},{8,12},{9,13},{10,... | collective-permute-start | bytes 983048 | tf_op jit(solution)/shard_map/ppermute | solution.py:43
  101.8 0.9 copy-start.5
  110.6 0.9 copy-start.8
  110.6 1.0 copy-start.9
  115.8 0.8 copy-start.13
  115.8 0.8 copy-start.14
  162.7 0.8 copy-start.6
  164.0 2.4 %copy-start.3 = (f32[3,8,32,256]{3,2,1,0:T(8,128)S(1)}, f32[3,8,32,256]{3,2,1,0:T(8,128)}, u32[]{:S(2)}) copy-start(f32[3,8,32,256]{3,2,1,0:T(8,128)} %get-tuple-element.61) | copy-start | bytes 2359300
  164.0 2.4 %copy-start.7 = (f32[8,32,256]{2,1,0:T(8,128)S(1)}, f32[8,32,256]{2,1,0:T(8,128)}, u32[]{:S(2)}) copy-start(f32[8,32,256]{2,1,0:T(8,128)} %get-tuple-element.56) | copy-start | bytes 786436
  164.6 1.7 %copy-start.12 = (bf16[256,256]{1,0:T(8,128)(2,1)S(1)}, bf16[256,256]{1,0:T(8,128)(2,1)}, u32[]{:S(2)}) copy-start(bf16[256,256]{1,0:T(8,128)(2,1)} %param.13) | copy-start | bytes 393220
  (2 other events, 1.3 us)

commit v7 on v6

--- a/solution.py
+++ b/solution.py
@@ -98,8 +98,7 @@
     gzn = lax.axis_size("gz")
     mine = lax.axis_index("gz")
     zs = jnp.concatenate([adjoint, viscosity[None], strain[None]], axis=0)
-    zt = butterfly(zs.transpose(1, 0, 2, 3), mine)
-    zt = zt.transpose(1, 0, 2, 3).reshape(zs.shape[0], gzn * nzl, ny)
+    zt = lax.all_to_all(zs, "gz", 1, 2, tiled=True)[:, 0]
     span_visc = zt[comps].astype(f32)
     span_strain = zt[comps + 1].astype(f32)
     span_grad = derivative(zt[:comps], span_inverse)

time: 171 us -> 144 us (0.84); the launches traced: 168 us -> 143 us
  starting transfers between devices: 52.3 us -> 35.8 us
  local copies, waits for them, and re-layouts: 23.8 us -> 17.9 us
    ppermute x6 -> x3, starting transfers between devices: 32.6 us -> 8.36 us  [butterfly(): moved = lax.ppermute(split[:, 1], 'gz', pairs)]
    ppermute x6 -> x3, waiting for transfers between devices: 25 us -> 13.5 us  [butterfly(): moved = lax.ppermute(split[:, 1], 'gz', pairs)]
    all_to_all x0 -> x1, waiting for transfers between devices: none -> 9.36 us  [on_device(): zt = lax.all_to_all(zs, 'gz', 1, 2, tiled=True)[:, 0]]
    all_to_all x0 -> x1, starting transfers between devices: none -> 7.47 us  [on_device(): zt = lax.all_to_all(zs, 'gz', 1, 2, tiled=True)[:, 0]]
    rev x12 -> x6, local copies, waits for them, and re-layouts: 6.58 us -> 2.46 us  [xor_order(): blocks.reshape(size // (2 * bit), 2, bit, *blocks.shape[1:])[:, ::-1]]
    unnamed x44 -> x30, local copies, waits for them, and re-layouts: 5.79 us -> 2.52 us
    select_n x11 -> x6, other arithmetic: 5.37 us -> 3.1 us  [xor_order(): jnp.where(mine // bit % 2 == 1, swapped.reshape(blocks.shape), blocks)]
  transfers between devices with their start and end apart: 7 -> 5, of which waited for: 6 -> 4; matrix products, arithmetic and copies ran while one was open for 6% -> 9% of each run, Pallas kernels for 0% -> 0%
where the time goes in v7:
time: 144 us; the launch traced here: 143 us
  blocking collectives  44.8 us (31%)
  starting transfers between devices  35.8 us (25%)
  waiting for transfers between devices  25.8 us (18%)
  local copies, waits for them, and re-layouts  17.9 us (12%)
  other arithmetic  9.69 us (7%)
  matrix products  8.06 us (6%)
    all_to_all x1, blocking collectives, on_device(): back = lax.all_to_all(back, 'gx', 0, 0, tiled=True)  44.8 us
    all_to_all x1, starting transfers between devices, on_device(): lax.all_to_all(xs, 'gx', 0, 0, tiled=True).reshape(nx, (comps + 1) * lanes)  19.9 us
    ppermute x3, waiting for transfers between devices, butterfly(): moved = lax.ppermute(split[:, 1], 'gz', pairs)  13.5 us
    all_to_all x1, waiting for transfers between devices, on_device(): zt = lax.all_to_all(zs, 'gz', 1, 2, tiled=True)[:, 0]  9.36 us
    ppermute x3, starting transfers between devices, butterfly(): moved = lax.ppermute(split[:, 1], 'gz', pairs)  8.36 us
    all_to_all x1, starting transfers between devices, on_device(): zt = lax.all_to_all(zs, 'gz', 1, 2, tiled=True)[:, 0]  7.47 us
    dot_general x2, matrix products, wall_derivative(): jnp.einsum('kxzj,ij->kxzi', source, wall_operator, preferred_element_type...  4.02 us
    select_n x6, other arithmetic, xor_order(): jnp.where(mine // bit % 2 == 1, swapped.reshape(blocks.shape), blocks)  3.1 us
  transfers between devices with their start and end apart: 5, of which 4 were waited for; matrix products, arithmetic and copies ran while one was open for 9% of the time, Pallas kernels for 0%

profile of v7, /device:TPU:1, one launch (start us, length us, event | category | flops | bytes accessed | tf_op | source)
XLA Modules:
  0.0 143.3 jit_solution(535685703489380704)
XLA Ops:
  0.7 1.7 %fusion.47 = (f32[8,32,256]{2,1,0:T(8,128)}, bf16[1,8,32,256]{3,2,0,1:T(8,128)(2,1)S(1)}) fusion(bf16[8,32,256]{2,1,0:T(8,128)(2,1)} %param.8, f32[32,256]{1,0:T(8,128)} %param.9), kind=kLoop, calls=%fused_computation.92 | loop fusion | flops 262144 | bytes 557056 | tf_op jit(solution)/shard_map/convert_element_type | solution.py:76
  2.4 1.8 %pad_maximum_fusion = bf16[5,8,32,256]{3,2,0,1:T(8,128)(2,1)} fusion(bf16[1,8,32,256]{3,2,0,1:T(8,128)(2,1)} %bitcast.145, bf16[1,8,32,256]{3,2,0,1:T(8,128)(2,1)S(1)} %get-tuple-element.50, bf16[3,8,32,256]{3,2,1,0:T(8,128)(2,1)S(1)} %copy-done.1), kind=kLoop, calls=%fused_computation.49 | loop fusion | flops 1966080 | bytes 1310720 | tf_op jit(solution)/shard_map/concatenate | solution.py:100
  4.2 7.5 %all-to-all-start.1 = ((bf16[5,8,32,256]{3,2,0,1:T(8,128)(2,1)}), bf16[5,8,32,256]{3,2,0,1:T(8,128)(2,1)S(1)}, u32[]{:S(2)}, u32[]{:S(2)}) async-start(bf16[5,8,32,256]{3,2,0,1:T(8,128)(2,1)} %pad_maximum_fusion), calls=%async_computation.1 | async-start | bytes 1310720 | tf_op jit(solution)/shard_map/all_to_all | solution.py:101
  11.6 9.4 %all-to-all-done.1 = bf16[5,8,32,256]{3,2,0,1:T(8,128)(2,1)S(1)} async-done(((bf16[5,8,32,256]{3,2,0,1:T(8,128)(2,1)}), bf16[5,8,32,256]{3,2,0,1:T(8,128)(2,1)S(1)}, u32[]{:S(2)}, u32[]{:S(2)}) %all-to-all-start.1) | async-done | bytes 655392 | tf_op jit(solution)/shard_map/all_to_all | solution.py:101
  24.2 3.4 %collective-permute-start = (bf16[4,1,5,32,256]{4,3,0,2,1:T(8,128)(2,1)S(1)}, bf16[4,1,5,32,256]{4,3,0,2,1:T(8,128)(2,1)S(1)}, u32[]{:S(2)}, u32[]{:S(2)}) collective-permute-start(bf16[4,1,5,32,256]{4,3,0,2,1:T(8,128)(2,1)S(1)} %get-tuple-element.36), channel_id=1, source_target_pairs={{0,1},{1,0},{2,3},{3,2},{4,5},{5,4},{6,7},{7,6},{8,9},{9,8},{10,11... | collective-permute-start | bytes 983048 | tf_op jit(solution)/shard_map/ppermute | solution.py:43
  29.2 19.9 %all-to-all-start = ((bf16[64,8,512]{2,1,0:T(8,128)(2,1)}), bf16[64,8,512]{2,1,0:T(8,128)(2,1)}, u32[]{:S(2)}, u32[]{:S(2)}) async-start(bf16[64,8,512]{2,1,0:T(8,128)(2,1)} %bitcast.2), calls=%async_computation | async-start | bytes 1048576 | tf_op jit(solution)/shard_map/all_to_all | solution.py:81
  49.4 2.2 %collective-permute-start.1 = (bf16[2,2,5,32,256]{4,3,1,2,0:T(8,128)(2,1)S(1)}, bf16[2,2,5,32,256]{4,3,1,2,0:T(8,128)(2,1)S(1)}, u32[]{:S(2)}, u32[]{:S(2)}) collective-permute-start(bf16[2,2,5,32,256]{4,3,1,2,0:T(8,128)(2,1)S(1)} %bitcast.154), channel_id=1, source_target_pairs={{0,2},{1,3},{2,0},{3,1},{4,6},{5,7},{6,4},{7,5},{8,10},{9,11},{10,... | collective-permute-start | bytes 983048 | tf_op jit(solution)/shard_map/ppermute | solution.py:43
  52.7 7.4 %collective-permute-done.1 = bf16[2,2,5,32,256]{4,3,1,2,0:T(8,128)(2,1)S(1)} collective-permute-done((bf16[2,2,5,32,256]{4,3,1,2,0:T(8,128)(2,1)S(1)}, bf16[2,2,5,32,256]{4,3,1,2,0:T(8,128)(2,1)S(1)}, u32[]{:S(2)}, u32[]{:S(2)}) %collective-permute-start.1) | collective-permute-done | bytes 327712 | tf_op jit(solution)/shard_map/ppermute | solution.py:43
  60.3 2.8 %collective-permute-start.2 = (bf16[1,4,5,32,256]{4,3,1,2,0:T(8,128)(2,1)S(1)}, bf16[1,4,5,32,256]{4,3,1,2,0:T(8,128)(2,1)S(1)}, u32[]{:S(2)}, u32[]{:S(2)}) collective-permute-start(bf16[1,4,5,32,256]{4,3,1,2,0:T(8,128)(2,1)S(1)} %get-tuple-element.32), channel_id=1, source_target_pairs={{0,4},{1,5},{2,6},{3,7},{4,0},{5,1},{6,2},{7,3},{8,12},{9,13},{10,... | collective-permute-start | bytes 983048 | tf_op jit(solution)/shard_map/ppermute | solution.py:43
  63.9 1.8 %multiply_reduce_fusion = (f32[32,256]{1,0:T(8,128)}, f32[3,8,32,256]{3,2,1,0:T(8,128)}) fusion(f32[8,32,256]{2,1,0:T(8,128)S(1)} %convert_element_type.211, f32[256]{0:T(256)S(1)} %copy-done.10, bf16[3,8,32,256]{3,2,1,0:T(8,128)(2,1)S(1)} %copy-done.1, bf16[256,256]{1,0:T(8,128)(2,1)S(1)} %copy-done.7), kind=kOutput, calls=%fused_computation.46 | convolution fusion | flops 101834752 | bytes 1606656 | tf_op jit(solution)/shard_map/kxzj,ij->kxzi/dot_general | solution.py:64
  65.7 6.1 %collective-permute-done.2 = bf16[1,4,5,32,256]{4,3,1,2,0:T(8,128)(2,1)S(1)} collective-permute-done((bf16[1,4,5,32,256]{4,3,1,2,0:T(8,128)(2,1)S(1)}, bf16[1,4,5,32,256]{4,3,1,2,0:T(8,128)(2,1)S(1)}, u32[]{:S(2)}, u32[]{:S(2)}) %collective-permute-start.2) | collective-permute-done | bytes 327712 | tf_op jit(solution)/shard_map/ppermute | solution.py:43
  71.9 1.0 maximum_select_fusion
  72.9 1.1 rev.22
  74.0 1.0 select_select_fusion.1
  75.0 1.1 rev.23
  76.1 1.0 select_select_fusion
  77.1 1.0 slice_bitcast_fusion.2
  78.7 2.9 %all-to-all-done = bf16[64,8,512]{2,1,0:T(8,128)(2,1)} async-done(((bf16[64,8,512]{2,1,0:T(8,128)(2,1)}), bf16[64,8,512]{2,1,0:T(8,128)(2,1)}, u32[]{:S(2)}, u32[]{:S(2)}) %all-to-all-start) | async-done | bytes 524320 | tf_op jit(solution)/shard_map/all_to_all | solution.py:81
  82.5 1.0 slice.225
  83.9 1.4 fusion.82
  87.1 2.3 %fusion.30 = (f32[512,384]{0,1:T(8,128)S(1)}, f32[512,384]{0,1:T(8,128)S(1)}) fusion(f32[512,128]{0,1:T(8,128)S(1)} %fusion.42, bf16[512,512]{1,0:T(8,128)(2,1)S(1)} %copy-done, f32[1,384]{0,1:T(8,128)} %get-tuple-element.44, f32[511,384]{0,1:T(8,128)} %get-tuple-element.46, f32[511,384]{0,1:T(8,128)} %get-tuple-element.45, ...), kind=kOutput, calls=%fused_computation.64 | convolution fusion | flops 204472320 | bytes 5505024 | tf_op jit(solution)/shard_map/dot_general | solution.py:60
  92.7 44.8 %all_to_all.19 = bf16[64,8,512]{2,1,0:T(8,128)(2,1)S(1)} all-to-all(bf16[64,8,512]{2,1,0:T(8,128)(2,1)S(1)} %maximum_maximum_fusion), channel_id=1, replica_groups=mesh['gx'=64,'gz'=8] {'gx'}, dimensions={0} | all-to-all | bytes 1048576 | tf_op jit(solution)/shard_map/all_to_all | solution.py:124
  139.4 0.9 slice_bitcast_fusion.3
  141.1 2.2 %fusion.6 = bf16[3,8,32,256]{3,2,1,0:T(8,128)(2,1)} fusion(f32[3,8,32,256]{3,2,1,0:T(8,128)S(1)} %reshape.254, bf16[3,8,32,256]{3,2,1,0:T(8,128)(2,1)S(1)} %copy-done.1, f32[3,8,32,256]{3,2,1,0:T(8,128)S(1)} %copy-done.2, bf16[8,5,32,256]{3,2,0,1:T(8,128)(2,1)} %select_select_fusion, f32[8,32,256]{2,1,0:T(8,128)S(1)} %copy-done.5, f32[256]{0:T(256)S(1)} %copy-done.10, ...), kind=kOutput, calls=%fused_computation.8 | convolution fusion | flops 102629376 | bytes 3146752 | tf_op jit(solution)/shard_map/kxzj,ij->kxzi/dot_general | solution.py:64
  (99 shorter events, 16.4 us)
Async XLA Ops:
  0.6 86.5 %copy-start = (bf16[512,512]{1,0:T(8,128)(2,1)S(1)}, bf16[512,512]{1,0:T(8,128)(2,1)}, u32[]{:S(2)}) copy-start(bf16[512,512]{1,0:T(8,128)(2,1)} %param.11) | copy-start | bytes 1572868
  0.6 1.7 %copy-start.1 = (bf16[3,8,32,256]{3,2,1,0:T(8,128)(2,1)S(1)}, bf16[3,8,32,256]{3,2,1,0:T(8,128)(2,1)}, u32[]{:S(2)}) copy-start(bf16[3,8,32,256]{3,2,1,0:T(8,128)(2,1)} %param.7) | copy-start | bytes 1179652
  4.2 16.8 %all-to-all-start.1 = ((bf16[5,8,32,256]{3,2,0,1:T(8,128)(2,1)}), bf16[5,8,32,256]{3,2,0,1:T(8,128)(2,1)S(1)}, u32[]{:S(2)}, u32[]{:S(2)}) async-start(bf16[5,8,32,256]{3,2,0,1:T(8,128)(2,1)} %pad_maximum_fusion), calls=%async_computation.1 | async-start | bytes 1310720 | tf_op jit(solution)/shard_map/all_to_all | solution.py:101
  21.4 0.9 copy-start.6
  24.1 3.5 %copy-start.3 = (bf16[8,32,256]{2,1,0:T(8,128)(2,1)S(1)}, bf16[8,32,256]{2,1,0:T(8,128)(2,1)}, u32[]{:S(2)}) copy-start(bf16[8,32,256]{2,1,0:T(8,128)(2,1)} %param.8) | copy-start | bytes 393220
  24.2 25.1 %collective-permute-start = (bf16[4,1,5,32,256]{4,3,0,2,1:T(8,128)(2,1)S(1)}, bf16[4,1,5,32,256]{4,3,0,2,1:T(8,128)(2,1)S(1)}, u32[]{:S(2)}, u32[]{:S(2)}) collective-permute-start(bf16[4,1,5,32,256]{4,3,0,2,1:T(8,128)(2,1)S(1)} %get-tuple-element.36), channel_id=1, source_target_pairs={{0,1},{1,0},{2,3},{3,2},{4,5},{5,4},{6,7},{7,6},{8,9},{9,8},{10,11... | collective-permute-start | bytes 983048 | tf_op jit(solution)/shard_map/ppermute | solution.py:43
  29.2 52.4 %all-to-all-start = ((bf16[64,8,512]{2,1,0:T(8,128)(2,1)}), bf16[64,8,512]{2,1,0:T(8,128)(2,1)}, u32[]{:S(2)}, u32[]{:S(2)}) async-start(bf16[64,8,512]{2,1,0:T(8,128)(2,1)} %bitcast.2), calls=%async_computation | async-start | bytes 1048576 | tf_op jit(solution)/shard_map/all_to_all | solution.py:81
  49.4 10.7 %collective-permute-start.1 = (bf16[2,2,5,32,256]{4,3,1,2,0:T(8,128)(2,1)S(1)}, bf16[2,2,5,32,256]{4,3,1,2,0:T(8,128)(2,1)S(1)}, u32[]{:S(2)}, u32[]{:S(2)}) collective-permute-start(bf16[2,2,5,32,256]{4,3,1,2,0:T(8,128)(2,1)S(1)} %bitcast.154), channel_id=1, source_target_pairs={{0,2},{1,3},{2,0},{3,1},{4,6},{5,7},{6,4},{7,5},{8,10},{9,11},{10,... | collective-permute-start | bytes 983048 | tf_op jit(solution)/shard_map/ppermute | solution.py:43
  60.2 3.7 %copy-start.7 = (bf16[256,256]{1,0:T(8,128)(2,1)S(1)}, bf16[256,256]{1,0:T(8,128)(2,1)}, u32[]{:S(2)}) copy-start(bf16[256,256]{1,0:T(8,128)(2,1)} %param.13) | copy-start | bytes 393220
  60.2 3.7 %copy-start.10 = (f32[256]{0:T(256)S(1)}, f32[256]{0:T(256)}, u32[]{:S(2)}) copy-start(f32[256]{0:T(256)} %param.10) | copy-start | bytes 3076
  60.3 11.5 %collective-permute-start.2 = (bf16[1,4,5,32,256]{4,3,1,2,0:T(8,128)(2,1)S(1)}, bf16[1,4,5,32,256]{4,3,1,2,0:T(8,128)(2,1)S(1)}, u32[]{:S(2)}, u32[]{:S(2)}) collective-permute-start(bf16[1,4,5,32,256]{4,3,1,2,0:T(8,128)(2,1)S(1)} %get-tuple-element.32), channel_id=1, source_target_pairs={{0,4},{1,5},{2,6},{3,7},{4,0},{5,1},{6,2},{7,3},{8,12},{9,13},{10,... | collective-permute-start | bytes 983048 | tf_op jit(solution)/shard_map/ppermute | solution.py:43
  91.3 0.8 copy-start.8
  91.3 0.8 copy-start.9
  91.3 0.8 copy-start.11
  91.3 0.8 copy-start.12
  137.5 0.8 copy-start.4
  138.7 2.3 %copy-start.2 = (f32[3,8,32,256]{3,2,1,0:T(8,128)S(1)}, f32[3,8,32,256]{3,2,1,0:T(8,128)}, u32[]{:S(2)}) copy-start(f32[3,8,32,256]{3,2,1,0:T(8,128)} %get-tuple-element.54) | copy-start | bytes 2359300
  138.7 2.3 %copy-start.5 = (f32[8,32,256]{2,1,0:T(8,128)S(1)}, f32[8,32,256]{2,1,0:T(8,128)}, u32[]{:S(2)}) copy-start(f32[8,32,256]{2,1,0:T(8,128)} %get-tuple-element.49) | copy-start | bytes 786436

commit v8 on v7

--- a/solution.py
+++ b/solution.py
@@ -10,16 +10,17 @@
 bf16 = jnp.bfloat16
 
 
-def stencil(source, axis):
-    widened = source.astype(f32)
-    near_diff = jnp.roll(widened, -1, axis) - jnp.roll(widened, 1, axis)
-    far_diff = jnp.roll(widened, -2, axis) - jnp.roll(widened, 2, axis)
-    return (near_coef * near_diff + far_coef * far_diff).astype(bf16)
+def folded(operator):
+    wide = operator.astype(f32)
+    shifted = lambda step: jnp.roll(wide, step, 1)
+    merged = near_coef * (shifted(1) - shifted(-1)) + far_coef * (shifted(2) - shifted(-2))
+    return split_wide(merged)
 
 
 def derivative(pencil, operator):
-    right_side = stencil(pencil, 1)
-    product = jnp.einsum("ij,cjp->cip", operator, right_side, preferred_element_type=f32)
+    product = sum(
+        jnp.einsum("ij,cjp->cip", part, pencil, preferred_element_type=f32) for part in operator
+    )
     return product.astype(bf16)
 
 
@@ -56,8 +57,8 @@
 
 
 def row_derivative(pencil, operator):
-    right_side = stencil(pencil, 0)
-    return jnp.dot(operator, right_side, preferred_element_type=f32).astype(bf16)
+    product = sum(jnp.dot(part, pencil, preferred_element_type=f32) for part in operator)
+    return product.astype(bf16)
 
 
 def wall_derivative(source, wall_operator, metric):
@@ -71,6 +72,8 @@
     lanes = nzl * ny // gxn
     yparts = ny // lanes
     nx = nxl * gxn
+    stream_inverse = folded(stream_inverse)
+    span_inverse = folded(span_inverse)
     strain_wide = strain.astype(f32)
     viscosity = (correction[None] * strain_wide).astype(bf16)
     viscous = viscosity.astype(f32)

time: 144 us -> 149 us (1.035)
  waiting for transfers between devices: 25.8 us -> 21.4 us
  blocking collectives: 44.8 us -> 49 us
  other arithmetic: 9.69 us -> 12.1 us
  local copies, waits for them, and re-layouts: 17.9 us -> 19.6 us
    all_to_all x1, waiting for transfers between devices: 9.36 us -> 0.01 us  [on_device(): zt = lax.all_to_all(zs, 'gz', 1, 2, tiled=True)[:, 0]]
    ppermute x3, waiting for transfers between devices: 13.5 us -> 21.3 us  [butterfly(): moved = lax.ppermute(split[:, 1], 'gz', pairs)]
    all_to_all x1, blocking collectives: 44.8 us -> 49 us  [on_device(): back = lax.all_to_all(back, 'gx', 0, 0, tiled=True)]
    all_to_all x1, waiting for transfers between devices: 2.89 us -> 0.01 us  [on_device(): lax.all_to_all(xs, 'gx', 0, 0, tiled=True).reshape(nx, (comps + 1) * lanes)]
    add x0 -> x2, other arithmetic: none -> 2.01 us  [folded(): near_coef * (shifted(1) - shifted(-1))]
    dot_general x4 -> x8, matrix products: 4.04 us -> 4.97 us  [the longest x4 3.73 us: row_derivative(): jnp.dot(part, pencil, preferred_element_type=f32)]
    unnamed x30 -> x48, local copies, waits for them, and re-layouts: 2.52 us -> 3.02 us
    slice x17 -> x9, local copies, waits for them, and re-layouts: 5.58 us -> 5.97 us  [the longest x8 5.94 us: folded(): shifted = lambda step: jnp.roll(wide, step, 1)]
  transfers between devices with their start and end apart: 5 -> 5, of which waited for: 4 -> 3; matrix products, arithmetic and copies ran while one was open for 9% -> 16% of each run, Pallas kernels for 0% -> 0%
where the time goes in v8:
time: 149 us; the launch traced here: 148 us
  blocking collectives  49 us (33%)
  starting transfers between devices  35.9 us (24%)
  waiting for transfers between devices  21.4 us (14%)
  local copies, waits for them, and re-layouts  19.6 us (13%)
  other arithmetic  12.1 us (8%)
  matrix products  8.89 us (6%)
    all_to_all x1, blocking collectives, on_device(): back = lax.all_to_all(back, 'gx', 0, 0, tiled=True)  49 us
    ppermute x3, waiting for transfers between devices, butterfly(): moved = lax.ppermute(split[:, 1], 'gz', pairs)  21.3 us
    all_to_all x1, starting transfers between devices, on_device(): lax.all_to_all(xs, 'gx', 0, 0, tiled=True).reshape(nx, (comps + 1) * lanes)  18.8 us
    ppermute x3, starting transfers between devices, butterfly(): moved = lax.ppermute(split[:, 1], 'gz', pairs)  9.46 us
    all_to_all x1, starting transfers between devices, on_device(): zt = lax.all_to_all(zs, 'gz', 1, 2, tiled=True)[:, 0]  7.6 us
    slice x8, local copies, waits for them, and re-layouts, folded(): shifted = lambda step: jnp.roll(wide, step, 1)  5.94 us
    dot_general x2, matrix products, wall_derivative(): jnp.einsum('kxzj,ij->kxzi', source, wall_operator, preferred_element_type...  3.92 us
    dot_general x4, matrix products, row_derivative(): jnp.dot(part, pencil, preferred_element_type=f32)  3.73 us
  transfers between devices with their start and end apart: 5, of which 3 were waited for; matrix products, arithmetic and copies ran while one was open for 16% of the time, Pallas kernels for 0%

profile of v8, /device:TPU:1, one launch (start us, length us, event | category | flops | bytes accessed | tf_op | source)
XLA Modules:
  0.0 148.1 jit_solution(3005232984274471957)
XLA Ops:
  0.6 1.7 %fusion.40 = (f32[8,32,256]{2,1,0:T(8,128)}, bf16[1,8,32,256]{3,2,0,1:T(8,128)(2,1)S(1)}) fusion(bf16[8,32,256]{2,1,0:T(8,128)(2,1)} %param.8, f32[32,256]{1,0:T(8,128)} %param.9), kind=kLoop, calls=%fused_computation.86 | loop fusion | flops 262144 | bytes 557056 | tf_op jit(solution)/shard_map/convert_element_type | solution.py:79
  2.3 2.0 %pad_maximum_fusion = bf16[5,8,32,256]{3,2,0,1:T(8,128)(2,1)} fusion(bf16[1,8,32,256]{3,2,0,1:T(8,128)(2,1)} %bitcast.143, bf16[1,8,32,256]{3,2,0,1:T(8,128)(2,1)S(1)} %get-tuple-element.24, bf16[3,8,32,256]{3,2,1,0:T(8,128)(2,1)} %param.7), kind=kLoop, calls=%fused_computation.36 | loop fusion | flops 1966080 | bytes 1310720 | tf_op jit(solution)/shard_map/concatenate | solution.py:103
  4.3 7.6 %all-to-all-start.1 = ((bf16[5,8,32,256]{3,2,0,1:T(8,128)(2,1)}), bf16[5,8,32,256]{3,2,0,1:T(8,128)(2,1)S(1)}, u32[]{:S(2)}, u32[]{:S(2)}) async-start(bf16[5,8,32,256]{3,2,0,1:T(8,128)(2,1)} %pad_maximum_fusion), calls=%async_computation.1 | async-start | bytes 1310720 | tf_op jit(solution)/shard_map/all_to_all | solution.py:104
  15.2 1.4 copy.54
  17.5 1.2 fusion.30
  18.7 1.7 %fusion.54 = (f32[512,510]{1,0:T(8,128)}, f32[512,510]{1,0:T(8,128)}) fusion(bf16[512,512]{1,0:T(8,128)(2,1)S(1)} %copy-done.1), kind=kLoop, calls=%fused_computation.110 | loop fusion | bytes 4177920 | tf_op jit(solution)/shard_map/jit(_roll_static)/slice | solution.py:15
  20.4 1.7 %fusion.56 = (f32[512,511]{1,0:T(8,128)}, f32[512,511]{1,0:T(8,128)}) fusion(bf16[512,512]{1,0:T(8,128)(2,1)S(1)} %copy-done.1), kind=kLoop, calls=%fused_computation.112 | loop fusion | bytes 4186112 | tf_op jit(solution)/shard_map/jit(_roll_static)/slice | solution.py:15
  22.1 18.8 %all-to-all-start = ((bf16[64,8,512]{2,1,0:T(8,128)(2,1)}), bf16[64,8,512]{2,1,0:T(8,128)(2,1)}, u32[]{:S(2)}, u32[]{:S(2)}) async-start(bf16[64,8,512]{2,1,0:T(8,128)(2,1)} %bitcast.2), calls=%async_computation | async-start | bytes 1048576 | tf_op jit(solution)/shard_map/all_to_all | solution.py:84
  43.5 4.2 %collective-permute-start = (bf16[4,1,5,32,256]{4,3,0,2,1:T(8,128)(2,1)S(1)}, bf16[4,1,5,32,256]{4,3,0,2,1:T(8,128)(2,1)S(1)}, u32[]{:S(2)}, u32[]{:S(2)}) collective-permute-start(bf16[4,1,5,32,256]{4,3,0,2,1:T(8,128)(2,1)S(1)} %get-tuple-element.10), channel_id=1, source_target_pairs={{0,1},{1,0},{2,3},{3,2},{4,5},{5,4},{6,7},{7,6},{8,9},{9,8},{10,11... | collective-permute-start | bytes 983048 | tf_op jit(solution)/shard_map/ppermute | solution.py:44
  48.6 9.8 %collective-permute-done = bf16[4,1,5,32,256]{4,3,0,2,1:T(8,128)(2,1)S(1)} collective-permute-done((bf16[4,1,5,32,256]{4,3,0,2,1:T(8,128)(2,1)S(1)}, bf16[4,1,5,32,256]{4,3,0,2,1:T(8,128)(2,1)S(1)}, u32[]{:S(2)}, u32[]{:S(2)}) %collective-permute-start) | collective-permute-done | bytes 327712 | tf_op jit(solution)/shard_map/ppermute | solution.py:44
  58.5 2.1 %collective-permute-start.1 = (bf16[2,2,5,32,256]{4,3,1,2,0:T(8,128)(2,1)S(1)}, bf16[2,2,5,32,256]{4,3,1,2,0:T(8,128)(2,1)S(1)}, u32[]{:S(2)}, u32[]{:S(2)}) collective-permute-start(bf16[2,2,5,32,256]{4,3,1,2,0:T(8,128)(2,1)S(1)} %bitcast.151), channel_id=1, source_target_pairs={{0,2},{1,3},{2,0},{3,1},{4,6},{5,7},{6,4},{7,5},{8,10},{9,11},{10,... | collective-permute-start | bytes 983048 | tf_op jit(solution)/shard_map/ppermute | solution.py:44
  61.8 6.7 %collective-permute-done.1 = bf16[2,2,5,32,256]{4,3,1,2,0:T(8,128)(2,1)S(1)} collective-permute-done((bf16[2,2,5,32,256]{4,3,1,2,0:T(8,128)(2,1)S(1)}, bf16[2,2,5,32,256]{4,3,1,2,0:T(8,128)(2,1)S(1)}, u32[]{:S(2)}, u32[]{:S(2)}) %collective-permute-start.1) | collective-permute-done | bytes 327712 | tf_op jit(solution)/shard_map/ppermute | solution.py:44
  68.7 3.1 %collective-permute-start.2 = (bf16[1,4,5,32,256]{4,3,1,2,0:T(8,128)(2,1)S(1)}, bf16[1,4,5,32,256]{4,3,1,2,0:T(8,128)(2,1)S(1)}, u32[]{:S(2)}, u32[]{:S(2)}) collective-permute-start(bf16[1,4,5,32,256]{4,3,1,2,0:T(8,128)(2,1)S(1)} %get-tuple-element.6), channel_id=1, source_target_pairs={{0,4},{1,5},{2,6},{3,7},{4,0},{5,1},{6,2},{7,3},{8,12},{9,13},{10,... | collective-permute-start | bytes 983048 | tf_op jit(solution)/shard_map/ppermute | solution.py:44
  72.6 1.8 %multiply_reduce_fusion = (f32[32,256]{1,0:T(8,128)}, f32[3,8,32,256]{3,2,1,0:T(8,128)}) fusion(f32[8,32,256]{2,1,0:T(8,128)S(1)} %copy-done.16, f32[256]{0:T(256)S(1)} %copy-done.19, bf16[3,8,32,256]{3,2,1,0:T(8,128)(2,1)S(1)} %copy-done.3, bf16[256,256]{1,0:T(8,128)(2,1)S(1)} %copy-done), kind=kOutput, calls=%fused_computation.33 | convolution fusion | flops 101834752 | bytes 1606656 | tf_op jit(solution)/shard_map/kxzj,ij->kxzi/dot_general | solution.py:65
  74.5 4.9 %collective-permute-done.2 = bf16[1,4,5,32,256]{4,3,1,2,0:T(8,128)(2,1)S(1)} collective-permute-done((bf16[1,4,5,32,256]{4,3,1,2,0:T(8,128)(2,1)S(1)}, bf16[1,4,5,32,256]{4,3,1,2,0:T(8,128)(2,1)S(1)}, u32[]{:S(2)}, u32[]{:S(2)}) %collective-permute-start.2) | collective-permute-done | bytes 327712 | tf_op jit(solution)/shard_map/ppermute | solution.py:44
  80.1 0.9 maximum_select_fusion
  81.0 1.1 rev.22
  82.1 2.0 %select_select_fusion.1 = bf16[1,2,4,5,32,256]{5,4,2,1,3,0:T(8,128)(2,1)} fusion(bf16[1,2,4,5,32,256]{5,4,2,1,3,0:T(8,128)(2,1)S(1)} %bitcast.123, bf16[1,2,4,5,32,256]{5,4,2,1,3,0:T(8,128)(2,1)S(1)} %bitcast.119, pred[]{:T(512)S(6)} %eq.40, pred[]{:T(512)S(6)} %eq.39, bf16[1,1,4,5,32,256]{5,4,2,1,3,0:T(8,128)(2,1)} %bitcast.135, ...), kind=kLoop, calls=%fused_computation.45 | loop fusion | flops 983040 | bytes 2621442 | tf_op jit(solution)/shard_map/jit(_where)/select_n | solution.py:32
  84.2 2.0 %rev.23 = bf16[1,2,4,5,32,256]{5,4,2,1,3,0:T(8,128)(2,1)} reverse(bf16[1,2,4,5,32,256]{5,4,2,1,3,0:T(8,128)(2,1)} %select_select_fusion.1), dimensions={1} | reverse | bytes 1310720 | tf_op jit(solution)/shard_map/rev | solution.py:31
  88.2 1.4 fusion.22
  89.7 1.4 fusion.19
  93.4 49.0 %all_to_all.19 = bf16[64,8,512]{2,1,0:T(8,128)(2,1)S(1)} all-to-all(bf16[64,8,512]{2,1,0:T(8,128)(2,1)S(1)} %maximum_maximum_fusion), channel_id=1, replica_groups=mesh['gx'=64,'gz'=8] {'gx'}, dimensions={0} | all-to-all | bytes 1048576 | tf_op jit(solution)/shard_map/all_to_all | solution.py:127
  144.3 0.9 slice_bitcast_fusion.3
  146.0 2.1 %fusion.13 = bf16[3,8,32,256]{3,2,1,0:T(8,128)(2,1)} fusion(f32[3,8,32,256]{3,2,1,0:T(8,128)S(1)} %reshape.251, bf16[3,8,32,256]{3,2,1,0:T(8,128)(2,1)S(1)} %copy-done.3, f32[3,8,32,256]{3,2,1,0:T(8,128)S(1)} %copy-done.8, bf16[8,5,32,256]{3,2,0,1:T(8,128)(2,1)S(1)} %copy-done.12, f32[8,32,256]{2,1,0:T(8,128)} %get-tuple-element.23, f32[256]{0:T(256)S(1)} %copy-done.19, ...), kind=kOutput, calls=%fused_computation.21 | convolution fusion | flops 102629376 | bytes 3146752 | tf_op jit(solution)/shard_map/kxzj,ij->kxzi/dot_general | solution.py:65
  (114 shorter events, 17.2 us)
Async XLA Ops:
  0.6 72.0 %copy-start = (bf16[256,256]{1,0:T(8,128)(2,1)S(1)}, bf16[256,256]{1,0:T(8,128)(2,1)}, u32[]{:S(2)}) copy-start(bf16[256,256]{1,0:T(8,128)(2,1)} %param.13) | copy-start | bytes 393220
  2.3 9.6 %copy-start.3 = (bf16[3,8,32,256]{3,2,1,0:T(8,128)(2,1)S(1)}, bf16[3,8,32,256]{3,2,1,0:T(8,128)(2,1)}, u32[]{:S(2)}) copy-start(bf16[3,8,32,256]{3,2,1,0:T(8,128)(2,1)} %param.7) | copy-start | bytes 1179652
  4.3 7.7 %copy-start.13 = (bf16[8,32,256]{2,1,0:T(8,128)(2,1)S(1)}, bf16[8,32,256]{2,1,0:T(8,128)(2,1)}, u32[]{:S(2)}) copy-start(bf16[8,32,256]{2,1,0:T(8,128)(2,1)} %param.8) | copy-start | bytes 393220
  4.3 7.8 %copy-start.2 = (bf16[256,256]{1,0:T(8,128)(2,1)S(1)}, bf16[256,256]{1,0:T(8,128)(2,1)}, u32[]{:S(2)}) copy-start(bf16[256,256]{1,0:T(8,128)(2,1)} %param.12) | copy-start | bytes 393220
  4.3 17.8 %all-to-all-start.1 = ((bf16[5,8,32,256]{3,2,0,1:T(8,128)(2,1)}), bf16[5,8,32,256]{3,2,0,1:T(8,128)(2,1)S(1)}, u32[]{:S(2)}, u32[]{:S(2)}) async-start(bf16[5,8,32,256]{3,2,0,1:T(8,128)(2,1)} %pad_maximum_fusion), calls=%async_computation.1 | async-start | bytes 1310720 | tf_op jit(solution)/shard_map/all_to_all | solution.py:104
  14.5 2.2 %copy-start.1 = (bf16[512,512]{1,0:T(8,128)(2,1)S(1)}, bf16[512,512]{1,0:T(8,128)(2,1)}, u32[]{:S(2)}) copy-start(bf16[512,512]{1,0:T(8,128)(2,1)} %param.11) | copy-start | bytes 1572868
  15.2 2.2 %copy-start.17 = (f32[256,2]{1,0:T(8,128)S(1)}, f32[256,2]{1,0:T(8,128)}, u32[]{:S(2)}) copy-start(f32[256,2]{1,0:T(8,128)} %get-tuple-element.28) | copy-start | bytes 6148
  22.1 65.1 %all-to-all-start = ((bf16[64,8,512]{2,1,0:T(8,128)(2,1)}), bf16[64,8,512]{2,1,0:T(8,128)(2,1)}, u32[]{:S(2)}, u32[]{:S(2)}) async-start(bf16[64,8,512]{2,1,0:T(8,128)(2,1)} %bitcast.2), calls=%async_computation | async-start | bytes 1048576 | tf_op jit(solution)/shard_map/all_to_all | solution.py:84
  43.2 4.6 %copy-start.15 = (f32[512,2]{1,0:T(8,128)S(1)}, f32[512,2]{1,0:T(8,128)}, u32[]{:S(2)}) copy-start(f32[512,2]{1,0:T(8,128)} %get-tuple-element.16) | copy-start | bytes 12292
  43.3 4.5 %copy-start.6 = (f32[512,511]{1,0:T(8,128)S(1)}, f32[512,511]{1,0:T(8,128)}, u32[]{:S(2)}) copy-start(f32[512,511]{1,0:T(8,128)} %get-tuple-element.17) | copy-start | bytes 3139588
  43.3 4.5 %copy-start.7 = (f32[512,511]{1,0:T(8,128)S(1)}, f32[512,511]{1,0:T(8,128)}, u32[]{:S(2)}) copy-start(f32[512,511]{1,0:T(8,128)} %get-tuple-element.18) | copy-start | bytes 3139588
  43.4 4.5 %copy-start.4 = (f32[512,510]{1,0:T(8,128)S(1)}, f32[512,510]{1,0:T(8,128)}, u32[]{:S(2)}) copy-start(f32[512,510]{1,0:T(8,128)} %get-tuple-element.13) | copy-start | bytes 3133444
  43.4 4.5 %copy-start.5 = (f32[512,510]{1,0:T(8,128)S(1)}, f32[512,510]{1,0:T(8,128)}, u32[]{:S(2)}) copy-start(f32[512,510]{1,0:T(8,128)} %get-tuple-element.14) | copy-start | bytes 3133444
  43.5 14.9 %collective-permute-start = (bf16[4,1,5,32,256]{4,3,0,2,1:T(8,128)(2,1)S(1)}, bf16[4,1,5,32,256]{4,3,0,2,1:T(8,128)(2,1)S(1)}, u32[]{:S(2)}, u32[]{:S(2)}) collective-permute-start(bf16[4,1,5,32,256]{4,3,0,2,1:T(8,128)(2,1)S(1)} %get-tuple-element.10), channel_id=1, source_target_pairs={{0,1},{1,0},{2,3},{3,2},{4,5},{5,4},{6,7},{7,6},{8,9},{9,8},{10,11... | collective-permute-start | bytes 983048 | tf_op jit(solution)/shard_map/ppermute | solution.py:44
  58.5 10.0 %collective-permute-start.1 = (bf16[2,2,5,32,256]{4,3,1,2,0:T(8,128)(2,1)S(1)}, bf16[2,2,5,32,256]{4,3,1,2,0:T(8,128)(2,1)S(1)}, u32[]{:S(2)}, u32[]{:S(2)}) collective-permute-start(bf16[2,2,5,32,256]{4,3,1,2,0:T(8,128)(2,1)S(1)} %bitcast.151), channel_id=1, source_target_pairs={{0,2},{1,3},{2,0},{3,1},{4,6},{5,7},{6,4},{7,5},{8,10},{9,11},{10,... | collective-permute-start | bytes 983048 | tf_op jit(solution)/shard_map/ppermute | solution.py:44
  68.5 4.1 %copy-start.16 = (f32[8,32,256]{2,1,0:T(8,128)S(1)}, f32[8,32,256]{2,1,0:T(8,128)}, u32[]{:S(2)}) copy-start(f32[8,32,256]{2,1,0:T(8,128)} %convert_element_type.192) | copy-start | bytes 786436
  68.6 4.1 %copy-start.19 = (f32[256]{0:T(256)S(1)}, f32[256]{0:T(256)}, u32[]{:S(2)}) copy-start(f32[256]{0:T(256)} %param.10) | copy-start | bytes 3076
  68.7 10.7 %copy-start.9 = (bf16[1,1,4,5,32,256]{5,4,2,1,3,0:T(8,128)(2,1)}, bf16[1,1,4,5,32,256]{5,4,2,1,3,0:T(8,128)(2,1)S(1)}, u32[]{:S(2)}) copy-start(bf16[1,1,4,5,32,256]{5,4,2,1,3,0:T(8,128)(2,1)S(1)} %get-tuple-element.5) | copy-start | bytes 983044
  68.7 10.6 %collective-permute-start.2 = (bf16[1,4,5,32,256]{4,3,1,2,0:T(8,128)(2,1)S(1)}, bf16[1,4,5,32,256]{4,3,1,2,0:T(8,128)(2,1)S(1)}, u32[]{:S(2)}, u32[]{:S(2)}) collective-permute-start(bf16[1,4,5,32,256]{4,3,1,2,0:T(8,128)(2,1)S(1)} %get-tuple-element.6), channel_id=1, source_target_pairs={{0,4},{1,5},{2,6},{3,7},{4,0},{5,1},{6,2},{7,3},{8,12},{9,13},{10,... | collective-permute-start | bytes 983048 | tf_op jit(solution)/shard_map/ppermute | solution.py:44
  86.2 0.9 copy-start.11
  92.1 0.8 copy-start.18
  142.4 0.8 copy-start.14
  143.6 2.3 %copy-start.8 = (f32[3,8,32,256]{3,2,1,0:T(8,128)S(1)}, f32[3,8,32,256]{3,2,1,0:T(8,128)}, u32[]{:S(2)}) copy-start(f32[3,8,32,256]{3,2,1,0:T(8,128)} %get-tuple-element.36) | copy-start | bytes 2359300
  143.6 2.3 %copy-start.12 = (bf16[8,5,32,256]{3,2,0,1:T(8,128)(2,1)S(1)}, bf16[8,5,32,256]{3,2,0,1:T(8,128)(2,1)}, u32[]{:S(2)}) copy-start(bf16[8,5,32,256]{3,2,0,1:T(8,128)(2,1)} %copy-done.11) | copy-start | bytes 1966084
  (3 other events, 2.2 us)

commit v9 on v7

--- a/solution.py
+++ b/solution.py
@@ -8,6 +8,13 @@
 time_step = 0.25
 f32 = jnp.float32
 bf16 = jnp.bfloat16
+
+
+def folded(operator):
+    wide = operator.astype(f32)
+    shifted = lambda step: jnp.roll(wide, step, 1)
+    merged = near_coef * (shifted(1) - shifted(-1)) + far_coef * (shifted(2) - shifted(-2))
+    return split_wide(merged)
 
 
 def stencil(source, axis):
@@ -56,8 +63,8 @@
 
 
 def row_derivative(pencil, operator):
-    right_side = stencil(pencil, 0)
-    return jnp.dot(operator, right_side, preferred_element_type=f32).astype(bf16)
+    product = sum(jnp.dot(part, pencil, preferred_element_type=f32) for part in operator)
+    return product.astype(bf16)
 
 
 def wall_derivative(source, wall_operator, metric):
@@ -65,12 +72,13 @@
     return product * metric
 
 
-def on_device(adjoint, strain, correction, metric, stream_inverse, span_inverse, wall_operator):
+def section(adjoint, strain, correction, metric, stream_inverse, span_inverse, wall_operator):
     comps, nxl, nzl, ny = adjoint.shape
     gxn = lax.axis_size("gx")
     lanes = nzl * ny // gxn
     yparts = ny // lanes
     nx = nxl * gxn
+    stream_inverse = folded(stream_inverse)
     strain_wide = strain.astype(f32)
     viscosity = (correction[None] * strain_wide).astype(bf16)
     viscous = viscosity.astype(f32)
@@ -78,7 +86,8 @@
     xs = jnp.concatenate([adjoint, strain[None]], axis=0)
     xs = xs.reshape(comps + 1, nxl, nzl, yparts, lanes).transpose(2, 3, 1, 0, 4)
     xs = xs.reshape(gxn, nxl, (comps + 1) * lanes)
-    xt = lax.all_to_all(xs, "gx", 0, 0, tiled=True).reshape(nx, (comps + 1) * lanes)
+    xt = lax.all_to_all(xs, "gx", 0, 0, tiled=True)
+    xt = xt.reshape(nx, (comps + 1) * lanes)
     stream_strain = xt[:, comps * lanes:].astype(f32)
     me = lax.axis_index("gx")
     z_at, y_at = me // yparts, me % yparts
@@ -139,5 +148,5 @@
     in_specs = (P(None, "gx", "gz", None), P("gx", "gz", None), P("gz", None), P(), P(), P(), P())
     out_specs = (P(None, "gx", "gz", None), P("gz", "gx"))
     return jax.shard_map(
-        on_device, mesh=mesh, in_specs=in_specs, out_specs=out_specs, check_vma=False
+        section, mesh=mesh, in_specs=in_specs, out_specs=out_specs, check_vma=False
     )

time: 144 us -> 149 us (1.035)
  blocking collectives: 44.8 us -> 49 us
  waiting for transfers between devices: 25.8 us -> 23.1 us
  starting transfers between devices: 35.8 us -> 37.8 us
    all_to_all x2, waiting for transfers between devices: 12.2 us -> 2.74 us  [the longest x1 2.73 us: section(): zt = lax.all_to_all(zs, 'gz', 1, 2, tiled=True)[:, 0]]
    ppermute x3, waiting for transfers between devices: 13.5 us -> 20.4 us  [butterfly(): moved = lax.ppermute(split[:, 1], 'gz', pairs)]
    all_to_all x1, blocking collectives: 44.8 us -> 49 us  [section(): back = lax.all_to_all(back, 'gx', 0, 0, tiled=True)]
    slice x8 -> x4, local copies, waits for them, and re-layouts: 2.85 us -> 0.27 us  [stencil(): near_diff = jnp.roll(widened, -1, axis) - jnp.roll(widened, 1, axis)]
    slice x4 -> x7, local copies, waits for them, and re-layouts: 2.01 us -> 4.54 us  [the longest x4 3.57 us: folded(): shifted = lambda step: jnp.roll(wide, step, 1)]
    ppermute x3, starting transfers between devices: 8.36 us -> 10.5 us  [butterfly(): moved = lax.ppermute(split[:, 1], 'gz', pairs)]
    dot_general x2 -> x4, matrix products: 3.09 us -> 3.74 us  [row_derivative(): jnp.dot(part, pencil, preferred_element_type=f32)]
    unnamed x30 -> x43, local copies, waits for them, and re-layouts: 2.52 us -> 2.99 us
  transfers between devices with their start and end apart: 5 -> 5, of which waited for: 4 -> 4; matrix products, arithmetic and copies ran while one was open for 9% -> 13% of each run, Pallas kernels for 0% -> 0%
where the time goes in v9:
time: 149 us; the launch traced here: 148 us
  blocking collectives  49 us (33%)
  starting transfers between devices  37.8 us (25%)
  waiting for transfers between devices  23.1 us (16%)
  local copies, waits for them, and re-layouts  17.4 us (12%)
  other arithmetic  10.8 us (7%)
  matrix products  8.63 us (6%)
    all_to_all x1, blocking collectives, section(): back = lax.all_to_all(back, 'gx', 0, 0, tiled=True)  49 us
    ppermute x3, waiting for transfers between devices, butterfly(): moved = lax.ppermute(split[:, 1], 'gz', pairs)  20.4 us
    all_to_all x1, starting transfers between devices, section(): xt = lax.all_to_all(xs, 'gx', 0, 0, tiled=True)  19.7 us
    ppermute x3, starting transfers between devices, butterfly(): moved = lax.ppermute(split[:, 1], 'gz', pairs)  10.5 us
    all_to_all x1, starting transfers between devices, section(): zt = lax.all_to_all(zs, 'gz', 1, 2, tiled=True)[:, 0]  7.6 us
    dot_general x2, matrix products, wall_derivative(): jnp.einsum('kxzj,ij->kxzi', source, wall_operator, preferred_element_type...  3.95 us
    dot_general x4, matrix products, row_derivative(): jnp.dot(part, pencil, preferred_element_type=f32)  3.74 us
    slice x4, local copies, waits for them, and re-layouts, folded(): shifted = lambda step: jnp.roll(wide, step, 1)  3.57 us
  transfers between devices with their start and end apart: 5, of which 4 were waited for; matrix products, arithmetic and copies ran while one was open for 13% of the time, Pallas kernels for 0%

profile of v9, /device:TPU:1, one launch (start us, length us, event | category | flops | bytes accessed | tf_op | source)
XLA Modules:
  0.0 148.0 jit_solution(17093696573845704923)
XLA Ops:
  0.6 1.7 %fusion.45 = (f32[8,32,256]{2,1,0:T(8,128)}, bf16[1,8,32,256]{3,2,0,1:T(8,128)(2,1)S(1)}) fusion(bf16[8,32,256]{2,1,0:T(8,128)(2,1)} %param.8, f32[32,256]{1,0:T(8,128)} %param.9), kind=kLoop, calls=%fused_computation.90 | loop fusion | flops 262144 | bytes 557056 | tf_op jit(solution)/shard_map/convert_element_type | solution.py:84
  2.3 2.0 %pad_maximum_fusion = bf16[5,8,32,256]{3,2,0,1:T(8,128)(2,1)} fusion(bf16[1,8,32,256]{3,2,0,1:T(8,128)(2,1)} %bitcast.140, bf16[1,8,32,256]{3,2,0,1:T(8,128)(2,1)S(1)} %get-tuple-element.42, bf16[3,8,32,256]{3,2,1,0:T(8,128)(2,1)} %param.7), kind=kLoop, calls=%fused_computation.46 | loop fusion | flops 1966080 | bytes 1310720 | tf_op jit(solution)/shard_map/concatenate | solution.py:109
  4.3 7.6 %all-to-all-start.1 = ((bf16[5,8,32,256]{3,2,0,1:T(8,128)(2,1)}), bf16[5,8,32,256]{3,2,0,1:T(8,128)(2,1)S(1)}, u32[]{:S(2)}, u32[]{:S(2)}) async-start(bf16[5,8,32,256]{3,2,0,1:T(8,128)(2,1)} %pad_maximum_fusion), calls=%async_computation.1 | async-start | bytes 1310720 | tf_op jit(solution)/shard_map/all_to_all | solution.py:110
  13.6 1.4 copy.37
  15.2 1.7 %fusion.67 = (f32[512,510]{1,0:T(8,128)}, f32[512,510]{1,0:T(8,128)}) fusion(bf16[512,512]{1,0:T(8,128)(2,1)S(1)} %copy-done.1), kind=kLoop, calls=%fused_computation.126 | loop fusion | bytes 4177920 | tf_op jit(solution)/shard_map/jit(_roll_static)/slice | solution.py:15
  16.9 1.7 %fusion.69 = (f32[512,511]{1,0:T(8,128)}, f32[512,511]{1,0:T(8,128)}) fusion(bf16[512,512]{1,0:T(8,128)(2,1)S(1)} %copy-done.1), kind=kLoop, calls=%fused_computation.128 | loop fusion | bytes 4186112 | tf_op jit(solution)/shard_map/jit(_roll_static)/slice | solution.py:15
  18.5 2.7 %all-to-all-done.1 = bf16[5,8,32,256]{3,2,0,1:T(8,128)(2,1)S(1)} async-done(((bf16[5,8,32,256]{3,2,0,1:T(8,128)(2,1)}), bf16[5,8,32,256]{3,2,0,1:T(8,128)(2,1)S(1)}, u32[]{:S(2)}, u32[]{:S(2)}) %all-to-all-start.1) | async-done | bytes 655392 | tf_op jit(solution)/shard_map/all_to_all | solution.py:110
  21.3 19.7 %all-to-all-start = ((bf16[64,8,512]{2,1,0:T(8,128)(2,1)}), bf16[64,8,512]{2,1,0:T(8,128)(2,1)}, u32[]{:S(2)}, u32[]{:S(2)}) async-start(bf16[64,8,512]{2,1,0:T(8,128)(2,1)} %bitcast.2), calls=%async_computation | async-start | bytes 1048576 | tf_op jit(solution)/shard_map/all_to_all | solution.py:89
  43.4 4.2 %collective-permute-start = (bf16[4,1,5,32,256]{4,3,0,2,1:T(8,128)(2,1)S(1)}, bf16[4,1,5,32,256]{4,3,0,2,1:T(8,128)(2,1)S(1)}, u32[]{:S(2)}, u32[]{:S(2)}) collective-permute-start(bf16[4,1,5,32,256]{4,3,0,2,1:T(8,128)(2,1)S(1)} %get-tuple-element.28), channel_id=1, source_target_pairs={{0,1},{1,0},{2,3},{3,2},{4,5},{5,4},{6,7},{7,6},{8,9},{9,8},{10,11... | collective-permute-start | bytes 983048 | tf_op jit(solution)/shard_map/ppermute | solution.py:50
  48.5 9.8 %collective-permute-done = bf16[4,1,5,32,256]{4,3,0,2,1:T(8,128)(2,1)S(1)} collective-permute-done((bf16[4,1,5,32,256]{4,3,0,2,1:T(8,128)(2,1)S(1)}, bf16[4,1,5,32,256]{4,3,0,2,1:T(8,128)(2,1)S(1)}, u32[]{:S(2)}, u32[]{:S(2)}) %collective-permute-start) | collective-permute-done | bytes 327712 | tf_op jit(solution)/shard_map/ppermute | solution.py:50
  58.4 2.4 %collective-permute-start.1 = (bf16[2,2,5,32,256]{4,3,1,2,0:T(8,128)(2,1)S(1)}, bf16[2,2,5,32,256]{4,3,1,2,0:T(8,128)(2,1)S(1)}, u32[]{:S(2)}, u32[]{:S(2)}) collective-permute-start(bf16[2,2,5,32,256]{4,3,1,2,0:T(8,128)(2,1)S(1)} %bitcast.148), channel_id=1, source_target_pairs={{0,2},{1,3},{2,0},{3,1},{4,6},{5,7},{6,4},{7,5},{8,10},{9,11},{10,... | collective-permute-start | bytes 983048 | tf_op jit(solution)/shard_map/ppermute | solution.py:50
  61.9 6.5 %collective-permute-done.1 = bf16[2,2,5,32,256]{4,3,1,2,0:T(8,128)(2,1)S(1)} collective-permute-done((bf16[2,2,5,32,256]{4,3,1,2,0:T(8,128)(2,1)S(1)}, bf16[2,2,5,32,256]{4,3,1,2,0:T(8,128)(2,1)S(1)}, u32[]{:S(2)}, u32[]{:S(2)}) %collective-permute-start.1) | collective-permute-done | bytes 327712 | tf_op jit(solution)/shard_map/ppermute | solution.py:50
  68.6 3.9 %collective-permute-start.2 = (bf16[1,4,5,32,256]{4,3,1,2,0:T(8,128)(2,1)S(1)}, bf16[1,4,5,32,256]{4,3,1,2,0:T(8,128)(2,1)S(1)}, u32[]{:S(2)}, u32[]{:S(2)}) collective-permute-start(bf16[1,4,5,32,256]{4,3,1,2,0:T(8,128)(2,1)S(1)} %get-tuple-element.24), channel_id=1, source_target_pairs={{0,4},{1,5},{2,6},{3,7},{4,0},{5,1},{6,2},{7,3},{8,12},{9,13},{10,... | collective-permute-start | bytes 983048 | tf_op jit(solution)/shard_map/ppermute | solution.py:50
  73.3 1.8 %multiply_reduce_fusion = (f32[32,256]{1,0:T(8,128)}, f32[3,8,32,256]{3,2,1,0:T(8,128)}) fusion(f32[8,32,256]{2,1,0:T(8,128)S(1)} %copy-done.14, f32[256]{0:T(256)S(1)} %copy-done.17, bf16[3,8,32,256]{3,2,1,0:T(8,128)(2,1)S(1)} %copy-done.2, bf16[256,256]{1,0:T(8,128)(2,1)S(1)} %copy-done.15), kind=kOutput, calls=%fused_computation.43 | convolution fusion | flops 101834752 | bytes 1606656 | tf_op jit(solution)/shard_map/kxzj,ij->kxzi/dot_general | solution.py:71
  75.1 4.1 %collective-permute-done.2 = bf16[1,4,5,32,256]{4,3,1,2,0:T(8,128)(2,1)S(1)} collective-permute-done((bf16[1,4,5,32,256]{4,3,1,2,0:T(8,128)(2,1)S(1)}, bf16[1,4,5,32,256]{4,3,1,2,0:T(8,128)(2,1)S(1)}, u32[]{:S(2)}, u32[]{:S(2)}) %collective-permute-start.2) | collective-permute-done | bytes 327712 | tf_op jit(solution)/shard_map/ppermute | solution.py:50
  80.0 0.9 maximum_select_fusion
  81.0 1.1 rev.22
  82.1 2.0 %select_select_fusion.1 = bf16[1,2,4,5,32,256]{5,4,2,1,3,0:T(8,128)(2,1)} fusion(bf16[1,2,4,5,32,256]{5,4,2,1,3,0:T(8,128)(2,1)S(1)} %bitcast.122, bf16[1,2,4,5,32,256]{5,4,2,1,3,0:T(8,128)(2,1)S(1)} %bitcast.118, pred[]{:T(512)S(6)} %eq.40, pred[]{:T(512)S(6)} %eq.39, bf16[1,1,4,5,32,256]{5,4,2,1,3,0:T(8,128)(2,1)} %bitcast.132, ...), kind=kLoop, calls=%fused_computation.55 | loop fusion | flops 983040 | bytes 2621442 | tf_op jit(solution)/shard_map/jit(_where)/select_n | solution.py:38
  84.1 2.0 %rev.23 = bf16[1,2,4,5,32,256]{5,4,2,1,3,0:T(8,128)(2,1)} reverse(bf16[1,2,4,5,32,256]{5,4,2,1,3,0:T(8,128)(2,1)} %select_select_fusion.1), dimensions={1} | reverse | bytes 1310720 | tf_op jit(solution)/shard_map/rev | solution.py:37
  88.2 1.4 fusion.31
  89.7 1.4 fusion.25
  93.4 49.0 %all_to_all.19 = bf16[64,8,512]{2,1,0:T(8,128)(2,1)S(1)} all-to-all(bf16[64,8,512]{2,1,0:T(8,128)(2,1)S(1)} %maximum_maximum_fusion), channel_id=1, replica_groups=mesh['gx'=64,'gz'=8] {'gx'}, dimensions={0} | all-to-all | bytes 1048576 | tf_op jit(solution)/shard_map/all_to_all | solution.py:133
  144.2 0.9 slice_bitcast_fusion.3
  145.9 2.1 %fusion.9 = bf16[3,8,32,256]{3,2,1,0:T(8,128)(2,1)} fusion(f32[3,8,32,256]{3,2,1,0:T(8,128)S(1)} %reshape.254, bf16[3,8,32,256]{3,2,1,0:T(8,128)(2,1)S(1)} %copy-done.2, f32[3,8,32,256]{3,2,1,0:T(8,128)S(1)} %copy-done.7, bf16[8,5,32,256]{3,2,0,1:T(8,128)(2,1)S(1)} %copy-done.11, f32[8,32,256]{2,1,0:T(8,128)} %get-tuple-element.41, f32[256]{0:T(256)S(1)} %copy-done.17, ...), kind=kOutput, calls=%fused_computation.15 | convolution fusion | flops 102629376 | bytes 3146752 | tf_op jit(solution)/shard_map/kxzj,ij->kxzi/dot_general | solution.py:71
  (108 shorter events, 14.6 us)
Async XLA Ops:
  0.6 40.8 %copy-start = (bf16[256,256]{1,0:T(8,128)(2,1)S(1)}, bf16[256,256]{1,0:T(8,128)(2,1)}, u32[]{:S(2)}) copy-start(bf16[256,256]{1,0:T(8,128)(2,1)} %param.12) | copy-start | bytes 393220
  2.3 9.6 %copy-start.2 = (bf16[3,8,32,256]{3,2,1,0:T(8,128)(2,1)S(1)}, bf16[3,8,32,256]{3,2,1,0:T(8,128)(2,1)}, u32[]{:S(2)}) copy-start(bf16[3,8,32,256]{3,2,1,0:T(8,128)(2,1)} %param.7) | copy-start | bytes 1179652
  4.3 7.7 %copy-start.12 = (bf16[8,32,256]{2,1,0:T(8,128)(2,1)S(1)}, bf16[8,32,256]{2,1,0:T(8,128)(2,1)}, u32[]{:S(2)}) copy-start(bf16[8,32,256]{2,1,0:T(8,128)(2,1)} %param.8) | copy-start | bytes 393220
  4.3 17.0 %all-to-all-start.1 = ((bf16[5,8,32,256]{3,2,0,1:T(8,128)(2,1)}), bf16[5,8,32,256]{3,2,0,1:T(8,128)(2,1)S(1)}, u32[]{:S(2)}, u32[]{:S(2)}) async-start(bf16[5,8,32,256]{3,2,0,1:T(8,128)(2,1)} %pad_maximum_fusion), calls=%async_computation.1 | async-start | bytes 1310720 | tf_op jit(solution)/shard_map/all_to_all | solution.py:110
  12.8 2.2 %copy-start.1 = (bf16[512,512]{1,0:T(8,128)(2,1)S(1)}, bf16[512,512]{1,0:T(8,128)(2,1)}, u32[]{:S(2)}) copy-start(bf16[512,512]{1,0:T(8,128)(2,1)} %param.11) | copy-start | bytes 1572868
  21.3 65.9 %all-to-all-start = ((bf16[64,8,512]{2,1,0:T(8,128)(2,1)}), bf16[64,8,512]{2,1,0:T(8,128)(2,1)}, u32[]{:S(2)}, u32[]{:S(2)}) async-start(bf16[64,8,512]{2,1,0:T(8,128)(2,1)} %bitcast.2), calls=%async_computation | async-start | bytes 1048576 | tf_op jit(solution)/shard_map/all_to_all | solution.py:89
  43.2 4.5 %copy-start.5 = (f32[512,511]{1,0:T(8,128)S(1)}, f32[512,511]{1,0:T(8,128)}, u32[]{:S(2)}) copy-start(f32[512,511]{1,0:T(8,128)} %get-tuple-element.35) | copy-start | bytes 3139588
  43.2 4.5 %copy-start.6 = (f32[512,511]{1,0:T(8,128)S(1)}, f32[512,511]{1,0:T(8,128)}, u32[]{:S(2)}) copy-start(f32[512,511]{1,0:T(8,128)} %get-tuple-element.36) | copy-start | bytes 3139588
  43.3 4.4 %copy-start.3 = (f32[512,510]{1,0:T(8,128)S(1)}, f32[512,510]{1,0:T(8,128)}, u32[]{:S(2)}) copy-start(f32[512,510]{1,0:T(8,128)} %get-tuple-element.31) | copy-start | bytes 3133444
  43.3 4.4 %copy-start.4 = (f32[512,510]{1,0:T(8,128)S(1)}, f32[512,510]{1,0:T(8,128)}, u32[]{:S(2)}) copy-start(f32[512,510]{1,0:T(8,128)} %get-tuple-element.32) | copy-start | bytes 3133444
  43.4 14.9 %collective-permute-start = (bf16[4,1,5,32,256]{4,3,0,2,1:T(8,128)(2,1)S(1)}, bf16[4,1,5,32,256]{4,3,0,2,1:T(8,128)(2,1)S(1)}, u32[]{:S(2)}, u32[]{:S(2)}) collective-permute-start(bf16[4,1,5,32,256]{4,3,0,2,1:T(8,128)(2,1)S(1)} %get-tuple-element.28), channel_id=1, source_target_pairs={{0,1},{1,0},{2,3},{3,2},{4,5},{5,4},{6,7},{7,6},{8,9},{9,8},{10,11... | collective-permute-start | bytes 983048 | tf_op jit(solution)/shard_map/ppermute | solution.py:50
  58.4 10.0 %collective-permute-start.1 = (bf16[2,2,5,32,256]{4,3,1,2,0:T(8,128)(2,1)S(1)}, bf16[2,2,5,32,256]{4,3,1,2,0:T(8,128)(2,1)S(1)}, u32[]{:S(2)}, u32[]{:S(2)}) collective-permute-start(bf16[2,2,5,32,256]{4,3,1,2,0:T(8,128)(2,1)S(1)} %bitcast.148), channel_id=1, source_target_pairs={{0,2},{1,3},{2,0},{3,1},{4,6},{5,7},{6,4},{7,5},{8,10},{9,11},{10,... | collective-permute-start | bytes 983048 | tf_op jit(solution)/shard_map/ppermute | solution.py:50
  68.5 4.8 %copy-start.14 = (f32[8,32,256]{2,1,0:T(8,128)S(1)}, f32[8,32,256]{2,1,0:T(8,128)}, u32[]{:S(2)}) copy-start(f32[8,32,256]{2,1,0:T(8,128)} %convert_element_type.198) | copy-start | bytes 786436
  68.5 4.8 %copy-start.15 = (bf16[256,256]{1,0:T(8,128)(2,1)S(1)}, bf16[256,256]{1,0:T(8,128)(2,1)}, u32[]{:S(2)}) copy-start(bf16[256,256]{1,0:T(8,128)(2,1)} %param.13) | copy-start | bytes 393220
  68.5 4.8 %copy-start.17 = (f32[256]{0:T(256)S(1)}, f32[256]{0:T(256)}, u32[]{:S(2)}) copy-start(f32[256]{0:T(256)} %param.10) | copy-start | bytes 3076
  68.6 10.7 %copy-start.8 = (bf16[1,1,4,5,32,256]{5,4,2,1,3,0:T(8,128)(2,1)}, bf16[1,1,4,5,32,256]{5,4,2,1,3,0:T(8,128)(2,1)S(1)}, u32[]{:S(2)}) copy-start(bf16[1,1,4,5,32,256]{5,4,2,1,3,0:T(8,128)(2,1)S(1)} %get-tuple-element.23) | copy-start | bytes 983044
  68.6 10.6 %collective-permute-start.2 = (bf16[1,4,5,32,256]{4,3,1,2,0:T(8,128)(2,1)S(1)}, bf16[1,4,5,32,256]{4,3,1,2,0:T(8,128)(2,1)S(1)}, u32[]{:S(2)}, u32[]{:S(2)}) collective-permute-start(bf16[1,4,5,32,256]{4,3,1,2,0:T(8,128)(2,1)S(1)} %get-tuple-element.24), channel_id=1, source_target_pairs={{0,4},{1,5},{2,6},{3,7},{4,0},{5,1},{6,2},{7,3},{8,12},{9,13},{10,... | collective-permute-start | bytes 983048 | tf_op jit(solution)/shard_map/ppermute | solution.py:50
  86.2 0.9 copy-start.10
  92.0 0.8 copy-start.16
  92.1 0.8 copy-start.18
  92.1 0.7 copy-start.19
  142.3 0.8 copy-start.13
  143.6 2.3 %copy-start.7 = (f32[3,8,32,256]{3,2,1,0:T(8,128)S(1)}, f32[3,8,32,256]{3,2,1,0:T(8,128)}, u32[]{:S(2)}) copy-start(f32[3,8,32,256]{3,2,1,0:T(8,128)} %get-tuple-element.46) | copy-start | bytes 2359300
  143.6 2.3 %copy-start.11 = (bf16[8,5,32,256]{3,2,0,1:T(8,128)(2,1)S(1)}, bf16[8,5,32,256]{3,2,0,1:T(8,128)(2,1)}, u32[]{:S(2)}) copy-start(bf16[8,5,32,256]{3,2,0,1:T(8,128)(2,1)} %copy-done.10) | copy-start | bytes 1966084
  (1 other events, 0.7 us)

commit v10 on v8

--- a/solution.py
+++ b/solution.py
@@ -26,12 +26,7 @@
 
 def xor_order(blocks, mine):
     size = blocks.shape[0]
-    bit = 1
-    while bit < size:
-        swapped = blocks.reshape(size // (2 * bit), 2, bit, *blocks.shape[1:])[:, ::-1]
-        blocks = jnp.where((mine // bit) % 2 == 1, swapped.reshape(blocks.shape), blocks)
-        bit *= 2
-    return blocks
+    return blocks[jnp.bitwise_xor(jnp.arange(size, dtype=jnp.int32), mine)]
 
 
 def butterfly(blocks, mine):
@@ -66,7 +61,7 @@
     return product * metric
 
 
-def on_device(adjoint, strain, correction, metric, stream_inverse, span_inverse, wall_operator):
+def section(adjoint, strain, correction, metric, stream_inverse, span_inverse, wall_operator):
     comps, nxl, nzl, ny = adjoint.shape
     gxn = lax.axis_size("gx")
     lanes = nzl * ny // gxn
@@ -81,7 +76,8 @@
     xs = jnp.concatenate([adjoint, strain[None]], axis=0)
     xs = xs.reshape(comps + 1, nxl, nzl, yparts, lanes).transpose(2, 3, 1, 0, 4)
     xs = xs.reshape(gxn, nxl, (comps + 1) * lanes)
-    xt = lax.all_to_all(xs, "gx", 0, 0, tiled=True).reshape(nx, (comps + 1) * lanes)
+    xt = lax.all_to_all(xs, "gx", 0, 0, tiled=True)
+    xt = xt.reshape(nx, (comps + 1) * lanes)
     stream_strain = xt[:, comps * lanes:].astype(f32)
     me = lax.axis_index("gx")
     z_at, y_at = me // yparts, me % yparts
@@ -124,6 +120,7 @@
     extra = jnp.zeros((gxn, nxl - 2, lanes), bf16)
     extra = jnp.concatenate([pieces[0][:, None], pieces[1][:, None], extra], axis=1)
     back = jnp.concatenate([stream_div.reshape(gxn, nxl, comps * lanes), extra], axis=2)
+    back, wall_div = lax.optimization_barrier((back, wall_div))
     back = lax.all_to_all(back, "gx", 0, 0, tiled=True)
     summed = jnp.sum(join_wide(back[:, :2, comps * lanes:].transpose(1, 0, 2)), axis=0)
     summed = summed.reshape(ny // gxn, nzl).T
@@ -142,5 +139,5 @@
     in_specs = (P(None, "gx", "gz", None), P("gx", "gz", None), P("gz", None), P(), P(), P(), P())
     out_specs = (P(None, "gx", "gz", None), P("gz", "gx"))
     return jax.shard_map(
-        on_device, mesh=mesh, in_specs=in_specs, out_specs=out_specs, check_vma=False
+        section, mesh=mesh, in_specs=in_specs, out_specs=out_specs, check_vma=False
     )

time: 149 us -> 151 us (1.013)
  matrix products: 8.89 us -> 6.58 us
  local copies, waits for them, and re-layouts: 19.6 us -> 21.9 us
  starting transfers between devices: 35.9 us -> 37.9 us
  blocking collectives: 49 us -> 47.3 us
  other arithmetic: 12.1 us -> 13.7 us
    ppermute x3, starting transfers between devices: 9.46 us -> 13.6 us  [butterfly(): moved = lax.ppermute(split[:, 1], 'gz', pairs)]
    select_n x6 -> x1, other arithmetic: 3.32 us -> 0.01 us  [xor_order(): return blocks[jnp.bitwise_xor(jnp.arange(size, dtype=jnp.int32), mine)]]
    rev x6 -> x0, local copies, waits for them, and re-layouts: 3.28 us -> none  [xor_order(): blocks.reshape(size // (2 * bit), 2, bit, *blocks.shape[1:])[:, ::-1]]
    dot_general x2, matrix products: 3.92 us -> 1.24 us  [wall_derivative(): jnp.einsum('kxzj,ij->kxzi', source, wall_operator, preferred_element_type...]
    all_to_all x2, starting transfers between devices: 26.4 us -> 24.3 us  [the longest x1 16.7 us: section(): xt = lax.all_to_all(xs, 'gx', 0, 0, tiled=True)]
    gather x0 -> x2, local copies, waits for them, and re-layouts: none -> 2.05 us  [xor_order(): return blocks[jnp.bitwise_xor(jnp.arange(size, dtype=jnp.int32), mine)]]
    transpose x3, local copies, waits for them, and re-layouts: 2.36 us -> 4.35 us  [the longest x1 2.46 us: section(): xs = xs.reshape(comps + 1, nxl, nzl, yparts, lanes).transpose(2, 3, 1, 0, 4)]
    transpose x1 -> x2, other arithmetic: 0.72 us -> 2.64 us  [the longest x1 2.56 us: section(): xs = xs.reshape(comps + 1, nxl, nzl, yparts, lanes).transpose(2, 3, 1, 0, 4)]
  transfers between devices with their start and end apart: 5 -> 5, of which waited for: 3 -> 3; matrix products, arithmetic and copies ran while one was open for 16% -> 17% of each run, Pallas kernels for 0% -> 0%
where the time goes in v10:
time: 151 us; the launch traced here: 149 us
  blocking collectives  47.3 us (31%)
  starting transfers between devices  37.9 us (25%)
  local copies, waits for them, and re-layouts  21.9 us (15%)
  waiting for transfers between devices  20.9 us (14%)
  other arithmetic  13.7 us (9%)
  matrix products  6.58 us (4%)
    all_to_all x1, blocking collectives, section(): back = lax.all_to_all(back, 'gx', 0, 0, tiled=True)  47.3 us
    ppermute x3, waiting for transfers between devices, butterfly(): moved = lax.ppermute(split[:, 1], 'gz', pairs)  20.9 us
    all_to_all x1, starting transfers between devices, section(): xt = lax.all_to_all(xs, 'gx', 0, 0, tiled=True)  16.7 us
    ppermute x3, starting transfers between devices, butterfly(): moved = lax.ppermute(split[:, 1], 'gz', pairs)  13.6 us
    all_to_all x1, starting transfers between devices, section(): zt = lax.all_to_all(zs, 'gz', 1, 2, tiled=True)[:, 0]  7.6 us
    slice x8, local copies, waits for them, and re-layouts, folded(): shifted = lambda step: jnp.roll(wide, step, 1)  6.43 us
    unnamed x54, local copies, waits for them, and re-layouts  3.56 us
    dot_general x4, matrix products, row_derivative(): jnp.dot(part, pencil, preferred_element_type=f32)  3.4 us
  transfers between devices with their start and end apart: 5, of which 3 were waited for; matrix products, arithmetic and copies ran while one was open for 17% of the time, Pallas kernels for 0%

profile of v10, /device:TPU:1, one launch (start us, length us, event | category | flops | bytes accessed | tf_op | source)
XLA Modules:
  0.0 149.4 jit_solution(15335676152088055659)
XLA Ops:
  0.6 1.7 %fusion.38 = (f32[8,32,256]{2,1,0:T(8,128)}, bf16[1,8,32,256]{3,2,0,1:T(8,128)(2,1)S(1)}) fusion(bf16[8,32,256]{2,1,0:T(8,128)(2,1)} %param.8, f32[32,256]{1,0:T(8,128)} %param.9), kind=kLoop, calls=%fused_computation.81 | loop fusion | flops 262144 | bytes 557056 | tf_op jit(solution)/shard_map/convert_element_type | solution.py:74
  2.3 2.0 %pad_maximum_fusion = bf16[5,8,32,256]{3,2,0,1:T(8,128)(2,1)} fusion(bf16[1,8,32,256]{3,2,0,1:T(8,128)(2,1)} %bitcast.114, bf16[1,8,32,256]{3,2,0,1:T(8,128)(2,1)S(1)} %get-tuple-element.27, bf16[3,8,32,256]{3,2,1,0:T(8,128)(2,1)} %param.7), kind=kLoop, calls=%fused_computation.37 | loop fusion | flops 1966080 | bytes 1310720 | tf_op jit(solution)/shard_map/concatenate | solution.py:99
  4.3 7.6 %all-to-all-start.1 = ((bf16[5,8,32,256]{3,2,0,1:T(8,128)(2,1)}), bf16[5,8,32,256]{3,2,0,1:T(8,128)(2,1)S(1)}, u32[]{:S(2)}, u32[]{:S(2)}) async-start(bf16[5,8,32,256]{3,2,0,1:T(8,128)(2,1)} %pad_maximum_fusion), calls=%async_computation.1 | async-start | bytes 1310720 | tf_op jit(solution)/shard_map/all_to_all | solution.py:100
  12.8 1.3 fusion.53
  18.9 2.6 %maximum_bitcast_fusion.1 = bf16[32,2,8,4,128]{4,1,0,2,3:T(2,128)(2,1)} fusion(bf16[1,8,32,2,128]{4,3,2,1,0:T(2,128)(2,1)S(1)} %concatenate.61, bf16[3,8,32,2,128]{4,3,2,1,0:T(2,128)(2,1)} %concatenate.60), kind=kLoop, calls=%fused_computation.43 | loop fusion | flops 262144 | bytes 1048576 | tf_op jit(solution)/shard_map/transpose | solution.py:77
  22.2 2.5 %copy.66 = bf16[32,2,8,4,128]{4,2,3,1,0:T(8,128)(2,1)} copy(bf16[32,2,8,4,128]{4,1,0,2,3:T(2,128)(2,1)} %maximum_bitcast_fusion.1) | data formatting | bytes 1048576 | tf_op jit(solution)/shard_map/transpose | solution.py:77
  24.7 1.5 %fusion.28 = f32[256,256]{1,0:T(8,128)S(1)} fusion(f32[256,255]{1,0:T(8,128)} %get-tuple-element.33, f32[256,1]{1,0:T(8,128)} %get-tuple-element.35, f32[256,1]{1,0:T(8,128)} %get-tuple-element.34, f32[256,255]{1,0:T(8,128)} %get-tuple-element.32, f32[256,254]{1,0:T(8,128)} %get-tuple-element.29, f32[256,2]{1,0:T(8,128)} %get-tuple-element.31, ...), kind=kLoop, calls=%fused_computation.68 | loop fusion | flops 589824 | bytes 1310720 | tf_op jit(solution)/shard_map/add | solution.py:16
  28.5 16.7 %all-to-all-start = ((bf16[64,8,512]{2,1,0:T(8,128)(2,1)}), bf16[64,8,512]{2,1,0:T(8,128)(2,1)S(1)}, u32[]{:S(2)}, u32[]{:S(2)}) async-start(bf16[64,8,512]{2,1,0:T(8,128)(2,1)} %bitcast.115), calls=%async_computation | async-start | bytes 1048576 | tf_op jit(solution)/shard_map/all_to_all | solution.py:79
  47.3 1.0 multiply_reduce_fusion.1
  50.6 5.9 %collective-permute-start = (bf16[4,1,5,32,256]{4,3,2,0,1:T(8,128)(2,1)S(1)}, bf16[4,1,5,32,256]{4,3,2,0,1:T(8,128)(2,1)S(1)}, u32[]{:S(2)}, u32[]{:S(2)}) collective-permute-start(bf16[4,1,5,32,256]{4,3,2,0,1:T(8,128)(2,1)S(1)} %get-tuple-element.13), channel_id=1, source_target_pairs={{0,1},{1,0},{2,3},{3,2},{4,5},{5,4},{6,7},{7,6},{8,9},{9,8},{10,11... | collective-permute-start | bytes 983048 | tf_op jit(solution)/shard_map/ppermute | solution.py:39
  57.0 9.9 %collective-permute-done = bf16[4,1,5,32,256]{4,3,2,0,1:T(8,128)(2,1)S(1)} collective-permute-done((bf16[4,1,5,32,256]{4,3,2,0,1:T(8,128)(2,1)S(1)}, bf16[4,1,5,32,256]{4,3,2,0,1:T(8,128)(2,1)S(1)}, u32[]{:S(2)}, u32[]{:S(2)}) %collective-permute-start) | collective-permute-done | bytes 327712 | tf_op jit(solution)/shard_map/ppermute | solution.py:39
  67.0 3.1 %collective-permute-start.1 = (bf16[2,2,5,32,256]{4,3,2,1,0:T(8,128)(2,1)S(1)}, bf16[2,2,5,32,256]{4,3,2,1,0:T(8,128)(2,1)S(1)}, u32[]{:S(2)}, u32[]{:S(2)}) collective-permute-start(bf16[2,2,5,32,256]{4,3,2,1,0:T(8,128)(2,1)S(1)} %bitcast.124), channel_id=1, source_target_pairs={{0,2},{1,3},{2,0},{3,1},{4,6},{5,7},{6,4},{7,5},{8,10},{9,11},{10,... | collective-permute-start | bytes 983048 | tf_op jit(solution)/shard_map/ppermute | solution.py:39
  70.6 0.9 multiply_reduce_fusion
  71.6 5.8 %collective-permute-done.1 = bf16[2,2,5,32,256]{4,3,2,1,0:T(8,128)(2,1)S(1)} collective-permute-done((bf16[2,2,5,32,256]{4,3,2,1,0:T(8,128)(2,1)S(1)}, bf16[2,2,5,32,256]{4,3,2,1,0:T(8,128)(2,1)S(1)}, u32[]{:S(2)}, u32[]{:S(2)}) %collective-permute-start.1) | collective-permute-done | bytes 327712 | tf_op jit(solution)/shard_map/ppermute | solution.py:39
  77.5 4.6 %collective-permute-start.2 = (bf16[1,4,5,32,256]{4,3,2,1,0:T(8,128)(2,1)S(1)}, bf16[1,4,5,32,256]{4,3,2,1,0:T(8,128)(2,1)S(1)}, u32[]{:S(2)}, u32[]{:S(2)}) collective-permute-start(bf16[1,4,5,32,256]{4,3,2,1,0:T(8,128)(2,1)S(1)} %get-tuple-element.9), channel_id=1, source_target_pairs={{0,4},{1,5},{2,6},{3,7},{4,0},{5,1},{6,2},{7,3},{8,12},{9,13},{10,... | collective-permute-start | bytes 983048 | tf_op jit(solution)/shard_map/ppermute | solution.py:39
  83.2 5.3 %collective-permute-done.2 = bf16[1,4,5,32,256]{4,3,2,1,0:T(8,128)(2,1)S(1)} collective-permute-done((bf16[1,4,5,32,256]{4,3,2,1,0:T(8,128)(2,1)S(1)}, bf16[1,4,5,32,256]{4,3,2,1,0:T(8,128)(2,1)S(1)}, u32[]{:S(2)}, u32[]{:S(2)}) %collective-permute-start.2) | collective-permute-done | bytes 327712 | tf_op jit(solution)/shard_map/ppermute | solution.py:39
  88.6 1.5 gather_fusion.1
  90.0 1.0 slice_bitcast_fusion.2
  92.5 1.3 fusion.17
  94.3 1.2 fusion.9
  95.5 1.3 reduce_sum.60
  97.6 47.3 %all_to_all.19 = bf16[64,8,512]{2,1,0:T(8,128)(2,1)S(1)} all-to-all(bf16[64,8,512]{2,1,0:T(8,128)(2,1)S(1)} %maximum_maximum_fusion), channel_id=1, replica_groups=mesh['gx'=64,'gz'=8] {'gx'}, dimensions={0} | all-to-all | bytes 1048576 | tf_op jit(solution)/shard_map/all_to_all | solution.py:124
  146.7 0.9 slice_bitcast_fusion.3
  148.4 1.0 fusion.16
  (113 shorter events, 20.4 us)
Async XLA Ops:
  0.6 70.0 %copy-start = (bf16[256,256]{1,0:T(8,128)(2,1)S(1)}, bf16[256,256]{1,0:T(8,128)(2,1)}, u32[]{:S(2)}) copy-start(bf16[256,256]{1,0:T(8,128)(2,1)} %param.13) | copy-start | bytes 393220
  2.3 9.6 %copy-start.3 = (bf16[3,8,32,256]{3,2,1,0:T(8,128)(2,1)S(1)}, bf16[3,8,32,256]{3,2,1,0:T(8,128)(2,1)}, u32[]{:S(2)}) copy-start(bf16[3,8,32,256]{3,2,1,0:T(8,128)(2,1)} %param.7) | copy-start | bytes 1179652
  4.3 8.5 %copy-start.6 = (bf16[8,32,256]{2,1,0:T(8,128)(2,1)S(1)}, bf16[8,32,256]{2,1,0:T(8,128)(2,1)}, u32[]{:S(2)}) copy-start(bf16[8,32,256]{2,1,0:T(8,128)(2,1)} %param.8) | copy-start | bytes 393220
  4.3 8.5 %copy-start.1 = (bf16[512,512]{1,0:T(8,128)(2,1)S(1)}, bf16[512,512]{1,0:T(8,128)(2,1)}, u32[]{:S(2)}) copy-start(bf16[512,512]{1,0:T(8,128)(2,1)} %param.11) | copy-start | bytes 1572868
  4.3 24.2 %all-to-all-start.1 = ((bf16[5,8,32,256]{3,2,0,1:T(8,128)(2,1)}), bf16[5,8,32,256]{3,2,0,1:T(8,128)(2,1)S(1)}, u32[]{:S(2)}, u32[]{:S(2)}) async-start(bf16[5,8,32,256]{3,2,0,1:T(8,128)(2,1)} %pad_maximum_fusion), calls=%async_computation.1 | async-start | bytes 1310720 | tf_op jit(solution)/shard_map/all_to_all | solution.py:100
  14.2 1.7 %copy-start.2 = (bf16[256,256]{1,0:T(8,128)(2,1)S(1)}, bf16[256,256]{1,0:T(8,128)(2,1)}, u32[]{:S(2)}) copy-start(bf16[256,256]{1,0:T(8,128)(2,1)} %param.12) | copy-start | bytes 393220
  18.9 5.8 %copy-start.19 = (f32[256,2]{1,0:T(8,128)S(1)}, f32[256,2]{1,0:T(8,128)}, u32[]{:S(2)}) copy-start(f32[256,2]{1,0:T(8,128)} %get-tuple-element.30) | copy-start | bytes 6148
  26.2 1.3 copy-start.13
  26.2 1.4 copy-start.14
  26.2 1.5 copy-start.15
  28.5 63.1 %all-to-all-start = ((bf16[64,8,512]{2,1,0:T(8,128)(2,1)}), bf16[64,8,512]{2,1,0:T(8,128)(2,1)S(1)}, u32[]{:S(2)}, u32[]{:S(2)}) async-start(bf16[64,8,512]{2,1,0:T(8,128)(2,1)} %bitcast.115), calls=%async_computation | async-start | bytes 1048576 | tf_op jit(solution)/shard_map/all_to_all | solution.py:79
  50.5 20.1 %copy-start.16 = (f32[8,32,256]{2,1,0:T(8,128)S(1)}, f32[8,32,256]{2,1,0:T(8,128)}, u32[]{:S(2)}) copy-start(f32[8,32,256]{2,1,0:T(8,128)} %convert_element_type.192) | copy-start | bytes 786436
  50.5 20.1 %copy-start.22 = (f32[256]{0:T(256)S(1)}, f32[256]{0:T(256)}, u32[]{:S(2)}) copy-start(f32[256]{0:T(256)} %param.10) | copy-start | bytes 3076
  50.6 16.4 %collective-permute-start = (bf16[4,1,5,32,256]{4,3,2,0,1:T(8,128)(2,1)S(1)}, bf16[4,1,5,32,256]{4,3,2,0,1:T(8,128)(2,1)S(1)}, u32[]{:S(2)}, u32[]{:S(2)}) collective-permute-start(bf16[4,1,5,32,256]{4,3,2,0,1:T(8,128)(2,1)S(1)} %get-tuple-element.13), channel_id=1, source_target_pairs={{0,1},{1,0},{2,3},{3,2},{4,5},{5,4},{6,7},{7,6},{8,9},{9,8},{10,11... | collective-permute-start | bytes 983048 | tf_op jit(solution)/shard_map/ppermute | solution.py:39
  67.0 10.4 %collective-permute-start.1 = (bf16[2,2,5,32,256]{4,3,2,1,0:T(8,128)(2,1)S(1)}, bf16[2,2,5,32,256]{4,3,2,1,0:T(8,128)(2,1)S(1)}, u32[]{:S(2)}, u32[]{:S(2)}) collective-permute-start(bf16[2,2,5,32,256]{4,3,2,1,0:T(8,128)(2,1)S(1)} %bitcast.124), channel_id=1, source_target_pairs={{0,2},{1,3},{2,0},{3,1},{4,6},{5,7},{6,4},{7,5},{8,10},{9,11},{10,... | collective-permute-start | bytes 983048 | tf_op jit(solution)/shard_map/ppermute | solution.py:39
  77.4 5.5 %copy-start.11 = (f32[8,32,256]{2,1,0:T(8,128)S(1)}, f32[8,32,256]{2,1,0:T(8,128)}, u32[]{:S(2)}) copy-start(f32[8,32,256]{2,1,0:T(8,128)} %get-tuple-element.26) | copy-start | bytes 786436
  77.5 11.0 %collective-permute-start.2 = (bf16[1,4,5,32,256]{4,3,2,1,0:T(8,128)(2,1)S(1)}, bf16[1,4,5,32,256]{4,3,2,1,0:T(8,128)(2,1)S(1)}, u32[]{:S(2)}, u32[]{:S(2)}) collective-permute-start(bf16[1,4,5,32,256]{4,3,2,1,0:T(8,128)(2,1)S(1)} %get-tuple-element.9), channel_id=1, source_target_pairs={{0,4},{1,5},{2,6},{3,7},{4,0},{5,1},{6,2},{7,3},{8,12},{9,13},{10,... | collective-permute-start | bytes 983048 | tf_op jit(solution)/shard_map/ppermute | solution.py:39
  95.5 1.3 copy-start.10
  95.5 1.5 copy-start.20
  95.5 1.5 copy-start.21
  95.5 1.5 copy-start.23
  95.5 1.5 copy-start.24
  95.5 1.9 %copy-start.8 = (bf16[64,8,384]{2,1,0:T(8,128)(2,1)S(1)}, bf16[64,8,384]{2,1,0:T(8,128)(2,1)}, u32[]{:S(2)}) copy-start(bf16[64,8,384]{2,1,0:T(8,128)(2,1)} %fusion.9) | copy-start | bytes 1179652
  146.1 2.3 %copy-start.5 = (bf16[8,5,32,256]{3,2,1,0:T(8,128)(2,1)S(1)}, bf16[8,5,32,256]{3,2,1,0:T(8,128)(2,1)}, u32[]{:S(2)}) copy-start(bf16[8,5,32,256]{3,2,1,0:T(8,128)(2,1)} %gather_fusion.1) | copy-start | bytes 1966084
  (6 other events, 5.8 us)

commit v11 on v9

--- a/solution.py
+++ b/solution.py
@@ -32,12 +32,7 @@
 
 def xor_order(blocks, mine):
     size = blocks.shape[0]
-    bit = 1
-    while bit < size:
-        swapped = blocks.reshape(size // (2 * bit), 2, bit, *blocks.shape[1:])[:, ::-1]
-        blocks = jnp.where((mine // bit) % 2 == 1, swapped.reshape(blocks.shape), blocks)
-        bit *= 2
-    return blocks
+    return blocks[jnp.bitwise_xor(jnp.arange(size, dtype=jnp.int32), mine)]
 
 
 def butterfly(blocks, mine):
@@ -130,6 +125,7 @@
     extra = jnp.zeros((gxn, nxl - 2, lanes), bf16)
     extra = jnp.concatenate([pieces[0][:, None], pieces[1][:, None], extra], axis=1)
     back = jnp.concatenate([stream_div.reshape(gxn, nxl, comps * lanes), extra], axis=2)
+    back, wall_div = lax.optimization_barrier((back, wall_div))
     back = lax.all_to_all(back, "gx", 0, 0, tiled=True)
     summed = jnp.sum(join_wide(back[:, :2, comps * lanes:].transpose(1, 0, 2)), axis=0)
     summed = summed.reshape(ny // gxn, nzl).T

time: 149 us -> 141 us (0.946)
  waiting for transfers between devices: 23.1 us -> 19.2 us
  matrix products: 8.63 us -> 4.83 us
    select_n x6 -> x1, other arithmetic: 3.33 us -> 0.01 us  [xor_order(): return blocks[jnp.bitwise_xor(jnp.arange(size, dtype=jnp.int32), mine)]]
    rev x6 -> x0, local copies, waits for them, and re-layouts: 3.28 us -> none  [xor_order(): blocks.reshape(size // (2 * bit), 2, bit, *blocks.shape[1:])[:, ::-1]]
    all_to_all x1, waiting for transfers between devices: 2.73 us -> 0.01 us  [section(): zt = lax.all_to_all(zs, 'gz', 1, 2, tiled=True)[:, 0]]
    dot_general x2, matrix products: 3.95 us -> 1.24 us  [wall_derivative(): jnp.einsum('kxzj,ij->kxzi', source, wall_operator, preferred_element_type...]
    ppermute x3, starting transfers between devices: 10.5 us -> 13.1 us  [butterfly(): moved = lax.ppermute(split[:, 1], 'gz', pairs)]
    all_to_all x1, starting transfers between devices: 19.7 us -> 17.2 us  [section(): xt = lax.all_to_all(xs, 'gx', 0, 0, tiled=True)]
    gather x0 -> x2, local copies, waits for them, and re-layouts: none -> 2.04 us  [xor_order(): return blocks[jnp.bitwise_xor(jnp.arange(size, dtype=jnp.int32), mine)]]
    transpose x1, other arithmetic: 0.72 us -> 2.43 us  [section(): xs = xs.reshape(comps + 1, nxl, nzl, yparts, lanes).transpose(2, 3, 1, 0, 4)]
  transfers between devices with their start and end apart: 5 -> 5, of which waited for: 4 -> 3; matrix products, arithmetic and copies ran while one was open for 13% -> 14% of each run, Pallas kernels for 0% -> 0%
where the time goes in v11:
time: 141 us; the launch traced here: 139 us
  blocking collectives  47.7 us (34%)
  starting transfers between devices  37.9 us (27%)
  waiting for transfers between devices  19.2 us (14%)
  local copies, waits for them, and re-layouts  16.6 us (12%)
  other arithmetic  11.4 us (8%)
  matrix products  4.83 us (3%)
    all_to_all x1, blocking collectives, section(): back = lax.all_to_all(back, 'gx', 0, 0, tiled=True)  47.7 us
    ppermute x3, waiting for transfers between devices, butterfly(): moved = lax.ppermute(split[:, 1], 'gz', pairs)  19.2 us
    all_to_all x1, starting transfers between devices, section(): xt = lax.all_to_all(xs, 'gx', 0, 0, tiled=True)  17.2 us
    ppermute x3, starting transfers between devices, butterfly(): moved = lax.ppermute(split[:, 1], 'gz', pairs)  13.1 us
    all_to_all x1, starting transfers between devices, section(): zt = lax.all_to_all(zs, 'gz', 1, 2, tiled=True)[:, 0]  7.6 us
    slice x4, local copies, waits for them, and re-layouts, folded(): shifted = lambda step: jnp.roll(wide, step, 1)  3.33 us
  transfers between devices with their start and end apart: 5, of which 3 were waited for; matrix products, arithmetic and copies ran while one was open for 14% of the time, Pallas kernels for 0%

profile of v11, /device:TPU:1, one launch (start us, length us, event | category | flops | bytes accessed | tf_op | source)
XLA Modules:
  0.0 138.9 jit_solution(5759929947049054447)
XLA Ops:
  0.6 1.7 %fusion.43 = (f32[8,32,256]{2,1,0:T(8,128)}, bf16[1,8,32,256]{3,2,0,1:T(8,128)(2,1)S(1)}) fusion(bf16[8,32,256]{2,1,0:T(8,128)(2,1)} %param.8, f32[32,256]{1,0:T(8,128)} %param.9), kind=kLoop, calls=%fused_computation.85 | loop fusion | flops 262144 | bytes 557056 | tf_op jit(solution)/shard_map/convert_element_type | solution.py:79
  2.3 2.0 %pad_maximum_fusion = bf16[5,8,32,256]{3,2,0,1:T(8,128)(2,1)} fusion(bf16[1,8,32,256]{3,2,0,1:T(8,128)(2,1)} %bitcast.111, bf16[1,8,32,256]{3,2,0,1:T(8,128)(2,1)S(1)} %get-tuple-element.45, bf16[3,8,32,256]{3,2,1,0:T(8,128)(2,1)} %param.7), kind=kLoop, calls=%fused_computation.47 | loop fusion | flops 1966080 | bytes 1310720 | tf_op jit(solution)/shard_map/concatenate | solution.py:104
  4.3 7.6 %all-to-all-start.1 = ((bf16[5,8,32,256]{3,2,0,1:T(8,128)(2,1)}), bf16[5,8,32,256]{3,2,0,1:T(8,128)(2,1)S(1)}, u32[]{:S(2)}, u32[]{:S(2)}) async-start(bf16[5,8,32,256]{3,2,0,1:T(8,128)(2,1)} %pad_maximum_fusion), calls=%async_computation.1 | async-start | bytes 1310720 | tf_op jit(solution)/shard_map/all_to_all | solution.py:105
  12.7 1.3 fusion.66
  14.1 0.8 fusion.67
  14.9 0.8 fusion.69
  15.7 2.4 %maximum_bitcast_fusion.1 = bf16[32,2,8,4,128]{4,1,0,2,3:T(2,128)(2,1)} fusion(bf16[1,8,32,2,128]{4,3,2,1,0:T(2,128)(2,1)} %concatenate.73, bf16[3,8,32,2,128]{4,3,2,1,0:T(2,128)(2,1)S(1)} %concatenate.72), kind=kLoop, calls=%fused_computation.53 | loop fusion | flops 262144 | bytes 1048576 | tf_op jit(solution)/shard_map/transpose | solution.py:82
  18.9 2.4 %copy.29 = bf16[32,2,8,4,128]{4,2,3,1,0:T(8,128)(2,1)} copy(bf16[32,2,8,4,128]{4,1,0,2,3:T(2,128)(2,1)} %maximum_bitcast_fusion.1) | data formatting | bytes 1048576 | tf_op jit(solution)/shard_map/transpose | solution.py:82
  21.7 0.8 copy-done.3
  23.5 17.2 %all-to-all-start = ((bf16[64,8,512]{2,1,0:T(8,128)(2,1)}), bf16[64,8,512]{2,1,0:T(8,128)(2,1)S(1)}, u32[]{:S(2)}, u32[]{:S(2)}) async-start(bf16[64,8,512]{2,1,0:T(8,128)(2,1)} %bitcast.112), calls=%async_computation | async-start | bytes 1048576 | tf_op jit(solution)/shard_map/all_to_all | solution.py:84
  43.4 5.4 %collective-permute-start = (bf16[4,1,5,32,256]{4,3,2,0,1:T(8,128)(2,1)S(1)}, bf16[4,1,5,32,256]{4,3,2,0,1:T(8,128)(2,1)S(1)}, u32[]{:S(2)}, u32[]{:S(2)}) collective-permute-start(bf16[4,1,5,32,256]{4,3,2,0,1:T(8,128)(2,1)S(1)} %get-tuple-element.31), channel_id=1, source_target_pairs={{0,1},{1,0},{2,3},{3,2},{4,5},{5,4},{6,7},{7,6},{8,9},{9,8},{10,11... | collective-permute-start | bytes 983048 | tf_op jit(solution)/shard_map/ppermute | solution.py:45
  49.4 9.0 %collective-permute-done = bf16[4,1,5,32,256]{4,3,2,0,1:T(8,128)(2,1)S(1)} collective-permute-done((bf16[4,1,5,32,256]{4,3,2,0,1:T(8,128)(2,1)S(1)}, bf16[4,1,5,32,256]{4,3,2,0,1:T(8,128)(2,1)S(1)}, u32[]{:S(2)}, u32[]{:S(2)}) %collective-permute-start) | collective-permute-done | bytes 327712 | tf_op jit(solution)/shard_map/ppermute | solution.py:45
  58.4 3.1 %collective-permute-start.1 = (bf16[2,2,5,32,256]{4,3,2,1,0:T(8,128)(2,1)S(1)}, bf16[2,2,5,32,256]{4,3,2,1,0:T(8,128)(2,1)S(1)}, u32[]{:S(2)}, u32[]{:S(2)}) collective-permute-start(bf16[2,2,5,32,256]{4,3,2,1,0:T(8,128)(2,1)S(1)} %bitcast.121), channel_id=1, source_target_pairs={{0,2},{1,3},{2,0},{3,1},{4,6},{5,7},{6,4},{7,5},{8,10},{9,11},{10,... | collective-permute-start | bytes 983048 | tf_op jit(solution)/shard_map/ppermute | solution.py:45
  62.1 0.9 multiply_reduce_fusion
  63.0 5.4 %collective-permute-done.1 = bf16[2,2,5,32,256]{4,3,2,1,0:T(8,128)(2,1)S(1)} collective-permute-done((bf16[2,2,5,32,256]{4,3,2,1,0:T(8,128)(2,1)S(1)}, bf16[2,2,5,32,256]{4,3,2,1,0:T(8,128)(2,1)S(1)}, u32[]{:S(2)}, u32[]{:S(2)}) %collective-permute-start.1) | collective-permute-done | bytes 327712 | tf_op jit(solution)/shard_map/ppermute | solution.py:45
  68.5 4.6 %collective-permute-start.2 = (bf16[1,4,5,32,256]{4,3,2,1,0:T(8,128)(2,1)S(1)}, bf16[1,4,5,32,256]{4,3,2,1,0:T(8,128)(2,1)S(1)}, u32[]{:S(2)}, u32[]{:S(2)}) collective-permute-start(bf16[1,4,5,32,256]{4,3,2,1,0:T(8,128)(2,1)S(1)} %get-tuple-element.27), channel_id=1, source_target_pairs={{0,4},{1,5},{2,6},{3,7},{4,0},{5,1},{6,2},{7,3},{8,12},{9,13},{10,... | collective-permute-start | bytes 983048 | tf_op jit(solution)/shard_map/ppermute | solution.py:45
  74.2 4.9 %collective-permute-done.2 = bf16[1,4,5,32,256]{4,3,2,1,0:T(8,128)(2,1)S(1)} collective-permute-done((bf16[1,4,5,32,256]{4,3,2,1,0:T(8,128)(2,1)S(1)}, bf16[1,4,5,32,256]{4,3,2,1,0:T(8,128)(2,1)S(1)}, u32[]{:S(2)}, u32[]{:S(2)}) %collective-permute-start.2) | collective-permute-done | bytes 327712 | tf_op jit(solution)/shard_map/ppermute | solution.py:45
  79.2 1.5 %gather_fusion.1 = bf16[8,5,32,256]{3,2,1,0:T(8,128)(2,1)} fusion(bf16[8,5,32,256]{3,2,1,0:T(8,128)(2,1)S(1)} %bitcast.110, s32[1024]{0:T(1024)S(1)} %pad_clamp_fusion), kind=kCustom, calls=%fused_computation.1 | custom fusion | bytes 1310752 | tf_op jit(solution)/shard_map/gather | solution.py:35
  80.6 1.0 slice_bitcast_fusion.2
  82.3 1.3 fusion.23
  84.6 1.2 reduce_sum.60
  86.5 47.7 %all_to_all.19 = bf16[64,8,512]{2,1,0:T(8,128)(2,1)S(1)} all-to-all(bf16[64,8,512]{2,1,0:T(8,128)(2,1)S(1)} %maximum_maximum_fusion), channel_id=1, replica_groups=mesh['gx'=64,'gz'=8] {'gx'}, dimensions={0} | all-to-all | bytes 1048576 | tf_op jit(solution)/shard_map/all_to_all | solution.py:129
  136.2 0.9 slice_bitcast_fusion.3
  137.9 1.0 fusion.22
  (95 shorter events, 12.7 us)
Async XLA Ops:
  0.6 40.6 %copy-start = (bf16[256,256]{1,0:T(8,128)(2,1)S(1)}, bf16[256,256]{1,0:T(8,128)(2,1)}, u32[]{:S(2)}) copy-start(bf16[256,256]{1,0:T(8,128)(2,1)} %param.12) | copy-start | bytes 393220
  2.3 9.6 %copy-start.2 = (bf16[3,8,32,256]{3,2,1,0:T(8,128)(2,1)S(1)}, bf16[3,8,32,256]{3,2,1,0:T(8,128)(2,1)}, u32[]{:S(2)}) copy-start(bf16[3,8,32,256]{3,2,1,0:T(8,128)(2,1)} %param.7) | copy-start | bytes 1179652
  4.3 7.7 %copy-start.5 = (bf16[8,32,256]{2,1,0:T(8,128)(2,1)S(1)}, bf16[8,32,256]{2,1,0:T(8,128)(2,1)}, u32[]{:S(2)}) copy-start(bf16[8,32,256]{2,1,0:T(8,128)(2,1)} %param.8) | copy-start | bytes 393220
  4.3 8.4 %copy-start.1 = (bf16[512,512]{1,0:T(8,128)(2,1)S(1)}, bf16[512,512]{1,0:T(8,128)(2,1)}, u32[]{:S(2)}) copy-start(bf16[512,512]{1,0:T(8,128)(2,1)} %param.11) | copy-start | bytes 1572868
  4.3 19.2 %all-to-all-start.1 = ((bf16[5,8,32,256]{3,2,0,1:T(8,128)(2,1)}), bf16[5,8,32,256]{3,2,0,1:T(8,128)(2,1)S(1)}, u32[]{:S(2)}, u32[]{:S(2)}) async-start(bf16[5,8,32,256]{3,2,0,1:T(8,128)(2,1)} %pad_maximum_fusion), calls=%async_computation.1 | async-start | bytes 1310720 | tf_op jit(solution)/shard_map/all_to_all | solution.py:105
  21.3 1.2 copy-start.3
  21.3 1.3 copy-start.8
  21.3 1.3 copy-start.9
  21.3 1.4 %copy-start.10 = (f32[512,1]{1,0:T(8,128)S(1)}, f32[512,1]{1,0:T(8,128)}, u32[]{:S(2)}) copy-start(f32[512,1]{1,0:T(8,128)} %get-tuple-element.41) | copy-start | bytes 6148
  23.5 58.1 %all-to-all-start = ((bf16[64,8,512]{2,1,0:T(8,128)(2,1)}), bf16[64,8,512]{2,1,0:T(8,128)(2,1)S(1)}, u32[]{:S(2)}, u32[]{:S(2)}) async-start(bf16[64,8,512]{2,1,0:T(8,128)(2,1)} %bitcast.112), calls=%async_computation | async-start | bytes 1048576 | tf_op jit(solution)/shard_map/all_to_all | solution.py:84
  43.3 18.7 %copy-start.11 = (f32[8,32,256]{2,1,0:T(8,128)S(1)}, f32[8,32,256]{2,1,0:T(8,128)}, u32[]{:S(2)}) copy-start(f32[8,32,256]{2,1,0:T(8,128)} %convert_element_type.198) | copy-start | bytes 786436
  43.3 18.7 %copy-start.12 = (bf16[256,256]{1,0:T(8,128)(2,1)S(1)}, bf16[256,256]{1,0:T(8,128)(2,1)}, u32[]{:S(2)}) copy-start(bf16[256,256]{1,0:T(8,128)(2,1)} %param.13) | copy-start | bytes 393220
  43.4 18.7 %copy-start.14 = (f32[256]{0:T(256)S(1)}, f32[256]{0:T(256)}, u32[]{:S(2)}) copy-start(f32[256]{0:T(256)} %param.10) | copy-start | bytes 3076
  43.4 15.0 %collective-permute-start = (bf16[4,1,5,32,256]{4,3,2,0,1:T(8,128)(2,1)S(1)}, bf16[4,1,5,32,256]{4,3,2,0,1:T(8,128)(2,1)S(1)}, u32[]{:S(2)}, u32[]{:S(2)}) collective-permute-start(bf16[4,1,5,32,256]{4,3,2,0,1:T(8,128)(2,1)S(1)} %get-tuple-element.31), channel_id=1, source_target_pairs={{0,1},{1,0},{2,3},{3,2},{4,5},{5,4},{6,7},{7,6},{8,9},{9,8},{10,11... | collective-permute-start | bytes 983048 | tf_op jit(solution)/shard_map/ppermute | solution.py:45
  58.4 9.9 %collective-permute-start.1 = (bf16[2,2,5,32,256]{4,3,2,1,0:T(8,128)(2,1)S(1)}, bf16[2,2,5,32,256]{4,3,2,1,0:T(8,128)(2,1)S(1)}, u32[]{:S(2)}, u32[]{:S(2)}) collective-permute-start(bf16[2,2,5,32,256]{4,3,2,1,0:T(8,128)(2,1)S(1)} %bitcast.121), channel_id=1, source_target_pairs={{0,2},{1,3},{2,0},{3,1},{4,6},{5,7},{6,4},{7,5},{8,10},{9,11},{10,... | collective-permute-start | bytes 983048 | tf_op jit(solution)/shard_map/ppermute | solution.py:45
  68.4 5.5 %copy-start.7 = (f32[8,32,256]{2,1,0:T(8,128)S(1)}, f32[8,32,256]{2,1,0:T(8,128)}, u32[]{:S(2)}) copy-start(f32[8,32,256]{2,1,0:T(8,128)} %get-tuple-element.44) | copy-start | bytes 786436
  68.5 10.6 %collective-permute-start.2 = (bf16[1,4,5,32,256]{4,3,2,1,0:T(8,128)(2,1)S(1)}, bf16[1,4,5,32,256]{4,3,2,1,0:T(8,128)(2,1)S(1)}, u32[]{:S(2)}, u32[]{:S(2)}) collective-permute-start(bf16[1,4,5,32,256]{4,3,2,1,0:T(8,128)(2,1)S(1)} %get-tuple-element.27), channel_id=1, source_target_pairs={{0,4},{1,5},{2,6},{3,7},{4,0},{5,1},{6,2},{7,3},{8,12},{9,13},{10,... | collective-permute-start | bytes 983048 | tf_op jit(solution)/shard_map/ppermute | solution.py:45
  84.6 1.4 copy-start.13
  84.6 1.4 copy-start.15
  84.6 1.4 copy-start.16
  134.3 0.8 copy-start.6
  135.5 2.3 %copy-start.4 = (bf16[8,5,32,256]{3,2,1,0:T(8,128)(2,1)S(1)}, bf16[8,5,32,256]{3,2,1,0:T(8,128)(2,1)}, u32[]{:S(2)}) copy-start(bf16[8,5,32,256]{3,2,1,0:T(8,128)(2,1)} %gather_fusion.1) | copy-start | bytes 1966084

commit v12 on v11

--- a/solution.py
+++ b/solution.py
@@ -102,7 +102,8 @@
     gzn = lax.axis_size("gz")
     mine = lax.axis_index("gz")
     zs = jnp.concatenate([adjoint, viscosity[None], strain[None]], axis=0)
-    zt = lax.all_to_all(zs, "gz", 1, 2, tiled=True)[:, 0]
+    zt = lax.all_to_all(zs, "gz", 1, 2, tiled=True)
+    zt = zt[:, 0]
     span_visc = zt[comps].astype(f32)
     span_strain = zt[comps + 1].astype(f32)
     span_grad = derivative(zt[:comps], span_inverse)
@@ -120,7 +121,8 @@
     wall_div = wall_derivative(wall_flux, wall_operator, metric)
     wall_part = jnp.sum(strain_wide[None] * wall_grad.astype(f32) ** 2, axis=(0, 1))
 
-    partial_sum = stream_part + span_part + wall_part
+    other_part = lax.optimization_barrier(span_part + wall_part)
+    partial_sum = stream_part + other_part
     pieces = split_wide(partial_sum.T.reshape(gxn, -1))
     extra = jnp.zeros((gxn, nxl - 2, lanes), bf16)
     extra = jnp.concatenate([pieces[0][:, None], pieces[1][:, None], extra], axis=1)

time: 141 us -> 142 us (level)
  no operation moved by 1% of the time
where the time goes in v12:
time: 142 us; the launch traced here: 140 us
  blocking collectives  47.7 us (34%)
  starting transfers between devices  37.9 us (27%)
  waiting for transfers between devices  19.2 us (14%)
  local copies, waits for them, and re-layouts  16.6 us (12%)
  other arithmetic  12.2 us (9%)
  matrix products  4.85 us (3%)
    all_to_all x1, blocking collectives, section(): back = lax.all_to_all(back, 'gx', 0, 0, tiled=True)  47.7 us
    ppermute x3, waiting for transfers between devices, butterfly(): moved = lax.ppermute(split[:, 1], 'gz', pairs)  19.2 us
    all_to_all x1, starting transfers between devices, section(): xt = lax.all_to_all(xs, 'gx', 0, 0, tiled=True)  17.2 us
    ppermute x3, starting transfers between devices, butterfly(): moved = lax.ppermute(split[:, 1], 'gz', pairs)  13.1 us
    all_to_all x1, starting transfers between devices, section(): zt = lax.all_to_all(zs, 'gz', 1, 2, tiled=True)  7.6 us
    slice x4, local copies, waits for them, and re-layouts, folded(): shifted = lambda step: jnp.roll(wide, step, 1)  3.36 us
  transfers between devices with their start and end apart: 5, of which 3 were waited for; matrix products, arithmetic and copies ran while one was open for 14% of the time, Pallas kernels for 0%

profile of v12, /device:TPU:1, one launch (start us, length us, event | category | flops | bytes accessed | tf_op | source)
XLA Modules:
  0.0 139.6 jit_solution(16234361008997928275)
XLA Ops:
  0.6 1.7 %fusion.43 = (f32[8,32,256]{2,1,0:T(8,128)}, bf16[1,8,32,256]{3,2,0,1:T(8,128)(2,1)S(1)}) fusion(bf16[8,32,256]{2,1,0:T(8,128)(2,1)} %param.8, f32[32,256]{1,0:T(8,128)} %param.9), kind=kLoop, calls=%fused_computation.85 | loop fusion | flops 262144 | bytes 557056 | tf_op jit(solution)/shard_map/convert_element_type | solution.py:79
  2.3 2.0 %pad_maximum_fusion = bf16[5,8,32,256]{3,2,0,1:T(8,128)(2,1)} fusion(bf16[1,8,32,256]{3,2,0,1:T(8,128)(2,1)} %bitcast.107, bf16[1,8,32,256]{3,2,0,1:T(8,128)(2,1)S(1)} %get-tuple-element.45, bf16[3,8,32,256]{3,2,1,0:T(8,128)(2,1)} %param.7), kind=kLoop, calls=%fused_computation.47 | loop fusion | flops 1966080 | bytes 1310720 | tf_op jit(solution)/shard_map/concatenate | solution.py:104
  4.3 7.6 %all-to-all-start.1 = ((bf16[5,8,32,256]{3,2,0,1:T(8,128)(2,1)}), bf16[5,8,32,256]{3,2,0,1:T(8,128)(2,1)S(1)}, u32[]{:S(2)}, u32[]{:S(2)}) async-start(bf16[5,8,32,256]{3,2,0,1:T(8,128)(2,1)} %pad_maximum_fusion), calls=%async_computation.1 | async-start | bytes 1310720 | tf_op jit(solution)/shard_map/all_to_all | solution.py:105
  12.7 1.4 fusion.66
  14.1 0.8 fusion.67
  14.9 0.8 fusion.69
  15.7 2.4 %maximum_bitcast_fusion.1 = bf16[32,2,8,4,128]{4,1,0,2,3:T(2,128)(2,1)} fusion(bf16[1,8,32,2,128]{4,3,2,1,0:T(2,128)(2,1)} %concatenate.73, bf16[3,8,32,2,128]{4,3,2,1,0:T(2,128)(2,1)S(1)} %concatenate.72), kind=kLoop, calls=%fused_computation.53 | loop fusion | flops 262144 | bytes 1048576 | tf_op jit(solution)/shard_map/transpose | solution.py:82
  18.9 2.4 %copy.29 = bf16[32,2,8,4,128]{4,2,3,1,0:T(8,128)(2,1)} copy(bf16[32,2,8,4,128]{4,1,0,2,3:T(2,128)(2,1)} %maximum_bitcast_fusion.1) | data formatting | bytes 1048576 | tf_op jit(solution)/shard_map/transpose | solution.py:82
  21.7 0.8 copy-done.3
  23.6 17.2 %all-to-all-start = ((bf16[64,8,512]{2,1,0:T(8,128)(2,1)}), bf16[64,8,512]{2,1,0:T(8,128)(2,1)S(1)}, u32[]{:S(2)}, u32[]{:S(2)}) async-start(bf16[64,8,512]{2,1,0:T(8,128)(2,1)} %bitcast.108), calls=%async_computation | async-start | bytes 1048576 | tf_op jit(solution)/shard_map/all_to_all | solution.py:84
  43.4 5.4 %collective-permute-start = (bf16[4,1,5,32,256]{4,3,2,0,1:T(8,128)(2,1)S(1)}, bf16[4,1,5,32,256]{4,3,2,0,1:T(8,128)(2,1)S(1)}, u32[]{:S(2)}, u32[]{:S(2)}) collective-permute-start(bf16[4,1,5,32,256]{4,3,2,0,1:T(8,128)(2,1)S(1)} %get-tuple-element.31), channel_id=1, source_target_pairs={{0,1},{1,0},{2,3},{3,2},{4,5},{5,4},{6,7},{7,6},{8,9},{9,8},{10,11... | collective-permute-start | bytes 983048 | tf_op jit(solution)/shard_map/ppermute | solution.py:45
  49.4 9.0 %collective-permute-done = bf16[4,1,5,32,256]{4,3,2,0,1:T(8,128)(2,1)S(1)} collective-permute-done((bf16[4,1,5,32,256]{4,3,2,0,1:T(8,128)(2,1)S(1)}, bf16[4,1,5,32,256]{4,3,2,0,1:T(8,128)(2,1)S(1)}, u32[]{:S(2)}, u32[]{:S(2)}) %collective-permute-start) | collective-permute-done | bytes 327712 | tf_op jit(solution)/shard_map/ppermute | solution.py:45
  58.5 3.1 %collective-permute-start.1 = (bf16[2,2,5,32,256]{4,3,2,1,0:T(8,128)(2,1)S(1)}, bf16[2,2,5,32,256]{4,3,2,1,0:T(8,128)(2,1)S(1)}, u32[]{:S(2)}, u32[]{:S(2)}) collective-permute-start(bf16[2,2,5,32,256]{4,3,2,1,0:T(8,128)(2,1)S(1)} %bitcast.117), channel_id=1, source_target_pairs={{0,2},{1,3},{2,0},{3,1},{4,6},{5,7},{6,4},{7,5},{8,10},{9,11},{10,... | collective-permute-start | bytes 983048 | tf_op jit(solution)/shard_map/ppermute | solution.py:45
  62.2 0.9 multiply_reduce_fusion
  63.1 5.3 %collective-permute-done.1 = bf16[2,2,5,32,256]{4,3,2,1,0:T(8,128)(2,1)S(1)} collective-permute-done((bf16[2,2,5,32,256]{4,3,2,1,0:T(8,128)(2,1)S(1)}, bf16[2,2,5,32,256]{4,3,2,1,0:T(8,128)(2,1)S(1)}, u32[]{:S(2)}, u32[]{:S(2)}) %collective-permute-start.1) | collective-permute-done | bytes 327712 | tf_op jit(solution)/shard_map/ppermute | solution.py:45
  68.5 4.6 %collective-permute-start.2 = (bf16[1,4,5,32,256]{4,3,2,1,0:T(8,128)(2,1)S(1)}, bf16[1,4,5,32,256]{4,3,2,1,0:T(8,128)(2,1)S(1)}, u32[]{:S(2)}, u32[]{:S(2)}) collective-permute-start(bf16[1,4,5,32,256]{4,3,2,1,0:T(8,128)(2,1)S(1)} %get-tuple-element.27), channel_id=1, source_target_pairs={{0,4},{1,5},{2,6},{3,7},{4,0},{5,1},{6,2},{7,3},{8,12},{9,13},{10,... | collective-permute-start | bytes 983048 | tf_op jit(solution)/shard_map/ppermute | solution.py:45
  74.2 4.9 %collective-permute-done.2 = bf16[1,4,5,32,256]{4,3,2,1,0:T(8,128)(2,1)S(1)} collective-permute-done((bf16[1,4,5,32,256]{4,3,2,1,0:T(8,128)(2,1)S(1)}, bf16[1,4,5,32,256]{4,3,2,1,0:T(8,128)(2,1)S(1)}, u32[]{:S(2)}, u32[]{:S(2)}) %collective-permute-start.2) | collective-permute-done | bytes 327712 | tf_op jit(solution)/shard_map/ppermute | solution.py:45
  79.2 1.5 %gather_fusion.1 = bf16[8,5,32,256]{3,2,1,0:T(8,128)(2,1)} fusion(bf16[8,5,32,256]{3,2,1,0:T(8,128)(2,1)S(1)} %bitcast.106, s32[1024]{0:T(1024)S(1)} %pad_clamp_fusion), kind=kCustom, calls=%fused_computation.1 | custom fusion | bytes 1310752 | tf_op jit(solution)/shard_map/gather | solution.py:35
  80.7 1.0 slice_bitcast_fusion.2
  83.1 1.3 fusion.23
  85.4 1.2 reduce_sum.56
  87.3 47.7 %all_to_all.19 = bf16[64,8,512]{2,1,0:T(8,128)(2,1)S(1)} all-to-all(bf16[64,8,512]{2,1,0:T(8,128)(2,1)S(1)} %maximum_maximum_fusion), channel_id=1, replica_groups=mesh['gx'=64,'gz'=8] {'gx'}, dimensions={0} | all-to-all | bytes 1048576 | tf_op jit(solution)/shard_map/all_to_all | solution.py:131
  136.9 0.9 slice_bitcast_fusion.3
  138.6 1.0 fusion.22
  (94 shorter events, 13.5 us)
Async XLA Ops:
  0.6 40.6 %copy-start = (bf16[256,256]{1,0:T(8,128)(2,1)S(1)}, bf16[256,256]{1,0:T(8,128)(2,1)}, u32[]{:S(2)}) copy-start(bf16[256,256]{1,0:T(8,128)(2,1)} %param.12) | copy-start | bytes 393220
  2.3 9.6 %copy-start.2 = (bf16[3,8,32,256]{3,2,1,0:T(8,128)(2,1)S(1)}, bf16[3,8,32,256]{3,2,1,0:T(8,128)(2,1)}, u32[]{:S(2)}) copy-start(bf16[3,8,32,256]{3,2,1,0:T(8,128)(2,1)} %param.7) | copy-start | bytes 1179652
  4.3 7.7 %copy-start.5 = (bf16[8,32,256]{2,1,0:T(8,128)(2,1)S(1)}, bf16[8,32,256]{2,1,0:T(8,128)(2,1)}, u32[]{:S(2)}) copy-start(bf16[8,32,256]{2,1,0:T(8,128)(2,1)} %param.8) | copy-start | bytes 393220
  4.3 8.4 %copy-start.1 = (bf16[512,512]{1,0:T(8,128)(2,1)S(1)}, bf16[512,512]{1,0:T(8,128)(2,1)}, u32[]{:S(2)}) copy-start(bf16[512,512]{1,0:T(8,128)(2,1)} %param.11) | copy-start | bytes 1572868
  4.3 19.2 %all-to-all-start.1 = ((bf16[5,8,32,256]{3,2,0,1:T(8,128)(2,1)}), bf16[5,8,32,256]{3,2,0,1:T(8,128)(2,1)S(1)}, u32[]{:S(2)}, u32[]{:S(2)}) async-start(bf16[5,8,32,256]{3,2,0,1:T(8,128)(2,1)} %pad_maximum_fusion), calls=%async_computation.1 | async-start | bytes 1310720 | tf_op jit(solution)/shard_map/all_to_all | solution.py:105
  21.3 1.2 copy-start.3
  21.3 1.3 copy-start.8
  21.4 1.3 copy-start.9
  21.4 1.4 %copy-start.10 = (f32[512,1]{1,0:T(8,128)S(1)}, f32[512,1]{1,0:T(8,128)}, u32[]{:S(2)}) copy-start(f32[512,1]{1,0:T(8,128)} %get-tuple-element.41) | copy-start | bytes 6148
  23.6 58.9 %all-to-all-start = ((bf16[64,8,512]{2,1,0:T(8,128)(2,1)}), bf16[64,8,512]{2,1,0:T(8,128)(2,1)S(1)}, u32[]{:S(2)}, u32[]{:S(2)}) async-start(bf16[64,8,512]{2,1,0:T(8,128)(2,1)} %bitcast.108), calls=%async_computation | async-start | bytes 1048576 | tf_op jit(solution)/shard_map/all_to_all | solution.py:84
  43.3 18.8 %copy-start.11 = (f32[8,32,256]{2,1,0:T(8,128)S(1)}, f32[8,32,256]{2,1,0:T(8,128)}, u32[]{:S(2)}) copy-start(f32[8,32,256]{2,1,0:T(8,128)} %convert_element_type.198) | copy-start | bytes 786436
  43.3 18.8 %copy-start.12 = (bf16[256,256]{1,0:T(8,128)(2,1)S(1)}, bf16[256,256]{1,0:T(8,128)(2,1)}, u32[]{:S(2)}) copy-start(bf16[256,256]{1,0:T(8,128)(2,1)} %param.13) | copy-start | bytes 393220
  43.3 18.8 %copy-start.13 = (f32[256]{0:T(256)S(1)}, f32[256]{0:T(256)}, u32[]{:S(2)}) copy-start(f32[256]{0:T(256)} %param.10) | copy-start | bytes 3076
  43.4 15.0 %collective-permute-start = (bf16[4,1,5,32,256]{4,3,2,0,1:T(8,128)(2,1)S(1)}, bf16[4,1,5,32,256]{4,3,2,0,1:T(8,128)(2,1)S(1)}, u32[]{:S(2)}, u32[]{:S(2)}) collective-permute-start(bf16[4,1,5,32,256]{4,3,2,0,1:T(8,128)(2,1)S(1)} %get-tuple-element.31), channel_id=1, source_target_pairs={{0,1},{1,0},{2,3},{3,2},{4,5},{5,4},{6,7},{7,6},{8,9},{9,8},{10,11... | collective-permute-start | bytes 983048 | tf_op jit(solution)/shard_map/ppermute | solution.py:45
  58.5 10.0 %collective-permute-start.1 = (bf16[2,2,5,32,256]{4,3,2,1,0:T(8,128)(2,1)S(1)}, bf16[2,2,5,32,256]{4,3,2,1,0:T(8,128)(2,1)S(1)}, u32[]{:S(2)}, u32[]{:S(2)}) collective-permute-start(bf16[2,2,5,32,256]{4,3,2,1,0:T(8,128)(2,1)S(1)} %bitcast.117), channel_id=1, source_target_pairs={{0,2},{1,3},{2,0},{3,1},{4,6},{5,7},{6,4},{7,5},{8,10},{9,11},{10,... | collective-permute-start | bytes 983048 | tf_op jit(solution)/shard_map/ppermute | solution.py:45
  68.4 5.5 %copy-start.7 = (f32[8,32,256]{2,1,0:T(8,128)S(1)}, f32[8,32,256]{2,1,0:T(8,128)}, u32[]{:S(2)}) copy-start(f32[8,32,256]{2,1,0:T(8,128)} %get-tuple-element.44) | copy-start | bytes 786436
  68.5 10.6 %collective-permute-start.2 = (bf16[1,4,5,32,256]{4,3,2,1,0:T(8,128)(2,1)S(1)}, bf16[1,4,5,32,256]{4,3,2,1,0:T(8,128)(2,1)S(1)}, u32[]{:S(2)}, u32[]{:S(2)}) collective-permute-start(bf16[1,4,5,32,256]{4,3,2,1,0:T(8,128)(2,1)S(1)} %get-tuple-element.27), channel_id=1, source_target_pairs={{0,4},{1,5},{2,6},{3,7},{4,0},{5,1},{6,2},{7,3},{8,12},{9,13},{10,... | collective-permute-start | bytes 983048 | tf_op jit(solution)/shard_map/ppermute | solution.py:45
  85.3 1.4 copy-start.14
  85.4 1.4 copy-start.15
  135.0 0.8 copy-start.6
  136.3 2.3 %copy-start.4 = (bf16[8,5,32,256]{3,2,1,0:T(8,128)(2,1)S(1)}, bf16[8,5,32,256]{3,2,1,0:T(8,128)(2,1)}, u32[]{:S(2)}) copy-start(bf16[8,5,32,256]{3,2,1,0:T(8,128)(2,1)} %gather_fusion.1) | copy-start | bytes 1966084
